TPU v7x, 256 devices: a whole 4x4x8 slice. The times are simulated.
256 devices in a mesh: req: 64 (over z, x, core), kv: 4 (over y).
Axes of the slice: x: 4, y: 4, z: 8, core: 2. Of those that a mesh axis runs over, the one named last changes fastest.
Arguments:
- residual_in: bfloat16 [128, 2560], P('req', 'kv'), may hold values from -8 to 8
- queries: bfloat16 [128, 2560], P('req', 'kv'), may hold values from -480 to 480
- fresh_token_keys: bfloat16 [128, 512], P('req', 'kv'), may hold values from -6 to 6
- fresh_token_values: bfloat16 [128, 512], P('req', 'kv'), may hold values from -6 to 6
- cached_key_slots: bfloat16 [128, 4096, 512], P('req', None, 'kv'), may hold values from -6 to 6
- cached_value_slots: bfloat16 [128, 4096, 512], P('req', None, 'kv'), may hold values from -6 to 6
- lengths: int32 [128], replicated, may hold values from 1 to 4096, as said below
- slot_order: int32 [128], replicated, may hold values from 0 to 127, as said below
- out_proj: bfloat16 [2560, 2560], P('kv'), may hold values from -0.5 to 0.5
- norm_gain: bfloat16 [2560], P('kv'), may hold values from 0.5 to 1.5
- expert_ids: int32 [128, 6], replicated, may hold values from 0 to 63, all different within a row; in each aligned block of 128 rows (0 to 127, 128 to 255, ...) at most 24 rows name the same one
- gate_values: float32 [128, 6], replicated, may hold values from 0.1 to 0.5
- gate_proj: bfloat16 [64, 2560, 1536], P('req', None, 'kv'), may hold values from -0.125 to 0.125
- up_proj: bfloat16 [64, 2560, 1536], P('req', None, 'kv'), may hold values from -0.125 to 0.125
- down_proj: bfloat16 [64, 1536, 2560], P('req', 'kv'), may hold values from -0.15625 to 0.15625
Outputs:
- layer_out: bfloat16 [128, 2560], P('req', 'kv')
Inputs may be any that keep to these rules, and one draw needn't show every extreme that they name: `lengths`: each request's count of cached positions; some request has exactly 4096. A permutation of the requests: slot s serves request slot_order[s], and cached_key_slots[s], cached_value_slots[s] hold that request's cache. Requests sorted by decreasing length are dealt to the 64 groups of 2 consecutive slots, one round forward, the next backward. `expert_ids`: each token names 6 different experts; no expert is named by more than 24 tokens, a bound that some block reaches.
All inputs are finite; a program needn't handle non-finite values.
Results may differ from a plain program's by a relative error of at most 0.012.
Values may be sent and summed in bfloat16 or wider, within the bound.
No kernel may reach another device: no remote copies, remote signals or barrier semaphores. Data moves between devices by JAX's collectives and lax.ppermute only.
A program may use at most 64 MiB of HBM per device.

v0:
```python
import math

import jax
import jax.numpy as jnp
from jax import lax
from jax.sharding import PartitionSpec as P


def device_blocks(term, groups, parts):
    row_count = term.shape[0] // groups
    col_count = term.shape[1] // parts
    return (
        term.reshape(groups, row_count, parts, col_count)
        .transpose(0, 2, 1, 3)
        .reshape(groups * parts * row_count, col_count)
    )


def per_device(
    residual_in,
    queries,
    fresh_token_keys,
    fresh_token_values,
    cached_key_slots,
    cached_value_slots,
    lengths,
    slot_order,
    out_proj,
    norm_gain,
    expert_ids,
    gate_values,
    gate_proj,
    up_proj,
    down_proj,
):
    req_count = lax.axis_size("req")
    kv_count = lax.axis_size("kv")
    req_index = lax.axis_index("req")
    per_dev = residual_in.shape[0]
    head_dim = fresh_token_keys.shape[1]
    total_reqs = lengths.shape[0]
    model_width = out_proj.shape[1]
    all_queries, all_keys, all_values = (
        lax.all_gather(queries, "req", axis=0, tiled=True),
        lax.all_gather(fresh_token_keys, "req", axis=0, tiled=True),
        lax.all_gather(fresh_token_values, "req", axis=0, tiled=True),
    )
    served = lax.dynamic_slice_in_dim(slot_order, req_index * per_dev, per_dev)
    query_rows = all_queries[served].reshape(per_dev, -1, head_dim)
    self_key_row = all_keys[served]
    self_value_row = all_values[served]
    live_len = lengths[served]
    inv_root = 1.0 / math.sqrt(head_dim)
    scores = (
        jnp.einsum("rqd,rld->rql", query_rows, cached_key_slots, preferred_element_type=jnp.float32)
        * inv_root
    )
    positions = jnp.arange(cached_key_slots.shape[1])
    scores = jnp.where((positions[None, :] < live_len[:, None])[:, None, :], scores, -1e30)
    own_score = (
        jnp.einsum("rqd,rd->rq", query_rows, self_key_row, preferred_element_type=jnp.float32)
        * inv_root
    )
    highest = jnp.maximum(jnp.max(scores, axis=2), own_score)
    weights = jnp.exp(scores - highest[:, :, None])
    own_weight = jnp.exp(own_score - highest)
    totals = jnp.sum(weights, axis=2) + own_weight
    numerator = jnp.einsum(
        "rql,rld->rqd",
        weights.astype(jnp.bfloat16),
        cached_value_slots,
        preferred_element_type=jnp.float32,
    )
    own_low = lax.optimization_barrier(own_weight.astype(jnp.bfloat16)).astype(jnp.float32)
    numerator = numerator + own_low[:, :, None] * self_value_row.astype(jnp.float32)[:, None, :]
    attended = (numerator / totals[:, :, None]).astype(jnp.bfloat16).reshape(per_dev, -1)
    projected = jnp.dot(attended, out_proj, preferred_element_type=jnp.float32)
    placed = jnp.zeros((total_reqs, model_width), jnp.float32).at[served].set(projected)
    attn_part = lax.psum_scatter(
        device_blocks(placed, req_count, kv_count), ("req", "kv"), scatter_dimension=0, tiled=True
    )
    hidden = residual_in.astype(jnp.float32) + attn_part
    squares = lax.psum(jnp.sum(hidden * hidden, axis=1), "kv")
    normed = (
        hidden * lax.rsqrt(squares / model_width + 1e-06)[:, None] * norm_gain.astype(jnp.float32)
    ).astype(jnp.bfloat16)
    gathered = lax.all_gather(normed, ("req", "kv"), axis=0, tiled=True)
    tokens = (
        gathered.reshape(req_count, kv_count, per_dev, -1)
        .transpose(0, 2, 1, 3)
        .reshape(total_reqs, -1)
    )
    local_count = gate_proj.shape[0]
    capacity = min(2 * total_reqs * expert_ids.shape[1] // (local_count * req_count), total_reqs)
    expert = req_index * local_count + 0
    named_here = expert_ids == expert
    token_gate = jnp.sum(jnp.where(named_here, gate_values, 0.0), axis=1)
    uses_expert = jnp.any(named_here, axis=1)
    picked = jnp.nonzero(uses_expert, size=capacity, fill_value=0)[0].astype(jnp.int32)
    valid_rows = jnp.arange(capacity) < jnp.sum(uses_expert.astype(jnp.int32))
    row_block = tokens[picked]
    gate_h = jnp.dot(row_block, gate_proj[0], preferred_element_type=jnp.float32)
    up_h = jnp.dot(row_block, up_proj[0], preferred_element_type=jnp.float32)
    inner_act = (jax.nn.silu(gate_h) * up_h).astype(jnp.bfloat16)
    outputs = jnp.dot(inner_act, down_proj[0], preferred_element_type=jnp.float32)
    row_gate = jnp.where(valid_rows, token_gate[picked], 0.0)
    weighted_list = [outputs * row_gate[:, None]]
    picked_list = [picked]
    stacked_rows = jnp.concatenate(weighted_list, axis=0)
    stacked_idx = jnp.concatenate(picked_list, axis=0)
    mixture = jnp.zeros((total_reqs, model_width), jnp.float32).at[stacked_idx].add(stacked_rows)
    moe_part = lax.psum_scatter(
        device_blocks(mixture, req_count, kv_count), ("req", "kv"), scatter_dimension=0, tiled=True
    )
    return (hidden + moe_part).astype(jnp.bfloat16)


def solution(mesh):
    in_specs = (
        P("req", "kv"),
        P("req", "kv"),
        P("req", "kv"),
        P("req", "kv"),
        P("req", None, "kv"),
        P("req", None, "kv"),
        P(),
        P(),
        P("kv", None),
        P("kv"),
        P(),
        P(),
        P("req", None, "kv"),
        P("req", None, "kv"),
        P("req", "kv", None),
    )
    out_specs = P("req", "kv")
    return jax.shard_map(
        per_device, mesh=mesh, in_specs=in_specs, out_specs=out_specs, check_vma=False
    )
```

profile of v0, /device:TPU:1, one launch (start us, length us, event | category | flops | bytes accessed | tf_op | source)
XLA Modules:
  0.0 775.2 jit_solution(7634944071850056132)
XLA Ops:
  7.4 1.4 gather_fusion
  8.9 44.0 %all-gather.1 = bf16[64,2,128]{2,1,0:T(2,128)(2,1)S(1)} all-gather(bf16[1,2,128]{2,1,0:T(2,128)(2,1)} %bitcast.58), channel_id=1, replica_groups=mesh['req'=64,'kv'=4] {'req'}, dimensions={0}, use_global_device_ids=true | all-gather | bytes 33280 | tf_op jit(solution)/shard_map/all_gather | solution.py:45
  53.5 37.4 %all-gather.2 = bf16[64,2,128]{2,1,0:T(2,128)(2,1)S(1)} all-gather(bf16[1,2,128]{2,1,0:T(2,128)(2,1)} %bitcast.59), channel_id=1, replica_groups=mesh['req'=64,'kv'=4] {'req'}, dimensions={0}, use_global_device_ids=true | all-gather | bytes 33280 | tf_op jit(solution)/shard_map/all_gather | solution.py:46
  91.5 42.1 %all-gather = bf16[64,2,640]{2,1,0:T(2,128)(2,1)S(1)} all-gather(bf16[1,2,640]{2,1,0:T(2,128)(2,1)} %bitcast.57), channel_id=1, replica_groups=mesh['req'=64,'kv'=4] {'req'}, dimensions={0}, use_global_device_ids=true | all-gather | bytes 166400 | tf_op jit(solution)/shard_map/all_gather | solution.py:44
  134.4 1.5 gather_fusion.1
  136.0 2.4 fusion.47
  139.7 1.8 scatter_custom_fusion
  141.4 2.7 reshape.153
  144.1 3.1 copy.27
  147.2 3.1 reshape.154
  150.9 1.4 scatter_custom_fusion.1
  155.2 252.2 %all-reduce.5.cloned.1.call-done = f32[512,640]{1,0:T(8,128)} async-done(((f32[512,640]{1,0:T(8,128)}), f32[512,640]{1,0:T(8,128)}) %all-reduce.5.cloned.1.call-update) | async-done | bytes 1310736
  408.3 8.3 %psum.7 = f32[2]{0:T(128)S(1)} all-reduce(f32[2]{0:T(128)S(1)} %multiply_reduce_fusion), channel_id=1, replica_groups=mesh['req'=64,'kv'=4] {'kv'}, use_global_device_ids=true, to_apply=%region_10.11 | all-reduce | flops 2 | bytes 16 | tf_op jit(solution)/shard_map/psum | solution.py:83
  417.4 71.2 %all-gather.3 = bf16[256,2,640]{2,1,0:T(2,128)(2,1)S(1)} all-gather(bf16[1,2,640]{2,1,0:T(2,128)(2,1)S(1)} %fusion.39), channel_id=1, replica_groups=mesh['req'=64,'kv'=4] {'req','kv'}, dimensions={0}, use_global_device_ids=true | all-gather | bytes 657920 | tf_op jit(solution)/shard_map/all_gather | solution.py:87
  488.9 0.9 copy.35
  489.8 1.9 gather_fusion.4
  491.7 1.9 fusion.4
  493.7 3.8 convolution_multiply_fusion.1
  497.4 2.5 scatter_custom_fusion.2
  499.9 2.7 reshape.158
  502.6 3.1 copy.31
  505.7 3.1 reshape.159
  508.8 258.3 %all-reduce.7.cloned.1.call-done = f32[512,640]{1,0:T(8,128)} async-done(((f32[512,640]{1,0:T(8,128)}), f32[512,640]{1,0:T(8,128)}) %all-reduce.7.cloned.1.call-update) | async-done | bytes 1310736
  767.0 1.3 fusion.35
  (50 shorter events, 9.5 us)
Async XLA Ops:
  6.5 132.6 %copy-start = (bf16[640,2560]{1,0:T(8,128)(2,1)S(1)}, bf16[640,2560]{1,0:T(8,128)(2,1)}, u32[]{:S(2)}) copy-start(bf16[640,2560]{1,0:T(8,128)(2,1)} %param.23) | copy-start | bytes 9830404
  6.5 400.9 %all-reduce.5.cloned.1.call-start = ((), (), s32[]{:S(2)}) async-start(), calls=%async_computation | async-start | bytes 2621440
  135.9 2.8 copy-start.1
  147.2 3.2 copy-start.3
  147.2 3.2 copy-start.4
  147.2 260.2 %copy-start.2 = (bf16[2,640]{1,0:T(2,128)(2,1)S(1)}, bf16[2,640]{1,0:T(2,128)(2,1)}, u32[]{:S(2)}) copy-start(bf16[2,640]{1,0:T(2,128)(2,1)} %param.15) | copy-start | bytes 7684
  147.2 261.1 %copy-start.5 = (bf16[640]{0:T(1024)(128)(2,1)S(1)}, bf16[640]{0:T(1024)(128)(2,1)}, u32[]{:S(2)}) copy-start(bf16[640]{0:T(1024)(128)(2,1)} %param.24) | copy-start | bytes 3844
  150.3 616.7 %all-reduce.7.cloned.1.call-start = ((), (), s32[]{:S(2)}) async-start(), calls=%async_computation.1 | async-start | bytes 2621440
Sparse Core Ops, SparseCore 0:
  150.5 256.9 all-reduce.4
  508.9 258.0 all-reduce.6
where the time goes:
time: 777 us; the launch traced here: 775 us
  waiting for transfers between devices  511 us (66%)
  blocking collectives  203 us (26%)
  local copies, waits for them, and re-layouts  28.3 us (4%)
  between operations  13.5 us (2%)
  other arithmetic  10.5 us (1%)
  matrix products  9.24 us (1%)
    unnamed x4, waiting for transfers between devices  511 us
    all_gather x1, blocking collectives, per_device(): gathered = lax.all_gather(normed, ('req', 'kv'), axis=0, tiled=True)  71.2 us
    all_gather x1, blocking collectives, per_device(): lax.all_gather(fresh_token_keys, 'req', axis=0, tiled=True)  44 us
    all_gather x1, blocking collectives, per_device(): lax.all_gather(queries, 'req', axis=0, tiled=True)  42.1 us
    all_gather x1, blocking collectives, per_device(): lax.all_gather(fresh_token_values, 'req', axis=0, tiled=True)  37.4 us
  transfers between devices with their start and end apart: 2, of which 2 were waited for; matrix products, arithmetic and copies ran while one was open for 1% of the time, Pallas kernels for 0%

commit v1 on v0

v1 whole, which is shorter than its diff:
```python
import math

import jax
import jax.numpy as jnp
from jax import lax
from jax.sharding import PartitionSpec as P

COMBINE = "a2a"


def per_device(
    residual_in,
    queries,
    fresh_token_keys,
    fresh_token_values,
    cached_key_slots,
    cached_value_slots,
    lengths,
    slot_order,
    out_proj,
    norm_gain,
    expert_ids,
    gate_values,
    gate_proj,
    up_proj,
    down_proj,
):
    req_count = lax.axis_size("req")
    kv_count = lax.axis_size("kv")
    req_index = lax.axis_index("req")
    kv_index = lax.axis_index("kv")
    per_dev = residual_in.shape[0]
    head_dim = fresh_token_keys.shape[1]
    col_count = residual_in.shape[1]
    total_reqs = lengths.shape[0]
    model_width = out_proj.shape[1]
    q_width = queries.shape[1]

    packed = jnp.concatenate([queries, fresh_token_keys, fresh_token_values, residual_in], axis=1)
    all_packed = lax.all_gather(packed, "req", axis=0, tiled=True)
    served = lax.dynamic_slice_in_dim(slot_order, req_index * per_dev, per_dev)
    mine = all_packed[served]
    query_rows = mine[:, :q_width].reshape(per_dev, -1, head_dim)
    self_key_row = mine[:, q_width:q_width + head_dim]
    self_value_row = mine[:, q_width + head_dim:q_width + 2 * head_dim]
    residual_rows = mine[:, q_width + 2 * head_dim:]
    live_len = lengths[served]

    inv_root = 1.0 / math.sqrt(head_dim)
    scores = (
        jnp.einsum("rqd,rld->rql", query_rows, cached_key_slots, preferred_element_type=jnp.float32)
        * inv_root
    )
    positions = jnp.arange(cached_key_slots.shape[1])
    scores = jnp.where((positions[None, :] < live_len[:, None])[:, None, :], scores, -1e30)
    own_score = (
        jnp.einsum("rqd,rd->rq", query_rows, self_key_row, preferred_element_type=jnp.float32)
        * inv_root
    )
    highest = jnp.maximum(jnp.max(scores, axis=2), own_score)
    weights = jnp.exp(scores - highest[:, :, None])
    own_weight = jnp.exp(own_score - highest)
    totals = jnp.sum(weights, axis=2) + own_weight
    numerator = jnp.einsum(
        "rql,rld->rqd",
        weights.astype(jnp.bfloat16),
        cached_value_slots,
        preferred_element_type=jnp.float32,
    )
    own_low = lax.optimization_barrier(own_weight.astype(jnp.bfloat16)).astype(jnp.float32)
    numerator = numerator + own_low[:, :, None] * self_value_row.astype(jnp.float32)[:, None, :]
    attended = (numerator / totals[:, :, None]).astype(jnp.bfloat16).reshape(per_dev, -1)
    projected = jnp.dot(attended, out_proj, preferred_element_type=jnp.float32)

    col_start = kv_index * col_count
    own_cols = jnp.concatenate(
        [residual_rows.astype(jnp.float32), norm_gain.astype(jnp.float32)[None, :]], axis=0
    )
    summed_in = jnp.concatenate(
        [projected, jnp.zeros((1, model_width), jnp.float32)], axis=0
    ) + lax.dynamic_update_slice(
        jnp.zeros((per_dev + 1, model_width), jnp.float32), own_cols, (0, col_start)
    )
    summed = lax.psum(summed_in, "kv")
    hidden = summed[:per_dev]
    gain = summed[per_dev]
    squares = jnp.sum(hidden * hidden, axis=1)
    normed = (hidden * lax.rsqrt(squares / model_width + 1e-06)[:, None] * gain).astype(
        jnp.bfloat16
    )
    by_slot = lax.all_gather(normed, "req", axis=0, tiled=True)
    slot_of = jnp.zeros((total_reqs,), jnp.int32).at[slot_order].set(
        jnp.arange(total_reqs, dtype=jnp.int32)
    )

    local_count = gate_proj.shape[0]
    capacity = min(2 * total_reqs * expert_ids.shape[1] // (local_count * req_count), total_reqs)
    expert = req_index * local_count + 0
    named_here = expert_ids == expert
    token_gate = jnp.sum(jnp.where(named_here, gate_values, 0.0), axis=1)
    uses_expert = jnp.any(named_here, axis=1)
    picked = jnp.nonzero(uses_expert, size=capacity, fill_value=0)[0].astype(jnp.int32)
    valid_rows = jnp.arange(capacity) < jnp.sum(uses_expert.astype(jnp.int32))
    row_block = by_slot[slot_of[picked]]
    gate_h = jnp.dot(row_block, gate_proj[0], preferred_element_type=jnp.float32)
    up_h = jnp.dot(row_block, up_proj[0], preferred_element_type=jnp.float32)
    inner_act = (jax.nn.silu(gate_h) * up_h).astype(jnp.bfloat16)
    outputs = jnp.dot(inner_act, down_proj[0], preferred_element_type=jnp.float32)
    row_gate = jnp.where(valid_rows, token_gate[picked], 0.0)
    weighted = outputs * row_gate[:, None]
    weighted = lax.psum_scatter(weighted, "kv", scatter_dimension=1, tiled=True)

    own_hidden = lax.dynamic_slice_in_dim(hidden, col_start, col_count, axis=1)
    combined = (
        jnp.zeros((total_reqs, col_count), jnp.float32)
        .at[picked]
        .add(weighted)
        .at[served]
        .add(own_hidden)
    )
    if COMBINE == "rs":
        layer_rows = lax.psum_scatter(combined, "req", scatter_dimension=0, tiled=True)
    else:
        layer_rows = jnp.sum(
            lax.all_to_all(
                combined.reshape(req_count, per_dev, col_count), "req", 0, 0, tiled=False
            ),
            axis=0,
        )
    return layer_rows.astype(jnp.bfloat16)


def solution(mesh):
    in_specs = (
        P("req", "kv"),
        P("req", "kv"),
        P("req", "kv"),
        P("req", "kv"),
        P("req", None, "kv"),
        P("req", None, "kv"),
        P(),
        P(),
        P("kv", None),
        P("kv"),
        P(),
        P(),
        P("req", None, "kv"),
        P("req", None, "kv"),
        P("req", "kv", None),
    )
    out_specs = P("req", "kv")
    return jax.shard_map(
        per_device, mesh=mesh, in_specs=in_specs, out_specs=out_specs, check_vma=False
    )
```

time: 777 us -> 226 us (0.29)
  waiting for transfers between devices: 511 us -> 17 us
  blocking collectives: 203 us -> 156 us
  local copies, waits for them, and re-layouts: 28.3 us -> 15.3 us
    unnamed x4 -> x1, waiting for transfers between devices: 511 us -> 0.02 us
    all_gather x4 -> x2, blocking collectives: 195 us -> 114 us  [the longest x1 57.9 us: per_device(): all_packed = lax.all_gather(packed, 'req', axis=0, tiled=True)]
    all_to_all x0 -> x1, blocking collectives: none -> 27.2 us  [per_device(): lax.all_to_all(combined.reshape(req_count, per_dev, col_count), 'req', 0,...]
    reduce_scatter x0 -> x1, waiting for transfers between devices: none -> 16.9 us  [per_device(): weighted = lax.psum_scatter(weighted, 'kv', scatter_dimension=1, tiled=True)]
    reshape x6 -> x2, local copies, waits for them, and re-layouts: 11.8 us -> 1.9 us  [the longest x1 1.88 us: per_device(): combined.reshape(req_count, per_dev, col_count)]
  transfers between devices with their start and end apart: 2 -> 1, of which waited for: 2 -> 1; matrix products, arithmetic and copies ran while one was open for 1% -> 0% of each run, Pallas kernels for 0% -> 0%
where the time goes in v1:
time: 226 us; the launch traced here: 225 us
  blocking collectives  156 us (69%)
  waiting for transfers between devices  17 us (8%)
  local copies, waits for them, and re-layouts  15.3 us (7%)
  between operations  13.6 us (6%)
  other arithmetic  13.1 us (6%)
  matrix products  10.7 us (5%)
    all_gather x1, blocking collectives, per_device(): all_packed = lax.all_gather(packed, 'req', axis=0, tiled=True)  57.9 us
    all_gather x1, blocking collectives, per_device(): by_slot = lax.all_gather(normed, 'req', axis=0, tiled=True)  56.6 us
    all_to_all x1, blocking collectives, per_device(): lax.all_to_all(combined.reshape(req_count, per_dev, col_count), 'req', 0,...  27.2 us
    reduce_scatter x1, waiting for transfers between devices, per_device(): weighted = lax.psum_scatter(weighted, 'kv', scatter_dimension=1, tiled=True)  16.9 us
    psum x1, blocking collectives, per_device(): summed = lax.psum(summed_in, 'kv')  13.9 us
    unnamed x12, local copies, waits for them, and re-layouts  5.18 us
  transfers between devices with their start and end apart: 1, of which 1 were waited for; matrix products, arithmetic and copies ran while one was open for 0% of the time, Pallas kernels for 0%

profile of v1, /device:TPU:1, one launch (start us, length us, event | category | flops | bytes accessed | tf_op | source)
XLA Modules:
  0.0 225.2 jit_solution(8981033612592452208)
XLA Ops:
  6.5 0.9 compare_select_fusion.4
  8.0 0.7 maximum_bitcast_fusion
  8.7 57.9 %all-gather = bf16[64,2,1536]{2,1,0:T(2,128)(2,1)} all-gather(bf16[1,2,1536]{2,1,0:T(2,128)(2,1)S(1)} %maximum_bitcast_fusion), channel_id=1, replica_groups=mesh['req'=64,'kv'=4] {'req'}, dimensions={0}, use_global_device_ids=true | all-gather | bytes 399360 | tf_op jit(solution)/shard_map/all_gather | solution.py:40
  66.6 1.9 reshape.232
  68.5 1.6 gather_fusion.1
  70.2 1.3 gather_fusion
  71.7 2.3 %fusion.51 = (f32[2,5]{1,0:T(2,128)S(1)}, f32[2,5,4096]{2,1,0:T(8,128)S(1)}) fusion(bf16[2,5,128]{2,1,0:T(8,128)(2,1)S(1)} %reshape.151, bf16[2,4096,128]{2,1,0:T(8,128)(2,1)} %param.19, pred[2,4096]{1,0:T(4,128)(4,1)S(1)} %iota_compare_fusion), kind=kOutput, calls=%fused_computation.85 | convolution fusion | flops 10608630 | bytes 2271784 | tf_op jit(solution)/shard_map/rqd,rld->rql/dot_general | solution.py:51
  76.1 2.0 fusion.16
  78.8 13.9 %psum.7 = f32[3,2560]{1,0:T(4,128)S(1)} all-reduce(f32[3,2560]{1,0:T(4,128)S(1)} %add_dynamic-update-slice_fusion), channel_id=1, replica_groups=mesh['req'=64,'kv'=4] {'kv'}, use_global_device_ids=true, to_apply=%region_7.8 | all-reduce | flops 7680 | bytes 61440 | tf_op jit(solution)/shard_map/psum | solution.py:84
  93.6 56.6 %all-gather.1 = bf16[64,2,2560]{2,1,0:T(2,128)(2,1)} all-gather(bf16[1,2,2560]{2,1,0:T(2,128)(2,1)S(1)} %fusion.34), channel_id=1, replica_groups=mesh['req'=64,'kv'=4] {'req'}, dimensions={0}, use_global_device_ids=true | all-gather | bytes 665600 | tf_op jit(solution)/shard_map/all_gather | solution.py:91
  150.2 2.7 %reshape.234 = bf16[128,2560]{1,0:T(8,128)(2,1)} reshape(bf16[64,2,2560]{2,1,0:T(2,128)(2,1)} %all-gather.1) | data formatting | bytes 1310720
  153.3 1.4 scatter_custom_fusion
  154.9 0.8 fusion.32
  155.6 1.0 scatter_custom_fusion.1
  157.5 0.7 gather_fusion.4
  158.9 1.9 gather_fusion.3
  160.8 1.9 fusion.4
  162.8 3.8 %convolution_multiply_fusion.1 = f32[24,2560]{1,0:T(8,128)} fusion(bf16[1,384,2560]{2,1,0:T(8,128)(2,1)} %param.29, bf16[24,2560]{1,0:T(8,128)(2,1)S(1)} %gather_fusion.3, bf16[1,2560,384]{2,1,0:T(8,128)(2,1)} %param.28, f32[24]{0:T(128)S(1)} %compare_select_fusion.5, f32[24,384]{1,0:T(8,128)S(1)} %fusion.4), kind=kOutput, calls=%fused_computation.11 | convolution fusion | flops 94488576 | bytes 4337760 | tf_op jit(solution)/shard_map/dot_general | solution.py:108
  166.5 16.9 %reduce-scatter.2.cloned.1.call-done = f32[24,640]{1,0:T(8,128)} async-done(((f32[24,2560]{1,0:T(8,128)}), f32[24,640]{1,0:T(8,128)}) %reduce-scatter.2.cloned.1.call-update) | async-done | bytes 61456 | tf_op jit(solution)/shard_map/reduce_scatter | solution.py:111
  183.5 1.7 scatter_custom_fusion.2
  185.2 2.4 %scatter_custom_fusion.3 = f32[128,640]{1,0:T(8,128)} fusion(f32[128,640]{1,0:T(8,128)} %scatter_custom_fusion.2, s32[2]{0:T(128)} %copy-done.3, f32[2,2560]{1,0:T(2,128)S(1)} %get-tuple-element.7, s32[]{:T(128)} %constant.31.clone.1, s32[]{:T(128)S(6)} %select_n.104), kind=kCustom, calls=%fused_computation.54 | custom fusion | flops 1280 | bytes 333316 | tf_op jit(solution)/shard_map/scatter-add | solution.py:119
  187.6 1.9 reshape.153
  189.5 27.2 %all_to_all.5 = f32[64,2,640]{2,1,0:T(2,128)} all-to-all(f32[64,2,640]{2,1,0:T(2,128)} %reshape.153), channel_id=1, replica_groups=mesh['req'=64,'kv'=4] {'req'}, dimensions={0} | all-to-all | bytes 655360 | tf_op jit(solution)/shard_map/all_to_all | solution.py:125
  216.7 1.7 reduce_sum.53
  (47 shorter events, 6.5 us)
Async XLA Ops:
  6.5 71.6 %copy-start = (bf16[640,2560]{1,0:T(8,128)(2,1)S(1)}, bf16[640,2560]{1,0:T(8,128)(2,1)}, u32[]{:S(2)}) copy-start(bf16[640,2560]{1,0:T(8,128)(2,1)} %param.23) | copy-start | bytes 9830404
  6.5 176.9 %reduce-scatter.2.cloned.1.call-start = ((), (), s32[]{:S(2)}) async-start(), calls=%async_computation.2 | async-start | bytes 307200 | tf_op jit(solution)/shard_map/reduce_scatter | solution.py:111
  7.4 0.5 copy-start.3
  78.1 14.7 %copy-start.1 = (f32[128,6]{0,1:T(8,128)S(1)}, f32[128,6]{0,1:T(8,128)}, u32[]{:S(2)}) copy-start(f32[128,6]{0,1:T(8,128)} %param.26) | copy-start | bytes 9220
  78.1 14.7 %copy-start.2 = (s32[128,6]{0,1:T(8,128)S(1)}, s32[128,6]{0,1:T(8,128)}, u32[]{:S(2)}) copy-start(s32[128,6]{0,1:T(8,128)} %param.25) | copy-start | bytes 9220
  78.2 14.7 %copy-start.4 = (s32[128]{0:T(128)S(1)}, s32[128]{0:T(128)}, u32[]{:S(2)}) copy-start(s32[128]{0:T(128)} %param.22) | copy-start | bytes 1540
Sparse Core Ops, SparseCore 0:
  166.7 16.7 reduce-scatter.1

commit v2 on v1

--- a/solution.py
+++ b/solution.py
@@ -4,8 +4,6 @@
 import jax.numpy as jnp
 from jax import lax
 from jax.sharding import PartitionSpec as P
-
-COMBINE = "a2a"
 
 
 def per_device(
@@ -37,9 +35,16 @@
     q_width = queries.shape[1]
 
     packed = jnp.concatenate([queries, fresh_token_keys, fresh_token_values, residual_in], axis=1)
-    all_packed = lax.all_gather(packed, "req", axis=0, tiled=True)
+    slot_of = jnp.zeros((total_reqs,), jnp.int32).at[slot_order].set(
+        jnp.arange(total_reqs, dtype=jnp.int32)
+    )
+    home_slots = lax.dynamic_slice_in_dim(slot_of, req_index * per_dev, per_dev)
+    to_slots = jnp.zeros((total_reqs, packed.shape[1]), packed.dtype).at[home_slots].set(packed)
+    from_homes = lax.all_to_all(
+        to_slots.reshape(req_count, per_dev, -1), "req", 0, 0, tiled=False
+    )
     served = lax.dynamic_slice_in_dim(slot_order, req_index * per_dev, per_dev)
-    mine = all_packed[served]
+    mine = from_homes[served // per_dev, jnp.arange(per_dev)]
     query_rows = mine[:, :q_width].reshape(per_dev, -1, head_dim)
     self_key_row = mine[:, q_width:q_width + head_dim]
     self_value_row = mine[:, q_width + head_dim:q_width + 2 * head_dim]
@@ -81,19 +86,27 @@
     ) + lax.dynamic_update_slice(
         jnp.zeros((per_dev + 1, model_width), jnp.float32), own_cols, (0, col_start)
     )
-    summed = lax.psum(summed_in, "kv")
+    summed = summed_in
+    step = 1
+    while step < kv_count:
+        summed = summed + lax.ppermute(
+            summed, "kv", [(i, i ^ step) for i in range(kv_count)]
+        )
+        step *= 2
     hidden = summed[:per_dev]
     gain = summed[per_dev]
     squares = jnp.sum(hidden * hidden, axis=1)
     normed = (hidden * lax.rsqrt(squares / model_width + 1e-06)[:, None] * gain).astype(
         jnp.bfloat16
     )
-    by_slot = lax.all_gather(normed, "req", axis=0, tiled=True)
-    slot_of = jnp.zeros((total_reqs,), jnp.int32).at[slot_order].set(
-        jnp.arange(total_reqs, dtype=jnp.int32)
+    local_count = gate_proj.shape[0]
+    served_ids = expert_ids[served] // local_count
+    wanted = jnp.any(
+        served_ids[None, :, :] == jnp.arange(req_count, dtype=jnp.int32)[:, None, None], axis=2
     )
+    to_experts = jnp.where(wanted[:, :, None], normed[None, :, :], jnp.zeros_like(normed)[None])
+    by_slot = lax.all_to_all(to_experts, "req", 0, 0, tiled=False).reshape(total_reqs, -1)
 
-    local_count = gate_proj.shape[0]
     capacity = min(2 * total_reqs * expert_ids.shape[1] // (local_count * req_count), total_reqs)
     expert = req_index * local_count + 0
     named_here = expert_ids == expert
@@ -108,7 +121,16 @@
     outputs = jnp.dot(inner_act, down_proj[0], preferred_element_type=jnp.float32)
     row_gate = jnp.where(valid_rows, token_gate[picked], 0.0)
     weighted = outputs * row_gate[:, None]
-    weighted = lax.psum_scatter(weighted, "kv", scatter_dimension=1, tiled=True)
+    weighted = jnp.sum(
+        lax.all_to_all(
+            weighted.reshape(capacity, kv_count, col_count).transpose(1, 0, 2),
+            "kv",
+            0,
+            0,
+            tiled=False,
+        ),
+        axis=0,
+    )
 
     own_hidden = lax.dynamic_slice_in_dim(hidden, col_start, col_count, axis=1)
     combined = (
@@ -118,15 +140,10 @@
         .at[served]
         .add(own_hidden)
     )
-    if COMBINE == "rs":
-        layer_rows = lax.psum_scatter(combined, "req", scatter_dimension=0, tiled=True)
-    else:
-        layer_rows = jnp.sum(
-            lax.all_to_all(
-                combined.reshape(req_count, per_dev, col_count), "req", 0, 0, tiled=False
-            ),
-            axis=0,
-        )
+    layer_rows = jnp.sum(
+        lax.all_to_all(combined.reshape(req_count, per_dev, col_count), "req", 0, 0, tiled=False),
+        axis=0,
+    )
     return layer_rows.astype(jnp.bfloat16)
 
 

time: 226 us -> 128 us (0.57)
  blocking collectives: 156 us -> 31 us
  starting transfers between devices: 0.01 us -> 25.4 us
  waiting for transfers between devices: 17 us -> 30.9 us
  between operations: 13.6 us -> 0.25 us
  other arithmetic: 13.1 us -> 15.6 us
    all_gather x2 -> x0, blocking collectives: 114 us -> none  [the longest x1 57.9 us: per_device(): all_packed = lax.all_gather(packed, 'req', axis=0, tiled=True)]
    all_to_all x0 -> x2, waiting for transfers between devices: none -> 28.8 us  [the longest x1 14.6 us: per_device(): lax.all_to_all(to_experts, 'req', 0, 0, tiled=False).reshape(total_reqs, -1)]
    all_to_all x0 -> x2, starting transfers between devices: none -> 21.1 us  [the longest x1 13.1 us: per_device(): lax.all_to_all(to_slots.reshape(req_count, per_dev, -1), 'req', 0, 0, til...]
    reduce_scatter x1 -> x0, waiting for transfers between devices: 16.9 us -> none  [per_device(): weighted = lax.psum_scatter(weighted, 'kv', scatter_dimension=1, tiled=True)]
    psum x1 -> x0, blocking collectives: 13.9 us -> none  [per_device(): summed = lax.psum(summed_in, 'kv')]
    all_to_all x0 -> x1, blocking collectives: none -> 9.46 us  [per_device(): lax.all_to_all(weighted.reshape(capacity, kv_count, col_count).transpose(...]
    all_to_all x1, blocking collectives: 27.2 us -> 21.5 us  [per_device(): lax.all_to_all(combined.reshape(req_count, per_dev, col_count), 'req', 0,...]
    reshape x0 -> x3, local copies, waits for them, and re-layouts: none -> 5.55 us  [the longest x1 2.71 us: per_device(): lax.all_to_all(to_experts, 'req', 0, 0, tiled=False).reshape(total_reqs, -1)]
  transfers between devices with their start and end apart: 1 -> 4, of which waited for: 1 -> 4; matrix products, arithmetic and copies ran while one was open for 0% -> 6% of each run, Pallas kernels for 0% -> 0%
where the time goes in v2:
time: 128 us
  blocking collectives  31 us (24%)
  waiting for transfers between devices  30.9 us (24%)
  starting transfers between devices  25.4 us (20%)
  other arithmetic  15.6 us (12%)
  local copies, waits for them, and re-layouts  15.2 us (12%)
  matrix products  9.21 us (7%)
    all_to_all x1, blocking collectives, per_device(): lax.all_to_all(combined.reshape(req_count, per_dev, col_count), 'req', 0,...  21.5 us
    all_to_all x1, waiting for transfers between devices, per_device(): lax.all_to_all(to_experts, 'req', 0, 0, tiled=False).reshape(total_reqs, -1)  14.6 us
    all_to_all x1, waiting for transfers between devices, per_device(): lax.all_to_all(to_slots.reshape(req_count, per_dev, -1), 'req', 0, 0, til...  14.2 us
    all_to_all x1, starting transfers between devices, per_device(): lax.all_to_all(to_slots.reshape(req_count, per_dev, -1), 'req', 0, 0, til...  13.1 us
    all_to_all x1, blocking collectives, per_device(): lax.all_to_all(weighted.reshape(capacity, kv_count, col_count).transpose(...  9.46 us
    all_to_all x1, starting transfers between devices, per_device(): lax.all_to_all(to_experts, 'req', 0, 0, tiled=False).reshape(total_reqs, -1)  7.91 us
    ppermute x2, starting transfers between devices, per_device(): lax.ppermute(summed, 'kv', [(i, i ^ step) for i in range(kv_count)])  4.38 us
    scatter-add x2, other arithmetic, per_device(): combined = jnp.zeros((total_reqs, col_count), jnp.float32).at[picked].add...  3.98 us
  transfers between devices with their start and end apart: 4, of which 4 were waited for; matrix products, arithmetic and copies ran while one was open for 6% of the time, Pallas kernels for 0%

profile of v2, /device:TPU:1, one launch (start us, length us, event | category | flops | bytes accessed | tf_op | source)
XLA Modules:
  0.0 127.5 jit_solution(7058640959241887330)
XLA Ops:
  0.8 1.0 scatter_custom_fusion.1
  2.6 1.6 %scatter_custom_fusion.2 = bf16[128,1536]{1,0:T(8,128)(2,1)} fusion(s32[2]{0:T(128)S(1)} %get-tuple-element.17, bf16[]{:T(256)} %constant.97.clone.1, bf16[2,640]{1,0:T(2,128)(2,1)} %param.15, bf16[]{:T(256)} %constant.137, bf16[2,128]{1,0:T(2,128)(2,1)} %param.18, bf16[2,128]{1,0:T(2,128)(2,1)} %param.17, bf16[2,640]{1,0:T(2,128)(2,1)} %param.16), kind=kCustom, calls=%fused_computation.30 | custom fusion | flops 24576 | bytes 399364 | tf_op jit(solution)/shard_map/scatter | solution.py:42
  4.2 1.9 %reshape.164 = bf16[64,2,1536]{2,1,0:T(2,128)(2,1)} reshape(bf16[128,1536]{1,0:T(8,128)(2,1)} %scatter_custom_fusion.2) | data formatting | bytes 786432 | tf_op jit(solution)/shard_map/reshape | solution.py:44
  6.0 13.1 %all-to-all-start = ((bf16[64,2,1536]{2,1,0:T(2,128)(2,1)}), bf16[64,2,1536]{2,1,0:T(2,128)(2,1)}, u32[]{:S(2)}, u32[]{:S(2)}) async-start(bf16[64,2,1536]{2,1,0:T(2,128)(2,1)} %reshape.164), calls=%async_computation | async-start | bytes 786432 | tf_op jit(solution)/shard_map/all_to_all | solution.py:43
  20.1 14.2 %all-to-all-done = bf16[64,2,1536]{2,1,0:T(2,128)(2,1)} async-done(((bf16[64,2,1536]{2,1,0:T(2,128)(2,1)}), bf16[64,2,1536]{2,1,0:T(2,128)(2,1)}, u32[]{:S(2)}, u32[]{:S(2)}) %all-to-all-start) | async-done | bytes 393248 | tf_op jit(solution)/shard_map/all_to_all | solution.py:43
  34.3 1.6 %gather_fusion.2 = bf16[2,1536]{1,0:T(2,128)(2,1)S(1)} fusion(bf16[64,2,1536]{2,1,0:T(2,128)(2,1)} %all-to-all-done, s32[2]{0:T(128)S(1)} %fusion.55), kind=kCustom, calls=%fused_computation.2 | custom fusion | bytes 12304 | tf_op jit(solution)/shard_map/gather | solution.py:47
  36.1 2.4 %fusion.65 = (f32[2,5]{1,0:T(2,128)S(1)}, f32[2,5,4096]{2,1,0:T(8,128)S(1)}) fusion(bf16[2,5,128]{2,1,0:T(8,128)(2,1)S(1)} %reshape.165, bf16[2,4096,128]{2,1,0:T(8,128)(2,1)} %param.19, pred[2,4096]{1,0:T(4,128)(4,1)S(1)} %iota_compare_fusion), kind=kOutput, calls=%fused_computation.109 | convolution fusion | flops 10608630 | bytes 2271784 | tf_op jit(solution)/shard_map/rqd,rld->rql/dot_general | solution.py:56
  39.8 1.4 %collective-permute-start = (f32[3,2560]{1,0:T(4,128)S(1)}, f32[3,2560]{1,0:T(4,128)S(1)}, u32[]{:S(2)}, u32[]{:S(2)}) collective-permute-start(f32[3,2560]{1,0:T(4,128)S(1)} %add_dynamic-update-slice_fusion), channel_id=1, source_target_pairs={{0,1},{1,0},{2,3},{3,2},{4,5},{5,4},{6,7},{7,6},{8,9},{9,8},{10,11... | collective-permute-start | bytes 92168 | tf_op jit(solution)/shard_map/ppermute | solution.py:92
  42.8 3.0 %collective-permute-start.1 = (f32[3,2560]{1,0:T(4,128)S(1)}, f32[3,2560]{1,0:T(4,128)S(1)}, u32[]{:S(2)}, u32[]{:S(2)}) collective-permute-start(f32[3,2560]{1,0:T(4,128)S(1)} %add.128), channel_id=1, source_target_pairs={{0,2},{1,3},{2,0},{3,1},{4,6},{5,7},{6,4},{7,5},{8,10},{9,11},{10,... | collective-permute-start | bytes 92168 | tf_op jit(solution)/shard_map/ppermute | solution.py:92
  46.0 1.2 collective-permute-done.1
  47.5 1.4 %broadcast_select_fusion = bf16[64,2,2560]{2,1,0:T(2,128)(2,1)} fusion(pred[64,2]{1,0:T(8,128)(4,1)S(1)} %copy.46, bf16[2,2560]{1,0:T(2,128)(2,1)S(1)} %multiply_convert_fusion), kind=kLoop, calls=%fused_computation.19 | loop fusion | flops 327680 | bytes 665728 | tf_op jit(solution)/shard_map/jit(_where)/select_n | solution.py:107
  48.9 7.9 %all-to-all-start.1 = ((bf16[64,2,2560]{2,1,0:T(2,128)(2,1)}), bf16[64,2,2560]{2,1,0:T(2,128)(2,1)}, u32[]{:S(2)}, u32[]{:S(2)}) async-start(bf16[64,2,2560]{2,1,0:T(2,128)(2,1)} %broadcast_select_fusion), calls=%async_computation.1 | async-start | bytes 1310720 | tf_op jit(solution)/shard_map/all_to_all | solution.py:108
  57.3 1.4 %scatter_custom_fusion = s32[24]{0:T(128)S(1)} fusion(s32[128]{0:T(128)S(1)} %fusion.25, s32[128]{0:T(128)S(1)} %broadcast.228, s32[]{:T(128)} %constant.91.clone.1), kind=kCustom, calls=%fused_computation.102 | custom fusion | flops 128 | bytes 100 | tf_op jit(solution)/shard_map/scatter-add | solution.py:115
  62.5 14.6 %all-to-all-done.1 = bf16[64,2,2560]{2,1,0:T(2,128)(2,1)} async-done(((bf16[64,2,2560]{2,1,0:T(2,128)(2,1)}), bf16[64,2,2560]{2,1,0:T(2,128)(2,1)}, u32[]{:S(2)}, u32[]{:S(2)}) %all-to-all-start.1) | async-done | bytes 655392 | tf_op jit(solution)/shard_map/all_to_all | solution.py:108
  77.1 2.7 %reshape.167 = bf16[128,2560]{1,0:T(8,128)(2,1)} reshape(bf16[64,2,2560]{2,1,0:T(2,128)(2,1)} %all-to-all-done.1) | data formatting | bytes 1310720 | tf_op jit(solution)/shard_map/reshape | solution.py:108
  79.8 1.9 %gather_fusion.4 = bf16[24,2560]{1,0:T(8,128)(2,1)S(1)} fusion(bf16[128,2560]{1,0:T(8,128)(2,1)} %reshape.167, s32[1024]{0:T(1024)S(1)} %pad_clamp_fusion), kind=kCustom, calls=%fused_computation.4 | custom fusion | bytes 245856 | tf_op jit(solution)/shard_map/gather | solution.py:117
  81.7 1.9 %fusion.4 = f32[24,384]{1,0:T(8,128)S(1)} fusion(bf16[24,2560]{1,0:T(8,128)(2,1)S(1)} %gather_fusion.4, bf16[1,2560,384]{2,1,0:T(8,128)(2,1)} %param.27), kind=kOutput, calls=%fused_computation.17 | convolution fusion | flops 47185920 | bytes 2125824 | tf_op jit(solution)/shard_map/dot_general | solution.py:118
  83.7 3.8 %convolution_multiply_fusion.1 = f32[24,2560]{1,0:T(8,128)} fusion(bf16[1,384,2560]{2,1,0:T(8,128)(2,1)} %param.29, bf16[24,2560]{1,0:T(8,128)(2,1)S(1)} %gather_fusion.4, bf16[1,2560,384]{2,1,0:T(8,128)(2,1)} %param.28, f32[24]{0:T(128)S(1)} %compare_select_fusion.6, f32[24,384]{1,0:T(8,128)S(1)} %fusion.4), kind=kOutput, calls=%fused_computation.13 | convolution fusion | flops 94488576 | bytes 4337760 | tf_op jit(solution)/shard_map/dot_general | solution.py:121
  88.4 9.5 %all_to_all.20 = f32[4,24,640]{2,1,0:T(8,128)S(1)} all-to-all(f32[4,24,640]{2,1,0:T(8,128)S(1)} %bitcast.50), channel_id=1, replica_groups=mesh['req'=64,'kv'=4] {'kv'}, dimensions={0} | all-to-all | bytes 491520 | tf_op jit(solution)/shard_map/all_to_all | solution.py:125
  98.5 1.7 %scatter_custom_fusion.3 = f32[128,640]{1,0:T(8,128)} fusion(s32[24]{0:T(128)S(1)} %fusion.34, f32[24,640]{1,0:T(8,128)} %reduce_sum.62, f32[]{:T(128)} %constant.50.clone.1), kind=kCustom, calls=%fused_computation.33 | custom fusion | flops 15360 | bytes 328192 | tf_op jit(solution)/shard_map/scatter-add | solution.py:139
  100.2 2.2 %scatter_custom_fusion.4 = f32[128,640]{1,0:T(8,128)} fusion(f32[128,640]{1,0:T(8,128)} %scatter_custom_fusion.3, s32[2]{0:T(128)S(1)} %get-tuple-element.18, f32[2,2560]{1,0:T(2,128)S(1)} %get-tuple-element.7, s32[]{:T(128)} %constant.91.clone.1, s32[]{:T(128)S(6)} %select_n.129), kind=kCustom, calls=%fused_computation.67 | custom fusion | flops 1280 | bytes 333316 | tf_op jit(solution)/shard_map/scatter-add | solution.py:141
  102.5 1.9 %reshape.169 = f32[64,2,640]{2,1,0:T(2,128)} reshape(f32[128,640]{1,0:T(8,128)} %scatter_custom_fusion.4) | data formatting | bytes 655360 | tf_op jit(solution)/shard_map/reshape | solution.py:144
  104.3 21.5 %all_to_all.21 = f32[64,2,640]{2,1,0:T(2,128)} all-to-all(f32[64,2,640]{2,1,0:T(2,128)} %reshape.169), channel_id=1, replica_groups=mesh['req'=64,'kv'=4] {'req'}, dimensions={0} | all-to-all | bytes 655360 | tf_op jit(solution)/shard_map/all_to_all | solution.py:144
  125.8 1.7 %reduce_sum.63 = bf16[2,640]{1,0:T(2,128)(2,1)} reduce(f32[64,2,640]{2,1,0:T(2,128)} %all_to_all.21, f32[]{:T(128)} %constant.50.clone.1), dimensions={0}, to_apply=%region_15.16 | reduce | flops 80640 | bytes 330244 | tf_op jit(solution)/shard_map/reduce_sum | solution.py:143
  (65 shorter events, 11.7 us)
Async XLA Ops:
  0.0 39.2 %copy-start = (bf16[640,2560]{1,0:T(8,128)(2,1)S(1)}, bf16[640,2560]{1,0:T(8,128)(2,1)}, u32[]{:S(2)}) copy-start(bf16[640,2560]{1,0:T(8,128)(2,1)} %param.23) | copy-start | bytes 9830404
  0.0 19.2 %copy-start.6 = (s32[128]{0:T(128)S(1)}, s32[128]{0:T(128)}, u32[]{:S(2)}) copy-start(s32[128]{0:T(128)} %param.22) | copy-start | bytes 1540
  0.0 19.3 %copy-start.5 = (bf16[640]{0:T(1024)(128)(2,1)S(1)}, bf16[640]{0:T(1024)(128)(2,1)}, u32[]{:S(2)}) copy-start(bf16[640]{0:T(1024)(128)(2,1)} %param.24) | copy-start | bytes 3844
  0.0 19.3 %copy-start.1 = (s32[128]{0:T(128)S(1)}, s32[128]{0:T(128)}, u32[]{:S(2)}) copy-start(s32[128]{0:T(128)} %param.21) | copy-start | bytes 1540
  6.0 28.3 %all-to-all-start = ((bf16[64,2,1536]{2,1,0:T(2,128)(2,1)}), bf16[64,2,1536]{2,1,0:T(2,128)(2,1)}, u32[]{:S(2)}, u32[]{:S(2)}) async-start(bf16[64,2,1536]{2,1,0:T(2,128)(2,1)} %reshape.164), calls=%async_computation | async-start | bytes 786432 | tf_op jit(solution)/shard_map/all_to_all | solution.py:43
  35.9 2.8 %copy-start.2 = (bf16[2,4096,128]{2,1,0:T(8,128)(2,1)S(1)}, bf16[2,4096,128]{2,1,0:T(8,128)(2,1)}, u32[]{:S(2)}) copy-start(bf16[2,4096,128]{2,1,0:T(8,128)(2,1)} %param.20) | copy-start | bytes 6291460
  39.2 2.0 %copy-start.3 = (s32[128,6]{0,1:T(8,128)S(1)}, s32[128,6]{0,1:T(8,128)}, u32[]{:S(2)}) copy-start(s32[128,6]{0,1:T(8,128)} %param.25) | copy-start | bytes 9220
  39.8 17.0 %copy-start.4 = (f32[128,6]{0,1:T(8,128)S(1)}, f32[128,6]{0,1:T(8,128)}, u32[]{:S(2)}) copy-start(f32[128,6]{0,1:T(8,128)} %param.26) | copy-start | bytes 9220
  39.8 2.9 %collective-permute-start = (f32[3,2560]{1,0:T(4,128)S(1)}, f32[3,2560]{1,0:T(4,128)S(1)}, u32[]{:S(2)}, u32[]{:S(2)}) collective-permute-start(f32[3,2560]{1,0:T(4,128)S(1)} %add_dynamic-update-slice_fusion), channel_id=1, source_target_pairs={{0,1},{1,0},{2,3},{3,2},{4,5},{5,4},{6,7},{7,6},{8,9},{9,8},{10,11... | collective-permute-start | bytes 92168 | tf_op jit(solution)/shard_map/ppermute | solution.py:92
  42.8 4.4 %collective-permute-start.1 = (f32[3,2560]{1,0:T(4,128)S(1)}, f32[3,2560]{1,0:T(4,128)S(1)}, u32[]{:S(2)}, u32[]{:S(2)}) collective-permute-start(f32[3,2560]{1,0:T(4,128)S(1)} %add.128), channel_id=1, source_target_pairs={{0,2},{1,3},{2,0},{3,1},{4,6},{5,7},{6,4},{7,5},{8,10},{9,11},{10,... | collective-permute-start | bytes 92168 | tf_op jit(solution)/shard_map/ppermute | solution.py:92
  48.9 28.2 %all-to-all-start.1 = ((bf16[64,2,2560]{2,1,0:T(2,128)(2,1)}), bf16[64,2,2560]{2,1,0:T(2,128)(2,1)}, u32[]{:S(2)}, u32[]{:S(2)}) async-start(bf16[64,2,2560]{2,1,0:T(2,128)(2,1)} %broadcast_select_fusion), calls=%async_computation.1 | async-start | bytes 1310720 | tf_op jit(solution)/shard_map/all_to_all | solution.py:108

commit v3 on v2

--- a/solution.py
+++ b/solution.py
@@ -39,10 +39,12 @@
         jnp.arange(total_reqs, dtype=jnp.int32)
     )
     home_slots = lax.dynamic_slice_in_dim(slot_of, req_index * per_dev, per_dev)
-    to_slots = jnp.zeros((total_reqs, packed.shape[1]), packed.dtype).at[home_slots].set(packed)
-    from_homes = lax.all_to_all(
-        to_slots.reshape(req_count, per_dev, -1), "req", 0, 0, tiled=False
+    to_slots = (
+        jnp.zeros((req_count, per_dev, packed.shape[1]), packed.dtype)
+        .at[home_slots // per_dev, home_slots % per_dev]
+        .set(packed)
     )
+    from_homes = lax.all_to_all(to_slots, "req", 0, 0, tiled=False)
     served = lax.dynamic_slice_in_dim(slot_order, req_index * per_dev, per_dev)
     mine = from_homes[served // per_dev, jnp.arange(per_dev)]
     query_rows = mine[:, :q_width].reshape(per_dev, -1, head_dim)
@@ -86,13 +88,14 @@
     ) + lax.dynamic_update_slice(
         jnp.zeros((per_dev + 1, model_width), jnp.float32), own_cols, (0, col_start)
     )
-    summed = summed_in
-    step = 1
-    while step < kv_count:
-        summed = summed + lax.ppermute(
-            summed, "kv", [(i, i ^ step) for i in range(kv_count)]
-        )
-        step *= 2
+    parts = [summed_in] + [
+        lax.ppermute(summed_in, "kv", [(i, (i + shift) % kv_count) for i in range(kv_count)])
+        for shift in range(1, kv_count)
+    ]
+    stacked = jnp.stack(parts)[(kv_index - jnp.arange(kv_count)) % kv_count]
+    summed = stacked[0]
+    for source in range(1, kv_count):
+        summed = summed + stacked[source]
     hidden = summed[:per_dev]
     gain = summed[per_dev]
     squares = jnp.sum(hidden * hidden, axis=1)
@@ -105,7 +108,7 @@
         served_ids[None, :, :] == jnp.arange(req_count, dtype=jnp.int32)[:, None, None], axis=2
     )
     to_experts = jnp.where(wanted[:, :, None], normed[None, :, :], jnp.zeros_like(normed)[None])
-    by_slot = lax.all_to_all(to_experts, "req", 0, 0, tiled=False).reshape(total_reqs, -1)
+    by_slot = lax.all_to_all(to_experts, "req", 0, 0, tiled=False)
 
     capacity = min(2 * total_reqs * expert_ids.shape[1] // (local_count * req_count), total_reqs)
     expert = req_index * local_count + 0
@@ -114,36 +117,34 @@
     uses_expert = jnp.any(named_here, axis=1)
     picked = jnp.nonzero(uses_expert, size=capacity, fill_value=0)[0].astype(jnp.int32)
     valid_rows = jnp.arange(capacity) < jnp.sum(uses_expert.astype(jnp.int32))
-    row_block = by_slot[slot_of[picked]]
+    picked_slots = slot_of[picked]
+    row_block = by_slot[picked_slots // per_dev, picked_slots % per_dev]
     gate_h = jnp.dot(row_block, gate_proj[0], preferred_element_type=jnp.float32)
     up_h = jnp.dot(row_block, up_proj[0], preferred_element_type=jnp.float32)
     inner_act = (jax.nn.silu(gate_h) * up_h).astype(jnp.bfloat16)
     outputs = jnp.dot(inner_act, down_proj[0], preferred_element_type=jnp.float32)
     row_gate = jnp.where(valid_rows, token_gate[picked], 0.0)
     weighted = outputs * row_gate[:, None]
-    weighted = jnp.sum(
-        lax.all_to_all(
-            weighted.reshape(capacity, kv_count, col_count).transpose(1, 0, 2),
+    weighted = lax.dynamic_slice_in_dim(weighted, col_start, col_count, axis=1) + sum(
+        lax.ppermute(
+            lax.dynamic_slice_in_dim(
+                weighted, ((kv_index + shift) % kv_count) * col_count, col_count, axis=1
+            ),
             "kv",
-            0,
-            0,
-            tiled=False,
-        ),
-        axis=0,
+            [(i, (i + shift) % kv_count) for i in range(kv_count)],
+        )
+        for shift in range(1, kv_count)
     )
 
     own_hidden = lax.dynamic_slice_in_dim(hidden, col_start, col_count, axis=1)
     combined = (
-        jnp.zeros((total_reqs, col_count), jnp.float32)
-        .at[picked]
+        jnp.zeros((req_count, per_dev, col_count), jnp.float32)
+        .at[picked // per_dev, picked % per_dev]
         .add(weighted)
-        .at[served]
+        .at[served // per_dev, served % per_dev]
         .add(own_hidden)
     )
-    layer_rows = jnp.sum(
-        lax.all_to_all(combined.reshape(req_count, per_dev, col_count), "req", 0, 0, tiled=False),
-        axis=0,
-    )
+    layer_rows = jnp.sum(lax.all_to_all(combined, "req", 0, 0, tiled=False), axis=0)
     return layer_rows.astype(jnp.bfloat16)
 
 

time: 128 us -> 128 us (level)
  blocking collectives: 31 us -> 21.9 us
  other arithmetic: 15.6 us -> 20.1 us
  starting transfers between devices: 25.4 us -> 28.9 us
    all_to_all x2 -> x1, blocking collectives: 31 us -> 21.9 us  [per_device(): lax.all_to_all(combined, 'req', 0, 0, tiled=False)]
    reshape x4 -> x0, local copies, waits for them, and re-layouts: 7.44 us -> none  [the longest x1 2.71 us: per_device(): lax.all_to_all(to_experts, 'req', 0, 0, tiled=False).reshape(total_reqs, -1)]
    all_to_all x2, waiting for transfers between devices: 28.8 us -> 24.6 us  [the longest x1 14.5 us: per_device(): by_slot = lax.all_to_all(to_experts, 'req', 0, 0, tiled=False)]
    ppermute x2 -> x6, starting transfers between devices: 4.38 us -> 8.6 us  [the longest x3 5.06 us: per_device(): lax.ppermute(summed_in, 'kv', [(i, (i + shift) % kv_count) for i in range...]
    ppermute x2 -> x6, waiting for transfers between devices: 2.12 us -> 5.43 us  [the longest x3 3.59 us: per_device(): lax.ppermute(lax.dynamic_slice_in_dim(weighted, (kv_index + shift) % kv_c...]
    scatter-add x2, other arithmetic: 3.98 us -> 6.68 us  [per_device(): combined = jnp.zeros((req_count, per_dev, col_count), jnp.float32).at[pic...]
    scatter x0 -> x1, local copies, waits for them, and re-layouts: none -> 2.01 us  [per_device(): to_slots = jnp.zeros((req_count, per_dev, packed.shape[1]), packed.dtype)...]
    broadcast_in_dim x0 -> x2, local copies, waits for them, and re-layouts: none -> 1.75 us  [the longest x1 0.95 us: per_device(): jnp.zeros((req_count, per_dev, packed.shape[1]), packed.dtype)]
  transfers between devices with their start and end apart: 4 -> 8, of which waited for: 4 -> 7; matrix products, arithmetic and copies ran while one was open for 6% -> 9% of each run, Pallas kernels for 0% -> 0%
where the time goes in v3:
time: 128 us; the launch traced here: 127 us
  waiting for transfers between devices  30 us (23%)
  starting transfers between devices  28.9 us (23%)
  blocking collectives  21.9 us (17%)
  other arithmetic  20.1 us (16%)
  local copies, waits for them, and re-layouts  16.3 us (13%)
  matrix products  9.23 us (7%)
    all_to_all x1, blocking collectives, per_device(): lax.all_to_all(combined, 'req', 0, 0, tiled=False)  21.9 us
    all_to_all x1, waiting for transfers between devices, per_device(): by_slot = lax.all_to_all(to_experts, 'req', 0, 0, tiled=False)  14.5 us
    all_to_all x1, starting transfers between devices, per_device(): from_homes = lax.all_to_all(to_slots, 'req', 0, 0, tiled=False)  13.1 us
    all_to_all x1, waiting for transfers between devices, per_device(): from_homes = lax.all_to_all(to_slots, 'req', 0, 0, tiled=False)  10.1 us
    all_to_all x1, starting transfers between devices, per_device(): by_slot = lax.all_to_all(to_experts, 'req', 0, 0, tiled=False)  7.14 us
    scatter-add x2, other arithmetic, per_device(): combined = jnp.zeros((req_count, per_dev, col_count), jnp.float32).at[pic...  6.68 us
    ppermute x3, starting transfers between devices, per_device(): lax.ppermute(summed_in, 'kv', [(i, (i + shift) % kv_count) for i in range...  5.06 us
    dot_general x1, matrix products, per_device(): jnp.dot(inner_act, down_proj[0], preferred_element_type=jnp.float32)  3.76 us
  transfers between devices with their start and end apart: 8, of which 7 were waited for; matrix products, arithmetic and copies ran while one was open for 9% of the time, Pallas kernels for 0%

profile of v3, /device:TPU:1, one launch (start us, length us, event | category | flops | bytes accessed | tf_op | source)
XLA Modules:
  0.0 126.7 jit_solution(12014633565944569944)
XLA Ops:
  3.6 2.0 %scatter_fusion = bf16[64,2,1536]{2,1,0:T(2,128)(2,1)} fusion(bf16[64,2,1536]{2,1,0:T(2,128)(2,1)} %broadcast_in_dim.116, s32[2]{0:T(128)S(1)} %fusion.64, bf16[2,1536]{1,0:T(2,128)(2,1)S(1)} %pad_maximum_fusion.1), kind=kCustom, calls=%fused_computation.9 | custom fusion | bytes 18448 | tf_op jit(solution)/shard_map/scatter | solution.py:45
  5.6 13.1 %all-to-all-start = ((bf16[64,2,1536]{2,1,0:T(2,128)(2,1)}), bf16[64,2,1536]{2,1,0:T(2,128)(2,1)}, u32[]{:S(2)}, u32[]{:S(2)}) async-start(bf16[64,2,1536]{2,1,0:T(2,128)(2,1)} %scatter_fusion), calls=%async_computation | async-start | bytes 786432 | tf_op jit(solution)/shard_map/all_to_all | solution.py:47
  21.7 1.3 %gather_fusion.1 = s32[2]{0:T(128)S(1)} fusion(s32[128]{0:T(128)} %param.21, s32[1024]{0:T(1024)S(1)} %pad_clamp_fusion.2), kind=kCustom, calls=%fused_computation.1 | custom fusion | bytes 24 | tf_op jit(solution)/shard_map/gather | solution.py:54
  23.8 10.1 %all-to-all-done = bf16[64,2,1536]{2,1,0:T(2,128)(2,1)} async-done(((bf16[64,2,1536]{2,1,0:T(2,128)(2,1)}), bf16[64,2,1536]{2,1,0:T(2,128)(2,1)}, u32[]{:S(2)}, u32[]{:S(2)}) %all-to-all-start) | async-done | bytes 393248 | tf_op jit(solution)/shard_map/all_to_all | solution.py:47
  33.8 1.6 %gather_fusion.2 = bf16[2,1536]{1,0:T(2,128)(2,1)S(1)} fusion(bf16[64,2,1536]{2,1,0:T(2,128)(2,1)} %all-to-all-done, s32[2]{0:T(128)S(1)} %get-tuple-element.19), kind=kCustom, calls=%fused_computation.2 | custom fusion | bytes 12304 | tf_op jit(solution)/shard_map/gather | solution.py:49
  35.6 2.4 %fusion.74 = (f32[2,5]{1,0:T(2,128)S(1)}, f32[2,5,4096]{2,1,0:T(8,128)S(1)}) fusion(bf16[2,5,128]{2,1,0:T(8,128)(2,1)S(1)} %reshape.366, bf16[2,4096,128]{2,1,0:T(8,128)(2,1)} %param.19, pred[2,4096]{1,0:T(4,128)(4,1)S(1)} %iota_compare_fusion), kind=kOutput, calls=%fused_computation.166 | convolution fusion | flops 10608630 | bytes 2271784 | tf_op jit(solution)/shard_map/rqd,rld->rql/dot_general | solution.py:58
  39.4 1.4 %collective-permute-start = (f32[3,2560]{1,0:T(4,128)S(1)}, f32[3,2560]{1,0:T(4,128)S(1)}, u32[]{:S(2)}, u32[]{:S(2)}) collective-permute-start(f32[3,2560]{1,0:T(4,128)S(1)} %add_dynamic-update-slice_fusion), channel_id=1, source_target_pairs={{0,1},{1,2},{2,3},{3,0},{4,5},{5,6},{6,7},{7,4},{8,9},{9,10},{10,1... | collective-permute-start | bytes 92168 | tf_op jit(solution)/shard_map/ppermute | solution.py:92
  40.7 2.6 %collective-permute-start.1 = (f32[3,2560]{1,0:T(4,128)S(1)}, f32[3,2560]{1,0:T(4,128)S(1)}, u32[]{:S(2)}, u32[]{:S(2)}) collective-permute-start(f32[3,2560]{1,0:T(4,128)S(1)} %add_dynamic-update-slice_fusion), channel_id=1, source_target_pairs={{0,2},{1,3},{2,0},{3,1},{4,6},{5,7},{6,4},{7,5},{8,10},{9,11},{10,... | collective-permute-start | bytes 92168 | tf_op jit(solution)/shard_map/ppermute | solution.py:92
  43.4 1.1 collective-permute-start.2
  45.3 1.1 collective-permute-done.2
  47.8 1.3 %gather_fusion.3 = f32[4,3,2560]{2,1,0:T(4,128)} fusion(f32[4,3,2560]{2,1,0:T(4,128)S(1)} %pad_maximum_fusion, s32[1024]{0:T(1024)S(1)} %pad_clamp_fusion.1), kind=kCustom, calls=%fused_computation.3 | custom fusion | bytes 245776 | tf_op jit(solution)/shard_map/gather | solution.py:95
  50.3 1.4 %broadcast_select_fusion = bf16[64,2,2560]{2,1,0:T(2,128)(2,1)} fusion(pred[64,2]{1,0:T(8,128)(4,1)S(1)} %copy.41, bf16[2,2560]{1,0:T(2,128)(2,1)S(1)} %fusion.29), kind=kLoop, calls=%fused_computation.20 | loop fusion | flops 327680 | bytes 665728 | tf_op jit(solution)/shard_map/jit(_where)/select_n | solution.py:110
  51.7 7.1 %all-to-all-start.1 = ((bf16[64,2,2560]{2,1,0:T(2,128)(2,1)}), bf16[64,2,2560]{2,1,0:T(2,128)(2,1)}, u32[]{:S(2)}, u32[]{:S(2)}) async-start(bf16[64,2,2560]{2,1,0:T(2,128)(2,1)} %broadcast_select_fusion), calls=%async_computation.1 | async-start | bytes 1310720 | tf_op jit(solution)/shard_map/all_to_all | solution.py:111
  59.3 1.4 %scatter_custom_fusion = s32[24]{0:T(128)S(1)} fusion(s32[128]{0:T(128)S(1)} %fusion.21, s32[128]{0:T(128)S(1)} %broadcast.649, s32[]{:T(128)} %constant.174.clone.1), kind=kCustom, calls=%fused_computation.160 | custom fusion | flops 128 | bytes 100 | tf_op jit(solution)/shard_map/scatter-add | solution.py:118
  64.6 14.5 %all-to-all-done.1 = bf16[64,2,2560]{2,1,0:T(2,128)(2,1)} async-done(((bf16[64,2,2560]{2,1,0:T(2,128)(2,1)}), bf16[64,2,2560]{2,1,0:T(2,128)(2,1)}, u32[]{:S(2)}, u32[]{:S(2)}) %all-to-all-start.1) | async-done | bytes 655392 | tf_op jit(solution)/shard_map/all_to_all | solution.py:111
  79.1 2.0 %gather_fusion.5 = bf16[24,2560]{1,0:T(8,128)(2,1)S(1)} fusion(bf16[64,2,2560]{2,1,0:T(2,128)(2,1)} %all-to-all-done.1, s32[24]{0:T(128)S(1)} %fusion.44), kind=kCustom, calls=%fused_computation.5 | custom fusion | bytes 245952 | tf_op jit(solution)/shard_map/gather | solution.py:121
  81.1 1.9 %fusion.4 = f32[24,384]{1,0:T(8,128)S(1)} fusion(bf16[24,2560]{1,0:T(8,128)(2,1)S(1)} %gather_fusion.5, bf16[1,2560,384]{2,1,0:T(8,128)(2,1)} %param.27), kind=kOutput, calls=%fused_computation.18 | convolution fusion | flops 47185920 | bytes 2125824 | tf_op jit(solution)/shard_map/dot_general | solution.py:122
  83.0 3.8 %convolution_multiply_fusion.1 = f32[24,2560]{1,0:T(8,128)} fusion(bf16[1,384,2560]{2,1,0:T(8,128)(2,1)} %param.29, bf16[24,2560]{1,0:T(8,128)(2,1)S(1)} %gather_fusion.5, bf16[1,2560,384]{2,1,0:T(8,128)(2,1)} %param.28, f32[24]{0:T(128)S(1)} %compare_select_fusion.13, f32[24,384]{1,0:T(8,128)S(1)} %fusion.4), kind=kOutput, calls=%fused_computation.14 | convolution fusion | flops 94488576 | bytes 4337760 | tf_op jit(solution)/shard_map/dot_general | solution.py:125
  87.8 3.4 %collective-permute-start.4 = (f32[24,640]{1,0:T(8,128)S(1)}, f32[24,640]{1,0:T(8,128)S(1)}, u32[]{:S(2)}, u32[]{:S(2)}) collective-permute-start(f32[24,640]{1,0:T(8,128)S(1)} %get-tuple-element.9), channel_id=1, source_target_pairs={{0,2},{1,3},{2,0},{3,1},{4,6},{5,7},{6,4},{7,5},{8,10},{9,11},{10,... | collective-permute-start | bytes 184328 | tf_op jit(solution)/shard_map/ppermute | solution.py:129
  92.0 1.8 %collective-permute-done.4 = f32[24,640]{1,0:T(8,128)S(1)} collective-permute-done((f32[24,640]{1,0:T(8,128)S(1)}, f32[24,640]{1,0:T(8,128)S(1)}, u32[]{:S(2)}, u32[]{:S(2)}) %collective-permute-start.4) | collective-permute-done | bytes 61472 | tf_op jit(solution)/shard_map/ppermute | solution.py:129
  96.4 4.7 %scatter_fusion.1 = f32[64,2,640]{2,1,0:T(2,128)} fusion(f32[64,2,640]{2,1,0:T(2,128)} %broadcast_in_dim.110, s32[24]{0:T(128)S(1)} %get-tuple-element.6, f32[24,640]{1,0:T(8,128)S(1)} %add_add_fusion), kind=kCustom, calls=%fused_computation.10 | custom fusion | flops 15360 | bytes 184512 | tf_op jit(solution)/shard_map/scatter-add | solution.py:143
  101.2 2.0 %scatter_fusion.2 = f32[64,2,640]{2,1,0:T(2,128)} fusion(f32[64,2,640]{2,1,0:T(2,128)} %scatter_fusion.1, s32[2]{0:T(128)S(1)} %get-tuple-element.18, f32[2,640]{1,0:T(2,128)S(1)} %dynamic-slice_bitcast_fusion), kind=kCustom, calls=%fused_computation.11 | custom fusion | flops 1280 | bytes 15376 | tf_op jit(solution)/shard_map/scatter-add | solution.py:145
  103.1 21.9 %all_to_all.15 = f32[64,2,640]{2,1,0:T(2,128)} all-to-all(f32[64,2,640]{2,1,0:T(2,128)} %scatter_fusion.2), channel_id=1, replica_groups=mesh['req'=64,'kv'=4] {'req'}, dimensions={0} | all-to-all | bytes 655360 | tf_op jit(solution)/shard_map/all_to_all | solution.py:147
  125.0 1.7 %reduce_sum.53 = bf16[2,640]{1,0:T(2,128)(2,1)} reduce(f32[64,2,640]{2,1,0:T(2,128)} %all_to_all.15, f32[]{:T(128)} %constant.170.clone.1), dimensions={0}, to_apply=%region_14.15 | reduce | flops 80640 | bytes 330244 | tf_op jit(solution)/shard_map/reduce_sum | solution.py:147
  (78 shorter events, 20.9 us)
Async XLA Ops:
  0.0 38.8 %copy-start = (bf16[640,2560]{1,0:T(8,128)(2,1)S(1)}, bf16[640,2560]{1,0:T(8,128)(2,1)}, u32[]{:S(2)}) copy-start(bf16[640,2560]{1,0:T(8,128)(2,1)} %param.23) | copy-start | bytes 9830404
  5.6 28.2 %all-to-all-start = ((bf16[64,2,1536]{2,1,0:T(2,128)(2,1)}), bf16[64,2,1536]{2,1,0:T(2,128)(2,1)}, u32[]{:S(2)}, u32[]{:S(2)}) async-start(bf16[64,2,1536]{2,1,0:T(2,128)(2,1)} %scatter_fusion), calls=%async_computation | async-start | bytes 786432 | tf_op jit(solution)/shard_map/all_to_all | solution.py:47
  35.5 2.8 %copy-start.1 = (bf16[2,4096,128]{2,1,0:T(8,128)(2,1)S(1)}, bf16[2,4096,128]{2,1,0:T(8,128)(2,1)}, u32[]{:S(2)}) copy-start(bf16[2,4096,128]{2,1,0:T(8,128)(2,1)} %param.20) | copy-start | bytes 6291460
  39.3 19.6 %copy-start.5 = (s32[128,6]{0,1:T(8,128)S(1)}, s32[128,6]{0,1:T(8,128)}, u32[]{:S(2)}) copy-start(s32[128,6]{0,1:T(8,128)} %param.25) | copy-start | bytes 9220
  39.3 19.6 %copy-start.6 = (f32[128,6]{0,1:T(8,128)S(1)}, f32[128,6]{0,1:T(8,128)}, u32[]{:S(2)}) copy-start(f32[128,6]{0,1:T(8,128)} %param.26) | copy-start | bytes 9220
  39.4 5.2 %collective-permute-start = (f32[3,2560]{1,0:T(4,128)S(1)}, f32[3,2560]{1,0:T(4,128)S(1)}, u32[]{:S(2)}, u32[]{:S(2)}) collective-permute-start(f32[3,2560]{1,0:T(4,128)S(1)} %add_dynamic-update-slice_fusion), channel_id=1, source_target_pairs={{0,1},{1,2},{2,3},{3,0},{4,5},{5,6},{6,7},{7,4},{8,9},{9,10},{10,1... | collective-permute-start | bytes 92168 | tf_op jit(solution)/shard_map/ppermute | solution.py:92
  40.7 4.6 %collective-permute-start.1 = (f32[3,2560]{1,0:T(4,128)S(1)}, f32[3,2560]{1,0:T(4,128)S(1)}, u32[]{:S(2)}, u32[]{:S(2)}) collective-permute-start(f32[3,2560]{1,0:T(4,128)S(1)} %add_dynamic-update-slice_fusion), channel_id=1, source_target_pairs={{0,2},{1,3},{2,0},{3,1},{4,6},{5,7},{6,4},{7,5},{8,10},{9,11},{10,... | collective-permute-start | bytes 92168 | tf_op jit(solution)/shard_map/ppermute | solution.py:92
  43.4 3.0 %collective-permute-start.2 = (f32[3,2560]{1,0:T(4,128)S(1)}, f32[3,2560]{1,0:T(4,128)S(1)}, u32[]{:S(2)}, u32[]{:S(2)}) collective-permute-start(f32[3,2560]{1,0:T(4,128)S(1)} %add_dynamic-update-slice_fusion), channel_id=1, source_target_pairs={{0,3},{1,0},{2,1},{3,2},{4,7},{5,4},{6,5},{7,6},{8,11},{9,8},{10,9... | collective-permute-start | bytes 92168 | tf_op jit(solution)/shard_map/ppermute | solution.py:92
  45.3 1.1 copy-start.3
  46.4 0.6 copy-start.4
  50.0 31.1 %copy-start.2 = (f32[1,3,2560]{2,1,0:T(4,128)}, f32[1,3,2560]{2,1,0:T(4,128)S(1)}, u32[]{:S(2)}) copy-start(f32[1,3,2560]{2,1,0:T(4,128)S(1)} %slice_add_fusion) | copy-start | bytes 92164
  51.7 27.4 %all-to-all-start.1 = ((bf16[64,2,2560]{2,1,0:T(2,128)(2,1)}), bf16[64,2,2560]{2,1,0:T(2,128)(2,1)}, u32[]{:S(2)}, u32[]{:S(2)}) async-start(bf16[64,2,2560]{2,1,0:T(2,128)(2,1)} %broadcast_select_fusion), calls=%async_computation.1 | async-start | bytes 1310720 | tf_op jit(solution)/shard_map/all_to_all | solution.py:111
  83.0 8.2 %slice-start = ((f32[1,3,2560]{2,1,0:T(4,128)}), f32[1,2,2560]{2,1,0:T(2,128)S(1)}, s32[]{:S(2)}) async-start(f32[1,3,2560]{2,1,0:T(4,128)} %copy-done.2), calls=%async_computation.3 | async-start | bytes 40960 | tf_op jit(solution)/shard_map/slice | solution.py:99
  87.7 4.4 %collective-permute-start.3 = (f32[24,640]{1,0:T(8,128)S(1)}, f32[24,640]{1,0:T(8,128)S(1)}, u32[]{:S(2)}, u32[]{:S(2)}) collective-permute-start(f32[24,640]{1,0:T(8,128)S(1)} %get-tuple-element.11), channel_id=1, source_target_pairs={{0,1},{1,2},{2,3},{3,0},{4,5},{5,6},{6,7},{7,4},{8,9},{9,10},{10,1... | collective-permute-start | bytes 184328 | tf_op jit(solution)/shard_map/ppermute | solution.py:129
  87.8 6.1 %collective-permute-start.4 = (f32[24,640]{1,0:T(8,128)S(1)}, f32[24,640]{1,0:T(8,128)S(1)}, u32[]{:S(2)}, u32[]{:S(2)}) collective-permute-start(f32[24,640]{1,0:T(8,128)S(1)} %get-tuple-element.9), channel_id=1, source_target_pairs={{0,2},{1,3},{2,0},{3,1},{4,6},{5,7},{6,4},{7,5},{8,10},{9,11},{10,... | collective-permute-start | bytes 184328 | tf_op jit(solution)/shard_map/ppermute | solution.py:129
  91.2 3.6 %collective-permute-start.5 = (f32[24,640]{1,0:T(8,128)S(1)}, f32[24,640]{1,0:T(8,128)S(1)}, u32[]{:S(2)}, u32[]{:S(2)}) collective-permute-start(f32[24,640]{1,0:T(8,128)S(1)} %get-tuple-element.10), channel_id=1, source_target_pairs={{0,3},{1,0},{2,1},{3,2},{4,7},{5,4},{6,5},{7,6},{8,11},{9,8},{10,9... | collective-permute-start | bytes 184328 | tf_op jit(solution)/shard_map/ppermute | solution.py:129

commit v4 on v3

--- a/solution.py
+++ b/solution.py
@@ -38,11 +38,11 @@
     slot_of = jnp.zeros((total_reqs,), jnp.int32).at[slot_order].set(
         jnp.arange(total_reqs, dtype=jnp.int32)
     )
-    home_slots = lax.dynamic_slice_in_dim(slot_of, req_index * per_dev, per_dev)
-    to_slots = (
-        jnp.zeros((req_count, per_dev, packed.shape[1]), packed.dtype)
-        .at[home_slots // per_dev, home_slots % per_dev]
-        .set(packed)
+    slots_grid = slot_order.reshape(req_count, per_dev)
+    to_slots = jnp.where(
+        (slots_grid // per_dev == req_index)[:, :, None],
+        packed[slots_grid % per_dev],
+        jnp.zeros((), packed.dtype),
     )
     from_homes = lax.all_to_all(to_slots, "req", 0, 0, tiled=False)
     served = lax.dynamic_slice_in_dim(slot_order, req_index * per_dev, per_dev)
@@ -137,12 +137,13 @@
     )
 
     own_hidden = lax.dynamic_slice_in_dim(hidden, col_start, col_count, axis=1)
-    combined = (
-        jnp.zeros((req_count, per_dev, col_count), jnp.float32)
-        .at[picked // per_dev, picked % per_dev]
-        .add(weighted)
-        .at[served // per_dev, served % per_dev]
-        .add(own_hidden)
+    at_pick = jnp.where(uses_expert, jnp.cumsum(uses_expert.astype(jnp.int32)) - 1, capacity)
+    weighted_ext = jnp.concatenate([weighted, jnp.zeros((1, col_count), jnp.float32)], axis=0)
+    slot_grid = slot_of.reshape(req_count, per_dev)
+    combined = weighted_ext[at_pick.reshape(req_count, per_dev)] + jnp.where(
+        (slot_grid // per_dev == req_index)[:, :, None],
+        own_hidden[slot_grid % per_dev],
+        0.0,
     )
     layer_rows = jnp.sum(lax.all_to_all(combined, "req", 0, 0, tiled=False), axis=0)
     return layer_rows.astype(jnp.bfloat16)

time: 128 us -> 128 us (level)
  local copies, waits for them, and re-layouts: 16.3 us -> 24.6 us
  other arithmetic: 20.1 us -> 15.4 us
  waiting for transfers between devices: 30 us -> 27.5 us
    gather x0 -> x6, local copies, waits for them, and re-layouts: none -> 10.4 us  [the longest x2 3.57 us: per_device(): packed[slots_grid % per_dev]]
    scatter-add x2 -> x0, other arithmetic: 6.68 us -> none  [per_device(): combined = jnp.zeros((req_count, per_dev, col_count), jnp.float32).at[pic...]
    ppermute x3, waiting for transfers between devices: 3.59 us -> 0.39 us  [per_device(): lax.ppermute(lax.dynamic_slice_in_dim(weighted, (kv_index + shift) % kv_c...]
    select_n x0 -> x4, other arithmetic: none -> 2.22 us  [the longest x1 2.17 us: per_device(): jnp.where((slots_grid // per_dev == req_index)[:, :, None], packed[slots_...]
    reshape x0 -> x4, local copies, waits for them, and re-layouts: none -> 2.03 us  [the longest x2 1.77 us: per_device(): slots_grid = slot_order.reshape(req_count, per_dev)]
    scatter x1 -> x0, local copies, waits for them, and re-layouts: 2.01 us -> none  [per_device(): to_slots = jnp.zeros((req_count, per_dev, packed.shape[1]), packed.dtype)...]
    broadcast_in_dim x3 -> x0, local copies, waits for them, and re-layouts: 1.75 us -> none  [the longest x1 0.95 us: per_device(): jnp.zeros((req_count, per_dev, packed.shape[1]), packed.dtype)]
    add x0 -> x1, other arithmetic: none -> 1.33 us  [per_device(): weighted_ext[at_pick.reshape(req_count, per_dev)]]
  transfers between devices with their start and end apart: 8 -> 8, of which waited for: 7 -> 5; matrix products, arithmetic and copies ran while one was open for 9% -> 10% of each run, Pallas kernels for 0% -> 0%
where the time goes in v4:
time: 128 us; the launch traced here: 127 us
  starting transfers between devices  28.8 us (22%)
  waiting for transfers between devices  27.5 us (21%)
  local copies, waits for them, and re-layouts  24.6 us (19%)
  blocking collectives  20.9 us (16%)
  other arithmetic  15.4 us (12%)
  matrix products  9.25 us (7%)
    all_to_all x1, blocking collectives, per_device(): lax.all_to_all(combined, 'req', 0, 0, tiled=False)  20.9 us
    all_to_all x1, waiting for transfers between devices, per_device(): by_slot = lax.all_to_all(to_experts, 'req', 0, 0, tiled=False)  15.4 us
    all_to_all x1, starting transfers between devices, per_device(): from_homes = lax.all_to_all(to_slots, 'req', 0, 0, tiled=False)  13.1 us
    all_to_all x1, waiting for transfers between devices, per_device(): from_homes = lax.all_to_all(to_slots, 'req', 0, 0, tiled=False)  9.93 us
    all_to_all x1, starting transfers between devices, per_device(): by_slot = lax.all_to_all(to_experts, 'req', 0, 0, tiled=False)  7.14 us
    ppermute x3, starting transfers between devices, per_device(): lax.ppermute(summed_in, 'kv', [(i, (i + shift) % kv_count) for i in range...  5.06 us
    dot_general x1, matrix products, per_device(): jnp.dot(inner_act, down_proj[0], preferred_element_type=jnp.float32)  3.78 us
    gather x2, local copies, waits for them, and re-layouts, per_device(): packed[slots_grid % per_dev]  3.57 us
  transfers between devices with their start and end apart: 8, of which 5 were waited for; matrix products, arithmetic and copies ran while one was open for 10% of the time, Pallas kernels for 0%

profile of v4, /device:TPU:1, one launch (start us, length us, event | category | flops | bytes accessed | tf_op | source)
XLA Modules:
  0.0 126.9 jit_solution(8186508638720561050)
XLA Ops:
  2.7 1.6 %gather_fusion.2 = bf16[128,1536]{1,0:T(8,128)(2,1)} fusion(bf16[2,1536]{1,0:T(2,128)(2,1)S(1)} %pad_maximum_fusion.1, s32[1024]{0:T(1024)S(1)} %pad_clamp_fusion.4), kind=kCustom, calls=%fused_computation.2 | custom fusion | bytes 786944 | tf_op jit(solution)/shard_map/gather | solution.py:44
  4.4 1.9 %reshape.533 = bf16[64,2,1536]{2,1,0:T(2,128)(2,1)} reshape(bf16[128,1536]{1,0:T(8,128)(2,1)} %gather_fusion.2) | data formatting | bytes 786432 | tf_op jit(solution)/shard_map/gather | solution.py:44
  6.3 2.2 %broadcast_select_fusion.1 = bf16[64,2,1536]{2,1,0:T(2,128)(2,1)} fusion(bf16[64,2,1536]{2,1,0:T(2,128)(2,1)} %reshape.533, pred[64,2]{1,0:T(8,128)(4,1)S(1)} %fusion.28), kind=kLoop, calls=%fused_computation.27 | loop fusion | flops 196608 | bytes 786560 | tf_op jit(solution)/shard_map/jit(_where)/select_n | solution.py:42
  8.5 13.1 %all-to-all-start = ((bf16[64,2,1536]{2,1,0:T(2,128)(2,1)}), bf16[64,2,1536]{2,1,0:T(2,128)(2,1)}, u32[]{:S(2)}, u32[]{:S(2)}) async-start(bf16[64,2,1536]{2,1,0:T(2,128)(2,1)} %broadcast_select_fusion.1), calls=%async_computation | async-start | bytes 786432 | tf_op jit(solution)/shard_map/all_to_all | solution.py:47
  24.4 1.4 %scatter_custom_fusion.1 = s32[24]{0:T(128)S(1)} fusion(s32[128]{0:T(128)S(1)} %get-tuple-element.6, s32[128]{0:T(128)S(1)} %broadcast.635, s32[]{:T(128)} %constant.173.clone.1), kind=kCustom, calls=%fused_computation.154 | custom fusion | flops 128 | bytes 100 | tf_op jit(solution)/shard_map/scatter-add | solution.py:118
  26.8 9.9 %all-to-all-done = bf16[64,2,1536]{2,1,0:T(2,128)(2,1)} async-done(((bf16[64,2,1536]{2,1,0:T(2,128)(2,1)}), bf16[64,2,1536]{2,1,0:T(2,128)(2,1)}, u32[]{:S(2)}, u32[]{:S(2)}) %all-to-all-start) | async-done | bytes 393248 | tf_op jit(solution)/shard_map/all_to_all | solution.py:47
  36.8 1.6 %gather_fusion.3 = bf16[2,1536]{1,0:T(2,128)(2,1)S(1)} fusion(bf16[64,2,1536]{2,1,0:T(2,128)(2,1)} %all-to-all-done, s32[2]{0:T(128)S(1)} %fusion.64), kind=kCustom, calls=%fused_computation.3 | custom fusion | bytes 12304 | tf_op jit(solution)/shard_map/gather | solution.py:49
  38.5 2.4 %fusion.73 = (f32[2,5]{1,0:T(2,128)S(1)}, f32[2,5,4096]{2,1,0:T(8,128)S(1)}) fusion(bf16[2,5,128]{2,1,0:T(8,128)(2,1)S(1)} %reshape.510, bf16[2,4096,128]{2,1,0:T(8,128)(2,1)} %param.19, pred[2,4096]{1,0:T(4,128)(4,1)S(1)} %iota_compare_fusion), kind=kOutput, calls=%fused_computation.162 | convolution fusion | flops 10608630 | bytes 2271784 | tf_op jit(solution)/shard_map/rqd,rld->rql/dot_general | solution.py:58
  42.3 1.4 %collective-permute-start = (f32[3,2560]{1,0:T(4,128)S(1)}, f32[3,2560]{1,0:T(4,128)S(1)}, u32[]{:S(2)}, u32[]{:S(2)}) collective-permute-start(f32[3,2560]{1,0:T(4,128)S(1)} %add_dynamic-update-slice_fusion), channel_id=1, source_target_pairs={{0,1},{1,2},{2,3},{3,0},{4,5},{5,6},{6,7},{7,4},{8,9},{9,10},{10,1... | collective-permute-start | bytes 92168 | tf_op jit(solution)/shard_map/ppermute | solution.py:92
  43.6 2.6 %collective-permute-start.1 = (f32[3,2560]{1,0:T(4,128)S(1)}, f32[3,2560]{1,0:T(4,128)S(1)}, u32[]{:S(2)}, u32[]{:S(2)}) collective-permute-start(f32[3,2560]{1,0:T(4,128)S(1)} %add_dynamic-update-slice_fusion), channel_id=1, source_target_pairs={{0,2},{1,3},{2,0},{3,1},{4,6},{5,7},{6,4},{7,5},{8,10},{9,11},{10,... | collective-permute-start | bytes 92168 | tf_op jit(solution)/shard_map/ppermute | solution.py:92
  53.2 1.4 %broadcast_select_fusion = bf16[64,2,2560]{2,1,0:T(2,128)(2,1)} fusion(pred[64,2]{1,0:T(8,128)(4,1)S(1)} %copy.31, bf16[2,2560]{1,0:T(2,128)(2,1)S(1)} %fusion.37), kind=kLoop, calls=%fused_computation.20 | loop fusion | flops 327680 | bytes 665728 | tf_op jit(solution)/shard_map/jit(_where)/select_n | solution.py:110
  54.6 7.1 %all-to-all-start.1 = ((bf16[64,2,2560]{2,1,0:T(2,128)(2,1)}), bf16[64,2,2560]{2,1,0:T(2,128)(2,1)}, u32[]{:S(2)}, u32[]{:S(2)}) async-start(bf16[64,2,2560]{2,1,0:T(2,128)(2,1)} %broadcast_select_fusion), calls=%async_computation.1 | async-start | bytes 1310720 | tf_op jit(solution)/shard_map/all_to_all | solution.py:111
  66.6 15.4 %all-to-all-done.1 = bf16[64,2,2560]{2,1,0:T(2,128)(2,1)} async-done(((bf16[64,2,2560]{2,1,0:T(2,128)(2,1)}), bf16[64,2,2560]{2,1,0:T(2,128)(2,1)}, u32[]{:S(2)}, u32[]{:S(2)}) %all-to-all-start.1) | async-done | bytes 655392 | tf_op jit(solution)/shard_map/all_to_all | solution.py:111
  82.0 2.2 %gather_fusion.6 = bf16[24,2560]{1,0:T(8,128)(2,1)S(1)} fusion(bf16[64,2,2560]{2,1,0:T(2,128)(2,1)} %all-to-all-done.1, s32[24]{0:T(128)S(1)} %fusion.49), kind=kCustom, calls=%fused_computation.6 | custom fusion | bytes 245952 | tf_op jit(solution)/shard_map/gather | solution.py:121
  84.2 1.9 %fusion.4 = f32[24,384]{1,0:T(8,128)S(1)} fusion(bf16[24,2560]{1,0:T(8,128)(2,1)S(1)} %gather_fusion.6, bf16[1,2560,384]{2,1,0:T(8,128)(2,1)} %param.27), kind=kOutput, calls=%fused_computation.18 | convolution fusion | flops 47185920 | bytes 2125824 | tf_op jit(solution)/shard_map/dot_general | solution.py:122
  86.2 3.8 %convolution_multiply_fusion.1 = f32[24,2560]{1,0:T(8,128)} fusion(bf16[1,384,2560]{2,1,0:T(8,128)(2,1)} %param.29, bf16[24,2560]{1,0:T(8,128)(2,1)S(1)} %gather_fusion.6, bf16[1,2560,384]{2,1,0:T(8,128)(2,1)} %param.28, f32[24]{0:T(128)S(1)} %compare_select_fusion.12, f32[24,384]{1,0:T(8,128)S(1)} %fusion.4), kind=kOutput, calls=%fused_computation.14 | convolution fusion | flops 94488576 | bytes 4337760 | tf_op jit(solution)/shard_map/dot_general | solution.py:125
  89.9 1.6 %constant_dynamic-slice_fusion.1 = (f32[24,640]{1,0:T(8,128)}, f32[24,640]{1,0:T(8,128)}, f32[24,640]{1,0:T(8,128)}) fusion(f32[24,2560]{1,0:T(8,128)} %convolution_multiply_fusion.1, s32[]{:T(128)S(6)} %select_n.307, s32[]{:T(128)S(6)} %select_n.309, s32[]{:T(128)S(6)} %select_n.305), kind=kLoop, calls=%fused_computation.132 | loop fusion | bytes 368652 | tf_op jit(solution)/shard_map/dynamic_slice | solution.py:130
  91.5 3.5 %collective-permute-start.4 = (f32[24,640]{1,0:T(8,128)}, f32[24,640]{1,0:T(8,128)S(1)}, u32[]{:S(2)}, u32[]{:S(2)}) collective-permute-start(f32[24,640]{1,0:T(8,128)} %get-tuple-element.9), channel_id=1, source_target_pairs={{0,2},{1,3},{2,0},{3,1},{4,6},{5,7},{6,4},{7,5},{8,10},{9,11},{10,... | collective-permute-start | bytes 184328 | tf_op jit(solution)/shard_map/ppermute | solution.py:129
  95.0 1.5 %gather_fusion.9 = f32[128,640]{1,0:T(8,128)} fusion(f32[2,640]{1,0:T(2,128)S(1)} %dynamic-slice_bitcast_fusion, s32[1024]{0:T(1024)S(1)} %pad_clamp_fusion), kind=kCustom, calls=%fused_computation.9 | custom fusion | bytes 655872 | tf_op jit(solution)/shard_map/gather | solution.py:145
  96.5 1.9 %reshape.585 = f32[64,2,640]{2,1,0:T(2,128)} reshape(f32[128,640]{1,0:T(8,128)} %gather_fusion.9) | data formatting | bytes 655360 | tf_op jit(solution)/shard_map/gather | solution.py:145
  99.6 1.5 %gather_fusion.8 = f32[128,640]{1,0:T(8,128)} fusion(f32[25,640]{1,0:T(8,128)S(1)} %concatenate.30, s32[1024]{0:T(1024)S(1)} %pad_clamp_fusion.1), kind=kCustom, calls=%fused_computation.8 | custom fusion | bytes 655872 | tf_op jit(solution)/shard_map/gather | solution.py:143
  101.1 1.9 %reshape.577 = f32[64,2,640]{2,1,0:T(2,128)} reshape(f32[128,640]{1,0:T(8,128)} %gather_fusion.8) | data formatting | bytes 655360 | tf_op jit(solution)/shard_map/gather | solution.py:143
  104.4 20.9 %all_to_all.15 = f32[64,2,640]{2,1,0:T(2,128)} all-to-all(f32[64,2,640]{2,1,0:T(2,128)S(1)} %select_add_fusion), channel_id=1, replica_groups=mesh['req'=64,'kv'=4] {'req'}, dimensions={0} | all-to-all | bytes 655360 | tf_op jit(solution)/shard_map/all_to_all | solution.py:148
  125.3 1.7 %reduce_sum.53 = bf16[2,640]{1,0:T(2,128)(2,1)} reduce(f32[64,2,640]{2,1,0:T(2,128)} %all_to_all.15, f32[]{:T(128)} %constant.183.clone.1), dimensions={0}, to_apply=%region_11.12 | reduce | flops 80640 | bytes 330244 | tf_op jit(solution)/shard_map/reduce_sum | solution.py:148
  (106 shorter events, 22.0 us)
Async XLA Ops:
  0.0 41.7 %copy-start = (bf16[640,2560]{1,0:T(8,128)(2,1)S(1)}, bf16[640,2560]{1,0:T(8,128)(2,1)}, u32[]{:S(2)}) copy-start(bf16[640,2560]{1,0:T(8,128)(2,1)} %param.23) | copy-start | bytes 9830404
  4.3 17.3 %copy-start.9 = (s32[128]{0:T(128)S(1)}, s32[128]{0:T(128)}, u32[]{:S(2)}) copy-start(s32[128]{0:T(128)} %param.22) | copy-start | bytes 1540
  4.3 17.5 %copy-start.7 = (s32[128,6]{0,1:T(8,128)S(1)}, s32[128,6]{0,1:T(8,128)}, u32[]{:S(2)}) copy-start(s32[128,6]{0,1:T(8,128)} %param.25) | copy-start | bytes 9220
  4.3 17.6 %copy-start.8 = (f32[128,6]{0,1:T(8,128)S(1)}, f32[128,6]{0,1:T(8,128)}, u32[]{:S(2)}) copy-start(f32[128,6]{0,1:T(8,128)} %param.26) | copy-start | bytes 9220
  4.4 18.3 %copy-start.10 = (bf16[640]{0:T(1024)(128)(2,1)S(1)}, bf16[640]{0:T(1024)(128)(2,1)}, u32[]{:S(2)}) copy-start(bf16[640]{0:T(1024)(128)(2,1)} %param.24) | copy-start | bytes 3844
  4.4 18.4 %copy-start.1 = (s32[128]{0:T(128)S(1)}, s32[128]{0:T(128)}, u32[]{:S(2)}) copy-start(s32[128]{0:T(128)} %param.21) | copy-start | bytes 1540
  8.5 28.3 %all-to-all-start = ((bf16[64,2,1536]{2,1,0:T(2,128)(2,1)}), bf16[64,2,1536]{2,1,0:T(2,128)(2,1)}, u32[]{:S(2)}, u32[]{:S(2)}) async-start(bf16[64,2,1536]{2,1,0:T(2,128)(2,1)} %broadcast_select_fusion.1), calls=%async_computation | async-start | bytes 786432 | tf_op jit(solution)/shard_map/all_to_all | solution.py:47
  38.4 2.8 %copy-start.2 = (bf16[2,4096,128]{2,1,0:T(8,128)(2,1)S(1)}, bf16[2,4096,128]{2,1,0:T(8,128)(2,1)}, u32[]{:S(2)}) copy-start(bf16[2,4096,128]{2,1,0:T(8,128)(2,1)} %param.20) | copy-start | bytes 6291460
  42.3 5.2 %collective-permute-start = (f32[3,2560]{1,0:T(4,128)S(1)}, f32[3,2560]{1,0:T(4,128)S(1)}, u32[]{:S(2)}, u32[]{:S(2)}) collective-permute-start(f32[3,2560]{1,0:T(4,128)S(1)} %add_dynamic-update-slice_fusion), channel_id=1, source_target_pairs={{0,1},{1,2},{2,3},{3,0},{4,5},{5,6},{6,7},{7,4},{8,9},{9,10},{10,1... | collective-permute-start | bytes 92168 | tf_op jit(solution)/shard_map/ppermute | solution.py:92
  43.6 4.6 %collective-permute-start.1 = (f32[3,2560]{1,0:T(4,128)S(1)}, f32[3,2560]{1,0:T(4,128)S(1)}, u32[]{:S(2)}, u32[]{:S(2)}) collective-permute-start(f32[3,2560]{1,0:T(4,128)S(1)} %add_dynamic-update-slice_fusion), channel_id=1, source_target_pairs={{0,2},{1,3},{2,0},{3,1},{4,6},{5,7},{6,4},{7,5},{8,10},{9,11},{10,... | collective-permute-start | bytes 92168 | tf_op jit(solution)/shard_map/ppermute | solution.py:92
  46.3 3.0 %collective-permute-start.2 = (f32[3,2560]{1,0:T(4,128)S(1)}, f32[3,2560]{1,0:T(4,128)S(1)}, u32[]{:S(2)}, u32[]{:S(2)}) collective-permute-start(f32[3,2560]{1,0:T(4,128)S(1)} %add_dynamic-update-slice_fusion), channel_id=1, source_target_pairs={{0,3},{1,0},{2,1},{3,2},{4,7},{5,4},{6,5},{7,6},{8,11},{9,8},{10,9... | collective-permute-start | bytes 92168 | tf_op jit(solution)/shard_map/ppermute | solution.py:92
  48.2 1.1 copy-start.4
  49.3 0.6 copy-start.5
  52.9 31.3 %copy-start.3 = (f32[1,3,2560]{2,1,0:T(4,128)}, f32[1,3,2560]{2,1,0:T(4,128)S(1)}, u32[]{:S(2)}) copy-start(f32[1,3,2560]{2,1,0:T(4,128)S(1)} %slice_add_fusion) | copy-start | bytes 92164
  54.6 27.4 %all-to-all-start.1 = ((bf16[64,2,2560]{2,1,0:T(2,128)(2,1)}), bf16[64,2,2560]{2,1,0:T(2,128)(2,1)}, u32[]{:S(2)}, u32[]{:S(2)}) async-start(bf16[64,2,2560]{2,1,0:T(2,128)(2,1)} %broadcast_select_fusion), calls=%async_computation.1 | async-start | bytes 1310720 | tf_op jit(solution)/shard_map/all_to_all | solution.py:111
  86.2 8.8 %slice-start = ((f32[1,3,2560]{2,1,0:T(4,128)}), f32[1,2,2560]{2,1,0:T(2,128)S(1)}, s32[]{:S(2)}) async-start(f32[1,3,2560]{2,1,0:T(4,128)} %copy-done.3), calls=%async_computation.3 | async-start | bytes 40960 | tf_op jit(solution)/shard_map/slice | solution.py:99
  91.5 6.9 %collective-permute-start.3 = (f32[24,640]{1,0:T(8,128)}, f32[24,640]{1,0:T(8,128)S(1)}, u32[]{:S(2)}, u32[]{:S(2)}) collective-permute-start(f32[24,640]{1,0:T(8,128)} %get-tuple-element.11), channel_id=1, source_target_pairs={{0,1},{1,2},{2,3},{3,0},{4,5},{5,6},{6,7},{7,4},{8,9},{9,10},{10,1... | collective-permute-start | bytes 184328 | tf_op jit(solution)/shard_map/ppermute | solution.py:129
  91.5 6.9 %collective-permute-start.4 = (f32[24,640]{1,0:T(8,128)}, f32[24,640]{1,0:T(8,128)S(1)}, u32[]{:S(2)}, u32[]{:S(2)}) collective-permute-start(f32[24,640]{1,0:T(8,128)} %get-tuple-element.9), channel_id=1, source_target_pairs={{0,2},{1,3},{2,0},{3,1},{4,6},{5,7},{6,4},{7,5},{8,10},{9,11},{10,... | collective-permute-start | bytes 184328 | tf_op jit(solution)/shard_map/ppermute | solution.py:129
  95.0 3.8 %collective-permute-start.5 = (f32[24,640]{1,0:T(8,128)}, f32[24,640]{1,0:T(8,128)S(1)}, u32[]{:S(2)}, u32[]{:S(2)}) collective-permute-start(f32[24,640]{1,0:T(8,128)} %get-tuple-element.10), channel_id=1, source_target_pairs={{0,3},{1,0},{2,1},{3,2},{4,7},{5,4},{6,5},{7,6},{8,11},{9,8},{10,9... | collective-permute-start | bytes 184328 | tf_op jit(solution)/shard_map/ppermute | solution.py:129
  99.6 3.4 %copy-start.6 = (pred[64,2]{1,0:T(8,128)(4,1)S(1)}, pred[64,2]{1,0:T(8,128)(4,1)}, u32[]{:S(2)}) copy-start(pred[64,2]{1,0:T(8,128)(4,1)} %fusion.31) | copy-start | bytes 388

commit v5 on v4

--- a/solution.py
+++ b/solution.py
@@ -38,15 +38,33 @@
     slot_of = jnp.zeros((total_reqs,), jnp.int32).at[slot_order].set(
         jnp.arange(total_reqs, dtype=jnp.int32)
     )
-    slots_grid = slot_order.reshape(req_count, per_dev)
-    to_slots = jnp.where(
-        (slots_grid // per_dev == req_index)[:, :, None],
-        packed[slots_grid % per_dev],
-        jnp.zeros((), packed.dtype),
-    )
-    from_homes = lax.all_to_all(to_slots, "req", 0, 0, tiled=False)
+    pack_width = packed.shape[1]
+
+    def pick_row(rows, which):
+        chosen = rows[0][None, :]
+        for i in range(1, rows.shape[0]):
+            chosen = jnp.where((which == i)[:, None], rows[i][None, :], chosen)
+        return chosen
+
+    to_slots = jnp.concatenate(
+        [
+            jnp.where(
+                (slot_order[j::per_dev] // per_dev == req_index)[:, None],
+                pick_row(packed, slot_order[j::per_dev] % per_dev),
+                jnp.zeros((), packed.dtype),
+            )
+            for j in range(per_dev)
+        ],
+        axis=1,
+    )
+    from_homes = lax.all_to_all(to_slots, "req", 0, 0, tiled=True)
     served = lax.dynamic_slice_in_dim(slot_order, req_index * per_dev, per_dev)
-    mine = from_homes[served // per_dev, jnp.arange(per_dev)]
+    mine = jnp.stack(
+        [
+            lax.dynamic_slice(from_homes, (served[j] // per_dev, j * pack_width), (1, pack_width))[0]
+            for j in range(per_dev)
+        ]
+    )
     query_rows = mine[:, :q_width].reshape(per_dev, -1, head_dim)
     self_key_row = mine[:, q_width:q_width + head_dim]
     self_value_row = mine[:, q_width + head_dim:q_width + 2 * head_dim]
@@ -107,8 +125,14 @@
     wanted = jnp.any(
         served_ids[None, :, :] == jnp.arange(req_count, dtype=jnp.int32)[:, None, None], axis=2
     )
-    to_experts = jnp.where(wanted[:, :, None], normed[None, :, :], jnp.zeros_like(normed)[None])
-    by_slot = lax.all_to_all(to_experts, "req", 0, 0, tiled=False)
+    to_experts = jnp.concatenate(
+        [
+            jnp.where(wanted[:, j, None], normed[j][None, :], jnp.zeros((), normed.dtype))
+            for j in range(per_dev)
+        ],
+        axis=1,
+    )
+    by_slot = lax.all_to_all(to_experts, "req", 0, 0, tiled=True)
 
     capacity = min(2 * total_reqs * expert_ids.shape[1] // (local_count * req_count), total_reqs)
     expert = req_index * local_count + 0
@@ -118,7 +142,14 @@
     picked = jnp.nonzero(uses_expert, size=capacity, fill_value=0)[0].astype(jnp.int32)
     valid_rows = jnp.arange(capacity) < jnp.sum(uses_expert.astype(jnp.int32))
     picked_slots = slot_of[picked]
-    row_block = by_slot[picked_slots // per_dev, picked_slots % per_dev]
+    picked_pairs = by_slot[picked_slots // per_dev]
+    row_block = picked_pairs[:, :model_width]
+    for j in range(1, per_dev):
+        row_block = jnp.where(
+            (picked_slots % per_dev == j)[:, None],
+            picked_pairs[:, j * model_width:(j + 1) * model_width],
+            row_block,
+        )
     gate_h = jnp.dot(row_block, gate_proj[0], preferred_element_type=jnp.float32)
     up_h = jnp.dot(row_block, up_proj[0], preferred_element_type=jnp.float32)
     inner_act = (jax.nn.silu(gate_h) * up_h).astype(jnp.bfloat16)
@@ -139,13 +170,20 @@
     own_hidden = lax.dynamic_slice_in_dim(hidden, col_start, col_count, axis=1)
     at_pick = jnp.where(uses_expert, jnp.cumsum(uses_expert.astype(jnp.int32)) - 1, capacity)
     weighted_ext = jnp.concatenate([weighted, jnp.zeros((1, col_count), jnp.float32)], axis=0)
-    slot_grid = slot_of.reshape(req_count, per_dev)
-    combined = weighted_ext[at_pick.reshape(req_count, per_dev)] + jnp.where(
-        (slot_grid // per_dev == req_index)[:, :, None],
-        own_hidden[slot_grid % per_dev],
-        0.0,
-    )
-    layer_rows = jnp.sum(lax.all_to_all(combined, "req", 0, 0, tiled=False), axis=0)
+    halves = []
+    for j in range(per_dev):
+        home_slot = slot_of[j::per_dev]
+        halves.append(
+            weighted_ext[at_pick[j::per_dev]]
+            + jnp.where(
+                (home_slot // per_dev == req_index)[:, None],
+                pick_row(own_hidden, home_slot % per_dev),
+                0.0,
+            )
+        )
+    combined = jnp.concatenate(halves, axis=1)
+    totals_out = jnp.sum(lax.all_to_all(combined, "req", 0, 0, tiled=True), axis=0)
+    layer_rows = totals_out.reshape(per_dev, col_count)
     return layer_rows.astype(jnp.bfloat16)
 
 

time: 128 us -> 143 us (1.12)
  local copies, waits for them, and re-layouts: 24.6 us -> 34.7 us
  between operations: 0.45 us -> 5.52 us
  waiting for transfers between devices: 27.5 us -> 25.7 us
  other arithmetic: 15.4 us -> 17.1 us
    unnamed x23 -> x27, local copies, waits for them, and re-layouts: 0.76 us -> 18.9 us
    gather x8 -> x3, local copies, waits for them, and re-layouts: 14.2 us -> 4.23 us  [the longest x2 2.14 us: per_device(): weighted_ext[at_pick[j::per_dev]]]
    all_to_all x0 -> x5, other arithmetic: none -> 7.08 us  [the longest x2 3.75 us: per_device(): by_slot = lax.all_to_all(to_experts, 'req', 0, 0, tiled=True)]
    all_to_all x2, waiting for transfers between devices: 25.3 us -> 19.2 us  [the longest x1 14.9 us: per_device(): by_slot = lax.all_to_all(to_experts, 'req', 0, 0, tiled=True)]
    slice x1 -> x10, local copies, waits for them, and re-layouts: 0.01 us -> 3.3 us  [the longest x2 1.82 us: per_device(): slot_order[j::per_dev] // per_dev == req_index]
    select_n x5 -> x6, other arithmetic: 3.6 us -> 1.07 us  [the longest x1 0.64 us: per_device(): jnp.where(uses_expert, jnp.cumsum(uses_expert.astype(jnp.int32)) - 1, cap...]
    ppermute x3, waiting for transfers between devices: 0.39 us -> 2.78 us  [per_device(): lax.ppermute(lax.dynamic_slice_in_dim(weighted, (kv_index + shift) % kv_c...]
    reshape x4 -> x0, local copies, waits for them, and re-layouts: 2.03 us -> none  [the longest x2 1.77 us: per_device(): slots_grid = slot_order.reshape(req_count, per_dev)]
  transfers between devices with their start and end apart: 8 -> 8, of which waited for: 5 -> 7; matrix products, arithmetic and copies ran while one was open for 10% -> 8% of each run, Pallas kernels for 0% -> 0%
where the time goes in v5:
time: 143 us; the launch traced here: 141 us
  local copies, waits for them, and re-layouts  34.7 us (24%)
  starting transfers between devices  27.5 us (19%)
  waiting for transfers between devices  25.7 us (18%)
  blocking collectives  21.4 us (15%)
  other arithmetic  17.1 us (12%)
  matrix products  9.39 us (7%)
  between operations  5.52 us (4%)
    all_to_all x1, blocking collectives, per_device(): lax.all_to_all(combined, 'req', 0, 0, tiled=True)  21.4 us
    unnamed x27, local copies, waits for them, and re-layouts  18.9 us
    all_to_all x1, waiting for transfers between devices, per_device(): by_slot = lax.all_to_all(to_experts, 'req', 0, 0, tiled=True)  14.9 us
    all_to_all x1, starting transfers between devices, per_device(): from_homes = lax.all_to_all(to_slots, 'req', 0, 0, tiled=True)  13.1 us
    all_to_all x1, starting transfers between devices, per_device(): by_slot = lax.all_to_all(to_experts, 'req', 0, 0, tiled=True)  7.64 us
    all_to_all x1, waiting for transfers between devices, per_device(): from_homes = lax.all_to_all(to_slots, 'req', 0, 0, tiled=True)  4.27 us
    ppermute x3, starting transfers between devices, per_device(): lax.ppermute(summed_in, 'kv', [(i, (i + shift) % kv_count) for i in range...  3.85 us
    all_to_all x2, other arithmetic, per_device(): by_slot = lax.all_to_all(to_experts, 'req', 0, 0, tiled=True)  3.75 us
  transfers between devices with their start and end apart: 8, of which 7 were waited for; matrix products, arithmetic and copies ran while one was open for 8% of the time, Pallas kernels for 0%

profile of v5, /device:TPU:1, one launch (start us, length us, event | category | flops | bytes accessed | tf_op | source)
XLA Modules:
  0.0 141.4 jit_solution(17979004608684239231)
XLA Ops:
  6.1 2.5 %reduce.23 = bf16[64,3072]{1,0:T(8,128)(2,1)} reduce(bf16[64,1,3072]{2,0,1:T(8,128)(2,1)} %maximum_bitcast_fusion.1, bf16[]{:T(256)} %broadcast.531), dimensions={1}, to_apply=%copy.51.reduce_sub_computation | reduce | bytes 786434 | tf_op jit(solution)/shard_map/all_to_all | solution.py:60
  8.6 2.0 %reshape.394 = bf16[64,2,1536]{2,1,0:T(2,128)(2,1)} reshape(bf16[64,3072]{1,0:T(8,128)(2,1)} %reduce.23) | data formatting | bytes 786432
  10.6 13.1 %all-to-all-start = ((bf16[64,2,1536]{2,1,0:T(2,128)(2,1)}), bf16[64,2,1536]{2,1,0:T(2,128)(2,1)}, u32[]{:S(2)}, u32[]{:S(2)}) async-start(bf16[64,2,1536]{2,1,0:T(2,128)(2,1)} %reshape.394), calls=%async_computation | async-start | bytes 786432 | tf_op jit(solution)/shard_map/all_to_all | solution.py:60
  30.9 1.4 %scatter_custom_fusion.1 = s32[24]{0:T(128)S(1)} fusion(s32[128]{0:T(128)S(1)} %get-tuple-element.6, s32[128]{0:T(128)S(1)} %broadcast.410, s32[]{:T(128)} %constant.201.clone.1), kind=kCustom, calls=%fused_computation.165 | custom fusion | flops 128 | bytes 100 | tf_op jit(solution)/shard_map/scatter-add | solution.py:142
  34.6 4.3 %all-to-all-done = bf16[64,2,1536]{2,1,0:T(2,128)(2,1)} async-done(((bf16[64,2,1536]{2,1,0:T(2,128)(2,1)}), bf16[64,2,1536]{2,1,0:T(2,128)(2,1)}, u32[]{:S(2)}, u32[]{:S(2)}) %all-to-all-start) | async-done | bytes 393248 | tf_op jit(solution)/shard_map/all_to_all | solution.py:60
  38.9 3.5 %reshape.395 = bf16[64,1,3072]{2,1,0:T(2,128)(2,1)} reshape(bf16[64,2,1536]{2,1,0:T(2,128)(2,1)} %all-to-all-done) | data formatting | bytes 786432
  43.3 2.4 %fusion.65 = (f32[2,5]{1,0:T(2,128)S(1)}, f32[2,5,4096]{2,1,0:T(8,128)S(1)}) fusion(bf16[2,5,128]{2,1,0:T(8,128)(2,1)S(1)} %reshape.289, bf16[2,4096,128]{2,1,0:T(8,128)(2,1)} %param.19, pred[2,4096]{1,0:T(4,128)(4,1)S(1)} %iota_compare_fusion), kind=kOutput, calls=%fused_computation.174 | convolution fusion | flops 10608630 | bytes 2271784 | tf_op jit(solution)/shard_map/rqd,rld->rql/dot_general | solution.py:76
  47.1 2.8 %collective-permute-start.2 = (f32[3,2560]{1,0:T(4,128)S(1)}, f32[3,2560]{1,0:T(4,128)S(1)}, u32[]{:S(2)}, u32[]{:S(2)}) collective-permute-start(f32[3,2560]{1,0:T(4,128)S(1)} %add_dynamic-update-slice_fusion), channel_id=1, source_target_pairs={{0,3},{1,0},{2,1},{3,2},{4,7},{5,4},{6,5},{7,6},{8,11},{9,8},{10,9... | collective-permute-start | bytes 92168 | tf_op jit(solution)/shard_map/ppermute | solution.py:110
  51.0 3.3 %collective-permute-done.1 = f32[3,2560]{1,0:T(4,128)S(1)} collective-permute-done((f32[3,2560]{1,0:T(4,128)S(1)}, f32[3,2560]{1,0:T(4,128)S(1)}, u32[]{:S(2)}, u32[]{:S(2)}) %collective-permute-start.1) | collective-permute-done | bytes 30752 | tf_op jit(solution)/shard_map/ppermute | solution.py:110
  54.7 1.3 gather_fusion.3
  58.5 2.9 %reduce.24 = bf16[64,5120]{1,0:T(8,128)(2,1)} reduce(bf16[64,1,5120]{2,0,1:T(8,128)(2,1)} %maximum_bitcast_fusion, bf16[]{:T(256)} %broadcast.531), dimensions={1}, to_apply=%copy.52.reduce_sub_computation | reduce | bytes 1310722 | tf_op jit(solution)/shard_map/all_to_all | solution.py:135
  61.3 3.0 %reshape.396 = bf16[64,2,2560]{2,1,0:T(2,128)(2,1)} reshape(bf16[64,5120]{1,0:T(8,128)(2,1)} %reduce.24) | data formatting | bytes 1310720
  64.3 7.6 %all-to-all-start.1 = ((bf16[64,2,2560]{2,1,0:T(2,128)(2,1)}), bf16[64,2,2560]{2,1,0:T(2,128)(2,1)}, u32[]{:S(2)}, u32[]{:S(2)}) async-start(bf16[64,2,2560]{2,1,0:T(2,128)(2,1)} %reshape.396), calls=%async_computation.1 | async-start | bytes 1310720 | tf_op jit(solution)/shard_map/all_to_all | solution.py:135
  75.5 1.2 compare_select_fusion.12
  77.3 14.9 %all-to-all-done.1 = bf16[64,2,2560]{2,1,0:T(2,128)(2,1)} async-done(((bf16[64,2,2560]{2,1,0:T(2,128)(2,1)}), bf16[64,2,2560]{2,1,0:T(2,128)(2,1)}, u32[]{:S(2)}, u32[]{:S(2)}) %all-to-all-start.1) | async-done | bytes 655392 | tf_op jit(solution)/shard_map/all_to_all | solution.py:135
  92.2 5.0 %reshape.397 = bf16[64,1,5120]{2,1,0:T(2,128)(2,1)} reshape(bf16[64,2,2560]{2,1,0:T(2,128)(2,1)} %all-to-all-done.1) | data formatting | bytes 1310720
  97.2 2.4 %copy.69 = bf16[64,1,5120]{2,0,1:T(8,128)(2,1)} copy(bf16[64,1,5120]{2,1,0:T(2,128)(2,1)} %reshape.397) | data formatting | bytes 1310720
  99.6 2.1 %gather_fusion.4 = bf16[24,5120]{1,0:T(8,128)(2,1)S(1)} fusion(bf16[64,5120]{1,0:T(8,128)(2,1)} %bitcast.68, s32[1024]{0:T(1024)S(1)} %pad_clamp_fusion.2), kind=kCustom, calls=%fused_computation.4 | custom fusion | bytes 491616 | tf_op jit(solution)/shard_map/gather | solution.py:145
  102.4 2.6 %fusion.4 = f32[24,384]{1,0:T(8,128)} fusion(bf16[1,2560,384]{2,1,0:T(8,128)(2,1)} %param.27, bf16[24,5120]{1,0:T(8,128)(2,1)S(1)} %gather_fusion.4, pred[24]{0:T(512)(128)(4,1)S(1)} %fusion.44), kind=kOutput, calls=%fused_computation.16 | convolution fusion | flops 47247360 | bytes 2248728 | tf_op jit(solution)/shard_map/dot_general | solution.py:153
  105.0 3.3 %convolution_multiply_fusion.1 = f32[24,2560]{1,0:T(8,128)S(1)} fusion(bf16[1,384,2560]{2,1,0:T(8,128)(2,1)} %param.29, bf16[1,2560,384]{2,1,0:T(8,128)(2,1)} %param.28, f32[24]{0:T(128)} %compare_select_fusion.12, f32[24,384]{1,0:T(8,128)} %fusion.4, bf16[24,5120]{1,0:T(8,128)(2,1)} %copy-done.3, pred[24]{0:T(512)(128)(4,1)S(1)} %fusion.44), kind=kOutput, calls=%fused_computation.12 | convolution fusion | flops 94550016 | bytes 4460664 | tf_op jit(solution)/shard_map/dot_general | solution.py:156
  108.3 1.4 collective-permute-start.4
  112.9 1.7 %collective-permute-done.3 = f32[24,640]{1,0:T(8,128)S(1)} collective-permute-done((f32[24,640]{1,0:T(8,128)S(1)}, f32[24,640]{1,0:T(8,128)S(1)}, u32[]{:S(2)}, u32[]{:S(2)}) %collective-permute-start.3) | collective-permute-done | bytes 61472 | tf_op jit(solution)/shard_map/ppermute | solution.py:160
  115.3 1.5 %gather_fusion.6 = f32[64,640]{1,0:T(8,128)} fusion(f32[25,640]{1,0:T(8,128)S(1)} %concatenate.33, s32[1024]{0:T(1024)} %pad_clamp_fusion.1), kind=kCustom, calls=%fused_computation.6 | custom fusion | bytes 327936 | tf_op jit(solution)/shard_map/gather | solution.py:177
  118.2 21.4 %all_to_all.30 = f32[64,1,1280]{2,1,0:T(1,128)} all-to-all(f32[64,1,1280]{2,1,0:T(1,128)S(1)} %copy.57), channel_id=1, replica_groups=mesh['req'=64,'kv'=4] {'req'}, dimensions={0} | all-to-all | bytes 655360 | tf_op jit(solution)/shard_map/all_to_all | solution.py:185
  (112 shorter events, 28.3 us)
Async XLA Ops:
  0.0 46.5 %copy-start = (bf16[640,2560]{1,0:T(8,128)(2,1)S(1)}, bf16[640,2560]{1,0:T(8,128)(2,1)}, u32[]{:S(2)}) copy-start(bf16[640,2560]{1,0:T(8,128)(2,1)} %param.23) | copy-start | bytes 9830404
  0.0 23.8 %copy-start.8 = (s32[128]{0:T(128)S(1)}, s32[128]{0:T(128)}, u32[]{:S(2)}) copy-start(s32[128]{0:T(128)} %param.22) | copy-start | bytes 1540
  0.0 29.6 %copy-start.5 = (s32[128,6]{0,1:T(8,128)S(1)}, s32[128,6]{0,1:T(8,128)}, u32[]{:S(2)}) copy-start(s32[128,6]{0,1:T(8,128)} %param.25) | copy-start | bytes 9220
  0.0 29.8 %copy-start.7 = (bf16[640]{0:T(1024)(128)(2,1)S(1)}, bf16[640]{0:T(1024)(128)(2,1)}, u32[]{:S(2)}) copy-start(bf16[640]{0:T(1024)(128)(2,1)} %param.24) | copy-start | bytes 3844
  4.6 28.6 %copy-start.1 = (s32[128]{0:T(128)S(1)}, s32[128]{0:T(128)}, u32[]{:S(2)}) copy-start(s32[128]{0:T(128)} %param.21) | copy-start | bytes 1540
  10.6 28.3 %all-to-all-start = ((bf16[64,2,1536]{2,1,0:T(2,128)(2,1)}), bf16[64,2,1536]{2,1,0:T(2,128)(2,1)}, u32[]{:S(2)}, u32[]{:S(2)}) async-start(bf16[64,2,1536]{2,1,0:T(2,128)(2,1)} %reshape.394), calls=%async_computation | async-start | bytes 786432 | tf_op jit(solution)/shard_map/all_to_all | solution.py:60
  43.2 2.8 %copy-start.2 = (bf16[2,4096,128]{2,1,0:T(8,128)(2,1)S(1)}, bf16[2,4096,128]{2,1,0:T(8,128)(2,1)}, u32[]{:S(2)}) copy-start(bf16[2,4096,128]{2,1,0:T(8,128)(2,1)} %param.20) | copy-start | bytes 6291460
  47.1 3.9 %collective-permute-start.2 = (f32[3,2560]{1,0:T(4,128)S(1)}, f32[3,2560]{1,0:T(4,128)S(1)}, u32[]{:S(2)}, u32[]{:S(2)}) collective-permute-start(f32[3,2560]{1,0:T(4,128)S(1)} %add_dynamic-update-slice_fusion), channel_id=1, source_target_pairs={{0,3},{1,0},{2,1},{3,2},{4,7},{5,4},{6,5},{7,6},{8,11},{9,8},{10,9... | collective-permute-start | bytes 92168 | tf_op jit(solution)/shard_map/ppermute | solution.py:110
  49.9 4.4 %collective-permute-start.1 = (f32[3,2560]{1,0:T(4,128)S(1)}, f32[3,2560]{1,0:T(4,128)S(1)}, u32[]{:S(2)}, u32[]{:S(2)}) collective-permute-start(f32[3,2560]{1,0:T(4,128)S(1)} %add_dynamic-update-slice_fusion), channel_id=1, source_target_pairs={{0,2},{1,3},{2,0},{3,1},{4,6},{5,7},{6,4},{7,5},{8,10},{9,11},{10,... | collective-permute-start | bytes 92168 | tf_op jit(solution)/shard_map/ppermute | solution.py:110
  50.2 4.4 %collective-permute-start = (f32[3,2560]{1,0:T(4,128)S(1)}, f32[3,2560]{1,0:T(4,128)S(1)}, u32[]{:S(2)}, u32[]{:S(2)}) collective-permute-start(f32[3,2560]{1,0:T(4,128)S(1)} %add_dynamic-update-slice_fusion), channel_id=1, source_target_pairs={{0,1},{1,2},{2,3},{3,0},{4,5},{5,6},{6,7},{7,4},{8,9},{9,10},{10,1... | collective-permute-start | bytes 92168 | tf_op jit(solution)/shard_map/ppermute | solution.py:110
  56.9 0.6 copy-start.4
  58.5 13.5 %copy-start.6 = (f32[128,6]{0,1:T(8,128)S(1)}, f32[128,6]{0,1:T(8,128)}, u32[]{:S(2)}) copy-start(f32[128,6]{0,1:T(8,128)} %param.26) | copy-start | bytes 9220
  64.3 27.9 %all-to-all-start.1 = ((bf16[64,2,2560]{2,1,0:T(2,128)(2,1)}), bf16[64,2,2560]{2,1,0:T(2,128)(2,1)}, u32[]{:S(2)}, u32[]{:S(2)}) async-start(bf16[64,2,2560]{2,1,0:T(2,128)(2,1)} %reshape.396), calls=%async_computation.1 | async-start | bytes 1310720 | tf_op jit(solution)/shard_map/all_to_all | solution.py:135
  101.7 0.7 copy-start.3
  105.0 6.7 %slice-start = ((f32[1,3,2560]{2,1,0:T(4,128)}), f32[1,2,2560]{2,1,0:T(2,128)S(1)}, s32[]{:S(2)}) async-start(f32[1,3,2560]{2,1,0:T(4,128)} %copy-done.4), calls=%async_computation.3 | async-start | bytes 40960 | tf_op jit(solution)/shard_map/slice | solution.py:117
  108.3 4.7 %collective-permute-start.4 = (f32[24,640]{1,0:T(8,128)S(1)}, f32[24,640]{1,0:T(8,128)S(1)}, u32[]{:S(2)}, u32[]{:S(2)}) collective-permute-start(f32[24,640]{1,0:T(8,128)S(1)} %get-tuple-element.19), channel_id=1, source_target_pairs={{0,2},{1,3},{2,0},{3,1},{4,6},{5,7},{6,4},{7,5},{8,10},{9,11},{10,... | collective-permute-start | bytes 184328 | tf_op jit(solution)/shard_map/ppermute | solution.py:160
  109.7 3.3 %collective-permute-start.5 = (f32[24,640]{1,0:T(8,128)S(1)}, f32[24,640]{1,0:T(8,128)S(1)}, u32[]{:S(2)}, u32[]{:S(2)}) collective-permute-start(f32[24,640]{1,0:T(8,128)S(1)} %get-tuple-element.20), channel_id=1, source_target_pairs={{0,3},{1,0},{2,1},{3,2},{4,7},{5,4},{6,5},{7,6},{8,11},{9,8},{10,9... | collective-permute-start | bytes 184328 | tf_op jit(solution)/shard_map/ppermute | solution.py:160
  110.1 4.5 %collective-permute-start.3 = (f32[24,640]{1,0:T(8,128)S(1)}, f32[24,640]{1,0:T(8,128)S(1)}, u32[]{:S(2)}, u32[]{:S(2)}) collective-permute-start(f32[24,640]{1,0:T(8,128)S(1)} %get-tuple-element.21), channel_id=1, source_target_pairs={{0,1},{1,2},{2,3},{3,0},{4,5},{5,6},{6,7},{7,4},{8,9},{9,10},{10,1... | collective-permute-start | bytes 184328 | tf_op jit(solution)/shard_map/ppermute | solution.py:160

commit v6 on v4

--- a/solution.py
+++ b/solution.py
@@ -39,10 +39,12 @@
         jnp.arange(total_reqs, dtype=jnp.int32)
     )
     slots_grid = slot_order.reshape(req_count, per_dev)
+    from_grid = slots_grid % per_dev
+    to_slots = jnp.broadcast_to(packed[0], (req_count, per_dev, packed.shape[1]))
+    for i in range(1, per_dev):
+        to_slots = jnp.where((from_grid == i)[:, :, None], packed[i][None, None, :], to_slots)
     to_slots = jnp.where(
-        (slots_grid // per_dev == req_index)[:, :, None],
-        packed[slots_grid % per_dev],
-        jnp.zeros((), packed.dtype),
+        (slots_grid // per_dev == req_index)[:, :, None], to_slots, jnp.zeros((), packed.dtype)
     )
     from_homes = lax.all_to_all(to_slots, "req", 0, 0, tiled=False)
     served = lax.dynamic_slice_in_dim(slot_order, req_index * per_dev, per_dev)
@@ -139,13 +141,19 @@
     own_hidden = lax.dynamic_slice_in_dim(hidden, col_start, col_count, axis=1)
     at_pick = jnp.where(uses_expert, jnp.cumsum(uses_expert.astype(jnp.int32)) - 1, capacity)
     weighted_ext = jnp.concatenate([weighted, jnp.zeros((1, col_count), jnp.float32)], axis=0)
-    slot_grid = slot_of.reshape(req_count, per_dev)
-    combined = weighted_ext[at_pick.reshape(req_count, per_dev)] + jnp.where(
-        (slot_grid // per_dev == req_index)[:, :, None],
-        own_hidden[slot_grid % per_dev],
-        0.0,
-    )
-    layer_rows = jnp.sum(lax.all_to_all(combined, "req", 0, 0, tiled=False), axis=0)
+    halves = []
+    for j in range(per_dev):
+        home_slot = slot_of[j::per_dev]
+        own_row = own_hidden[0][None, :]
+        for i in range(1, per_dev):
+            own_row = jnp.where((home_slot % per_dev == i)[:, None], own_hidden[i][None, :], own_row)
+        halves.append(
+            weighted_ext[at_pick[j::per_dev]]
+            + jnp.where((home_slot // per_dev == req_index)[:, None], own_row, 0.0)
+        )
+    combined = jnp.concatenate(halves, axis=1)
+    totals_out = jnp.sum(lax.all_to_all(combined, "req", 0, 0, tiled=True), axis=0)
+    layer_rows = totals_out.reshape(per_dev, col_count)
     return layer_rows.astype(jnp.bfloat16)
 
 

time: 128 us -> 123 us (0.961)
  local copies, waits for them, and re-layouts: 24.6 us -> 19.8 us
  waiting for transfers between devices: 27.5 us -> 29.7 us
  starting transfers between devices: 28.8 us -> 26.9 us
    gather x6 -> x2, local copies, waits for them, and re-layouts: 10.4 us -> 2.02 us  [per_device(): weighted_ext[at_pick[j::per_dev]]]
    all_to_all x1, waiting for transfers between devices: 9.93 us -> 6.61 us  [per_device(): from_homes = lax.all_to_all(to_slots, 'req', 0, 0, tiled=False)]
    unnamed x23 -> x16, local copies, waits for them, and re-layouts: 0.76 us -> 3.76 us
    ppermute x3, waiting for transfers between devices: 0.39 us -> 3.16 us  [per_device(): lax.ppermute(lax.dynamic_slice_in_dim(weighted, (kv_index + shift) % kv_c...]
    ppermute x3, waiting for transfers between devices: 1.84 us -> 3.63 us  [per_device(): lax.ppermute(summed_in, 'kv', [(i, (i + shift) % kv_count) for i in range...]
  transfers between devices with their start and end apart: 8 -> 8, of which waited for: 5 -> 6; matrix products, arithmetic and copies ran while one was open for 10% -> 10% of each run, Pallas kernels for 0% -> 0%
where the time goes in v6:
time: 123 us; the launch traced here: 122 us
  waiting for transfers between devices  29.7 us (24%)
  starting transfers between devices  26.9 us (22%)
  blocking collectives  21.6 us (18%)
  local copies, waits for them, and re-layouts  19.8 us (16%)
  other arithmetic  14.3 us (12%)
  matrix products  9.22 us (7%)
    all_to_all x1, blocking collectives, per_device(): lax.all_to_all(combined, 'req', 0, 0, tiled=True)  21.6 us
    all_to_all x1, waiting for transfers between devices, per_device(): by_slot = lax.all_to_all(to_experts, 'req', 0, 0, tiled=False)  16.3 us
    all_to_all x1, starting transfers between devices, per_device(): from_homes = lax.all_to_all(to_slots, 'req', 0, 0, tiled=False)  13.1 us
    all_to_all x1, starting transfers between devices, per_device(): by_slot = lax.all_to_all(to_experts, 'req', 0, 0, tiled=False)  7.04 us
    all_to_all x1, waiting for transfers between devices, per_device(): from_homes = lax.all_to_all(to_slots, 'req', 0, 0, tiled=False)  6.61 us
    ppermute x3, starting transfers between devices, per_device(): lax.ppermute(summed_in, 'kv', [(i, (i + shift) % kv_count) for i in range...  3.85 us
    unnamed x16, local copies, waits for them, and re-layouts  3.76 us
    dot_general x1, matrix products, per_device(): jnp.dot(inner_act, down_proj[0], preferred_element_type=jnp.float32)  3.75 us
  transfers between devices with their start and end apart: 8, of which 6 were waited for; matrix products, arithmetic and copies ran while one was open for 10% of the time, Pallas kernels for 0%

profile of v6, /device:TPU:1, one launch (start us, length us, event | category | flops | bytes accessed | tf_op | source)
XLA Modules:
  0.0 121.8 jit_solution(8435308632594375034)
XLA Ops:
  3.9 1.2 broadcast_select_fusion.2
  5.1 13.1 %all-to-all-start = ((bf16[64,2,1536]{2,1,0:T(2,128)(2,1)}), bf16[64,2,1536]{2,1,0:T(2,128)(2,1)}, u32[]{:S(2)}, u32[]{:S(2)}) async-start(bf16[64,2,1536]{2,1,0:T(2,128)(2,1)} %broadcast_select_fusion.2), calls=%async_computation | async-start | bytes 786432 | tf_op jit(solution)/shard_map/all_to_all | solution.py:49
  23.1 1.4 %scatter_custom_fusion.1 = s32[24]{0:T(128)S(1)} fusion(s32[128]{0:T(128)S(1)} %get-tuple-element.6, s32[128]{0:T(128)S(1)} %broadcast.523, s32[]{:T(128)} %constant.191.clone.1), kind=kCustom, calls=%fused_computation.161 | custom fusion | flops 128 | bytes 100 | tf_op jit(solution)/shard_map/scatter-add | solution.py:120
  26.8 6.6 %all-to-all-done = bf16[64,2,1536]{2,1,0:T(2,128)(2,1)} async-done(((bf16[64,2,1536]{2,1,0:T(2,128)(2,1)}), bf16[64,2,1536]{2,1,0:T(2,128)(2,1)}, u32[]{:S(2)}, u32[]{:S(2)}) %all-to-all-start) | async-done | bytes 393248 | tf_op jit(solution)/shard_map/all_to_all | solution.py:49
  33.4 1.6 %gather_fusion.2 = bf16[2,1536]{1,0:T(2,128)(2,1)S(1)} fusion(bf16[64,2,1536]{2,1,0:T(2,128)(2,1)} %all-to-all-done, s32[2]{0:T(128)S(1)} %fusion.62), kind=kCustom, calls=%fused_computation.2 | custom fusion | bytes 12304 | tf_op jit(solution)/shard_map/gather | solution.py:51
  35.2 2.4 %fusion.73 = (f32[2,5]{1,0:T(2,128)S(1)}, f32[2,5,4096]{2,1,0:T(8,128)S(1)}) fusion(bf16[2,5,128]{2,1,0:T(8,128)(2,1)S(1)} %reshape.354, bf16[2,4096,128]{2,1,0:T(8,128)(2,1)} %param.19, pred[2,4096]{1,0:T(4,128)(4,1)S(1)} %iota_compare_fusion), kind=kOutput, calls=%fused_computation.169 | convolution fusion | flops 10608630 | bytes 2271784 | tf_op jit(solution)/shard_map/rqd,rld->rql/dot_general | solution.py:60
  38.9 2.8 %collective-permute-start.2 = (f32[3,2560]{1,0:T(4,128)S(1)}, f32[3,2560]{1,0:T(4,128)S(1)}, u32[]{:S(2)}, u32[]{:S(2)}) collective-permute-start(f32[3,2560]{1,0:T(4,128)S(1)} %add_dynamic-update-slice_fusion), channel_id=1, source_target_pairs={{0,3},{1,0},{2,1},{3,2},{4,7},{5,4},{6,5},{7,6},{8,11},{9,8},{10,9... | collective-permute-start | bytes 92168 | tf_op jit(solution)/shard_map/ppermute | solution.py:94
  42.9 3.2 %collective-permute-done.1 = f32[3,2560]{1,0:T(4,128)S(1)} collective-permute-done((f32[3,2560]{1,0:T(4,128)S(1)}, f32[3,2560]{1,0:T(4,128)S(1)}, u32[]{:S(2)}, u32[]{:S(2)}) %collective-permute-start.1) | collective-permute-done | bytes 30752 | tf_op jit(solution)/shard_map/ppermute | solution.py:94
  48.0 1.3 %gather_fusion.3 = f32[4,3,2560]{2,1,0:T(4,128)} fusion(f32[4,3,2560]{2,1,0:T(4,128)S(1)} %pad_maximum_fusion, s32[1024]{0:T(1024)S(1)} %pad_clamp_fusion.3), kind=kCustom, calls=%fused_computation.3 | custom fusion | bytes 245776 | tf_op jit(solution)/shard_map/gather | solution.py:97
  50.4 1.4 %broadcast_select_fusion = bf16[64,2,2560]{2,1,0:T(2,128)(2,1)} fusion(pred[64,2]{1,0:T(8,128)(4,1)S(1)} %copy.39, bf16[2,2560]{1,0:T(2,128)(2,1)S(1)} %fusion.33), kind=kLoop, calls=%fused_computation.19 | loop fusion | flops 327680 | bytes 665728 | tf_op jit(solution)/shard_map/jit(_where)/select_n | solution.py:112
  51.8 7.0 %all-to-all-start.1 = ((bf16[64,2,2560]{2,1,0:T(2,128)(2,1)}), bf16[64,2,2560]{2,1,0:T(2,128)(2,1)}, u32[]{:S(2)}, u32[]{:S(2)}) async-start(bf16[64,2,2560]{2,1,0:T(2,128)(2,1)} %broadcast_select_fusion), calls=%async_computation.1 | async-start | bytes 1310720 | tf_op jit(solution)/shard_map/all_to_all | solution.py:113
  58.9 1.0 scatter_custom_fusion
  62.8 16.3 %all-to-all-done.1 = bf16[64,2,2560]{2,1,0:T(2,128)(2,1)} async-done(((bf16[64,2,2560]{2,1,0:T(2,128)(2,1)}), bf16[64,2,2560]{2,1,0:T(2,128)(2,1)}, u32[]{:S(2)}, u32[]{:S(2)}) %all-to-all-start.1) | async-done | bytes 655392 | tf_op jit(solution)/shard_map/all_to_all | solution.py:113
  79.1 2.3 %gather_fusion.5 = bf16[24,2560]{1,0:T(8,128)(2,1)S(1)} fusion(bf16[64,2,2560]{2,1,0:T(2,128)(2,1)} %all-to-all-done.1, s32[24]{0:T(128)S(1)} %fusion.45), kind=kCustom, calls=%fused_computation.5 | custom fusion | bytes 245952 | tf_op jit(solution)/shard_map/gather | solution.py:123
  81.4 1.9 %fusion.4 = f32[24,384]{1,0:T(8,128)S(1)} fusion(bf16[24,2560]{1,0:T(8,128)(2,1)S(1)} %gather_fusion.5, bf16[1,2560,384]{2,1,0:T(8,128)(2,1)} %param.27), kind=kOutput, calls=%fused_computation.17 | convolution fusion | flops 47185920 | bytes 2125824 | tf_op jit(solution)/shard_map/dot_general | solution.py:124
  83.3 3.8 %convolution_multiply_fusion.1 = f32[24,2560]{1,0:T(8,128)} fusion(bf16[1,384,2560]{2,1,0:T(8,128)(2,1)} %param.29, bf16[24,2560]{1,0:T(8,128)(2,1)S(1)} %gather_fusion.5, bf16[1,2560,384]{2,1,0:T(8,128)(2,1)} %param.28, f32[24]{0:T(128)S(1)} %compare_select_fusion.11, f32[24,384]{1,0:T(8,128)S(1)} %fusion.4), kind=kOutput, calls=%fused_computation.13 | convolution fusion | flops 94488576 | bytes 4337760 | tf_op jit(solution)/shard_map/dot_general | solution.py:127
  88.0 1.4 %collective-permute-start.4 = (f32[24,640]{1,0:T(8,128)S(1)}, f32[24,640]{1,0:T(8,128)S(1)}, u32[]{:S(2)}, u32[]{:S(2)}) collective-permute-start(f32[24,640]{1,0:T(8,128)S(1)} %get-tuple-element.13), channel_id=1, source_target_pairs={{0,2},{1,3},{2,0},{3,1},{4,6},{5,7},{6,4},{7,5},{8,10},{9,11},{10,... | collective-permute-start | bytes 184328 | tf_op jit(solution)/shard_map/ppermute | solution.py:131
  89.8 1.0 collective-permute-start.3
  91.0 2.0 %collective-permute-done.4 = f32[24,640]{1,0:T(8,128)S(1)} collective-permute-done((f32[24,640]{1,0:T(8,128)S(1)}, f32[24,640]{1,0:T(8,128)S(1)}, u32[]{:S(2)}, u32[]{:S(2)}) %collective-permute-start.4) | collective-permute-done | bytes 61472 | tf_op jit(solution)/shard_map/ppermute | solution.py:131
  93.0 1.2 collective-permute-done.3
  95.7 1.3 %gather_fusion.7 = f32[64,640]{1,0:T(8,128)} fusion(f32[25,640]{1,0:T(8,128)S(1)} %concatenate.33, s32[1024]{0:T(1024)S(1)} %pad_clamp_fusion.1), kind=kCustom, calls=%fused_computation.7 | custom fusion | bytes 327936 | tf_op jit(solution)/shard_map/gather | solution.py:151
  97.0 1.0 select_add_fusion.1
  98.4 21.6 %all_to_all.19 = f32[64,1,1280]{2,1,0:T(1,128)} all-to-all(f32[64,1,1280]{2,1,0:T(1,128)S(1)} %copy.46), channel_id=1, replica_groups=mesh['req'=64,'kv'=4] {'req'}, dimensions={0} | all-to-all | bytes 655360 | tf_op jit(solution)/shard_map/all_to_all | solution.py:155
  120.0 1.2 reduce_sum.53
  (90 shorter events, 23.4 us)
Async XLA Ops:
  0.0 38.3 %copy-start = (bf16[640,2560]{1,0:T(8,128)(2,1)S(1)}, bf16[640,2560]{1,0:T(8,128)(2,1)}, u32[]{:S(2)}) copy-start(bf16[640,2560]{1,0:T(8,128)(2,1)} %param.23) | copy-start | bytes 9830404
  0.0 25.4 %copy-start.1 = (s32[128]{0:T(128)S(1)}, s32[128]{0:T(128)}, u32[]{:S(2)}) copy-start(s32[128]{0:T(128)} %param.21) | copy-start | bytes 1540
  5.1 28.3 %all-to-all-start = ((bf16[64,2,1536]{2,1,0:T(2,128)(2,1)}), bf16[64,2,1536]{2,1,0:T(2,128)(2,1)}, u32[]{:S(2)}, u32[]{:S(2)}) async-start(bf16[64,2,1536]{2,1,0:T(2,128)(2,1)} %broadcast_select_fusion.2), calls=%async_computation | async-start | bytes 786432 | tf_op jit(solution)/shard_map/all_to_all | solution.py:49
  35.0 2.8 %copy-start.2 = (bf16[2,4096,128]{2,1,0:T(8,128)(2,1)S(1)}, bf16[2,4096,128]{2,1,0:T(8,128)(2,1)}, u32[]{:S(2)}) copy-start(bf16[2,4096,128]{2,1,0:T(8,128)(2,1)} %param.20) | copy-start | bytes 6291460
  38.8 20.0 %copy-start.5 = (s32[128]{0:T(128)S(1)}, s32[128]{0:T(128)}, u32[]{:S(2)}) copy-start(s32[128]{0:T(128)} %param.22) | copy-start | bytes 1540
  38.9 4.0 %collective-permute-start.2 = (f32[3,2560]{1,0:T(4,128)S(1)}, f32[3,2560]{1,0:T(4,128)S(1)}, u32[]{:S(2)}, u32[]{:S(2)}) collective-permute-start(f32[3,2560]{1,0:T(4,128)S(1)} %add_dynamic-update-slice_fusion), channel_id=1, source_target_pairs={{0,3},{1,0},{2,1},{3,2},{4,7},{5,4},{6,5},{7,6},{8,11},{9,8},{10,9... | collective-permute-start | bytes 92168 | tf_op jit(solution)/shard_map/ppermute | solution.py:94
  41.7 4.4 %collective-permute-start.1 = (f32[3,2560]{1,0:T(4,128)S(1)}, f32[3,2560]{1,0:T(4,128)S(1)}, u32[]{:S(2)}, u32[]{:S(2)}) collective-permute-start(f32[3,2560]{1,0:T(4,128)S(1)} %add_dynamic-update-slice_fusion), channel_id=1, source_target_pairs={{0,2},{1,3},{2,0},{3,1},{4,6},{5,7},{6,4},{7,5},{8,10},{9,11},{10,... | collective-permute-start | bytes 92168 | tf_op jit(solution)/shard_map/ppermute | solution.py:94
  42.1 4.4 %collective-permute-start = (f32[3,2560]{1,0:T(4,128)S(1)}, f32[3,2560]{1,0:T(4,128)S(1)}, u32[]{:S(2)}, u32[]{:S(2)}) collective-permute-start(f32[3,2560]{1,0:T(4,128)S(1)} %add_dynamic-update-slice_fusion), channel_id=1, source_target_pairs={{0,1},{1,2},{2,3},{3,0},{4,5},{5,6},{6,7},{7,4},{8,9},{9,10},{10,1... | collective-permute-start | bytes 92168 | tf_op jit(solution)/shard_map/ppermute | solution.py:94
  46.1 0.6 copy-start.3
  46.5 0.6 copy-start.4
  51.8 27.3 %all-to-all-start.1 = ((bf16[64,2,2560]{2,1,0:T(2,128)(2,1)}), bf16[64,2,2560]{2,1,0:T(2,128)(2,1)}, u32[]{:S(2)}, u32[]{:S(2)}) async-start(bf16[64,2,2560]{2,1,0:T(2,128)(2,1)} %broadcast_select_fusion), calls=%async_computation.1 | async-start | bytes 1310720 | tf_op jit(solution)/shard_map/all_to_all | solution.py:113
  88.0 5.0 %collective-permute-start.4 = (f32[24,640]{1,0:T(8,128)S(1)}, f32[24,640]{1,0:T(8,128)S(1)}, u32[]{:S(2)}, u32[]{:S(2)}) collective-permute-start(f32[24,640]{1,0:T(8,128)S(1)} %get-tuple-element.13), channel_id=1, source_target_pairs={{0,2},{1,3},{2,0},{3,1},{4,6},{5,7},{6,4},{7,5},{8,10},{9,11},{10,... | collective-permute-start | bytes 184328 | tf_op jit(solution)/shard_map/ppermute | solution.py:131
  89.4 3.6 %collective-permute-start.5 = (f32[24,640]{1,0:T(8,128)S(1)}, f32[24,640]{1,0:T(8,128)S(1)}, u32[]{:S(2)}, u32[]{:S(2)}) collective-permute-start(f32[24,640]{1,0:T(8,128)S(1)} %get-tuple-element.14), channel_id=1, source_target_pairs={{0,3},{1,0},{2,1},{3,2},{4,7},{5,4},{6,5},{7,6},{8,11},{9,8},{10,9... | collective-permute-start | bytes 184328 | tf_op jit(solution)/shard_map/ppermute | solution.py:131
  89.8 4.3 %collective-permute-start.3 = (f32[24,640]{1,0:T(8,128)S(1)}, f32[24,640]{1,0:T(8,128)S(1)}, u32[]{:S(2)}, u32[]{:S(2)}) collective-permute-start(f32[24,640]{1,0:T(8,128)S(1)} %get-tuple-element.15), channel_id=1, source_target_pairs={{0,1},{1,2},{2,3},{3,0},{4,5},{5,6},{6,7},{7,4},{8,9},{9,10},{10,1... | collective-permute-start | bytes 184328 | tf_op jit(solution)/shard_map/ppermute | solution.py:131

commit v7 on v6

--- a/solution.py
+++ b/solution.py
@@ -34,18 +34,21 @@
     model_width = out_proj.shape[1]
     q_width = queries.shape[1]
 
-    packed = jnp.concatenate([queries, fresh_token_keys, fresh_token_values, residual_in], axis=1)
+    pieces = (queries, fresh_token_keys, fresh_token_values, residual_in)
     slot_of = jnp.zeros((total_reqs,), jnp.int32).at[slot_order].set(
         jnp.arange(total_reqs, dtype=jnp.int32)
     )
     slots_grid = slot_order.reshape(req_count, per_dev)
     from_grid = slots_grid % per_dev
-    to_slots = jnp.broadcast_to(packed[0], (req_count, per_dev, packed.shape[1]))
-    for i in range(1, per_dev):
-        to_slots = jnp.where((from_grid == i)[:, :, None], packed[i][None, None, :], to_slots)
-    to_slots = jnp.where(
-        (slots_grid // per_dev == req_index)[:, :, None], to_slots, jnp.zeros((), packed.dtype)
-    )
+    sent_here = (slots_grid // per_dev == req_index)[:, :, None]
+
+    def to_slot_rows(piece):
+        rows = jnp.broadcast_to(piece[0], (req_count, per_dev, piece.shape[1]))
+        for i in range(1, per_dev):
+            rows = jnp.where((from_grid == i)[:, :, None], piece[i][None, None, :], rows)
+        return jnp.where(sent_here, rows, jnp.zeros((), piece.dtype))
+
+    to_slots = jnp.concatenate([to_slot_rows(piece) for piece in pieces], axis=2)
     from_homes = lax.all_to_all(to_slots, "req", 0, 0, tiled=False)
     served = lax.dynamic_slice_in_dim(slot_order, req_index * per_dev, per_dev)
     mine = from_homes[served // per_dev, jnp.arange(per_dev)]
@@ -94,10 +97,9 @@
         lax.ppermute(summed_in, "kv", [(i, (i + shift) % kv_count) for i in range(kv_count)])
         for shift in range(1, kv_count)
     ]
-    stacked = jnp.stack(parts)[(kv_index - jnp.arange(kv_count)) % kv_count]
-    summed = stacked[0]
-    for source in range(1, kv_count):
-        summed = summed + stacked[source]
+    summed = parts[0]
+    for part in parts[1:]:
+        summed = summed + part
     hidden = summed[:per_dev]
     gain = summed[per_dev]
     squares = jnp.sum(hidden * hidden, axis=1)

time: 123 us -> 118 us (0.959)
  local copies, waits for them, and re-layouts: 19.8 us -> 15 us
  waiting for transfers between devices: 29.7 us -> 33.1 us
  other arithmetic: 14.3 us -> 11.2 us
    all_to_all x1, waiting for transfers between devices: 6.61 us -> 13 us  [per_device(): from_homes = lax.all_to_all(to_slots, 'req', 0, 0, tiled=False)]
    unnamed x16 -> x15, local copies, waits for them, and re-layouts: 3.76 us -> 0.14 us
    all_to_all x1, waiting for transfers between devices: 16.3 us -> 14.7 us  [per_device(): by_slot = lax.all_to_all(to_experts, 'req', 0, 0, tiled=False)]
    ppermute x3, waiting for transfers between devices: 3.63 us -> 2.2 us  [per_device(): lax.ppermute(summed_in, 'kv', [(i, (i + shift) % kv_count) for i in range...]
    gather x1 -> x0, local copies, waits for them, and re-layouts: 1.29 us -> none  [per_device(): stacked = jnp.stack(parts)[(kv_index - jnp.arange(kv_count)) % kv_count]]
  transfers between devices with their start and end apart: 8 -> 8, of which waited for: 6 -> 6; matrix products, arithmetic and copies ran while one was open for 10% -> 8% of each run, Pallas kernels for 0% -> 0%
where the time goes in v7:
time: 118 us; the launch traced here: 117 us
  waiting for transfers between devices  33.1 us (28%)
  starting transfers between devices  26.9 us (23%)
  blocking collectives  21.4 us (18%)
  local copies, waits for them, and re-layouts  15 us (13%)
  other arithmetic  11.2 us (9%)
  matrix products  9.22 us (8%)
    all_to_all x1, blocking collectives, per_device(): lax.all_to_all(combined, 'req', 0, 0, tiled=True)  21.4 us
    all_to_all x1, waiting for transfers between devices, per_device(): by_slot = lax.all_to_all(to_experts, 'req', 0, 0, tiled=False)  14.7 us
    all_to_all x1, starting transfers between devices, per_device(): from_homes = lax.all_to_all(to_slots, 'req', 0, 0, tiled=False)  13.1 us
    all_to_all x1, waiting for transfers between devices, per_device(): from_homes = lax.all_to_all(to_slots, 'req', 0, 0, tiled=False)  13 us
    all_to_all x1, starting transfers between devices, per_device(): by_slot = lax.all_to_all(to_experts, 'req', 0, 0, tiled=False)  7.04 us
    ppermute x3, starting transfers between devices, per_device(): lax.ppermute(summed_in, 'kv', [(i, (i + shift) % kv_count) for i in range...  3.85 us
    dot_general x1, matrix products, per_device(): jnp.dot(inner_act, down_proj[0], preferred_element_type=jnp.float32)  3.75 us
    ppermute x3, waiting for transfers between devices, per_device(): lax.ppermute(lax.dynamic_slice_in_dim(weighted, (kv_index + shift) % kv_c...  3.25 us
  transfers between devices with their start and end apart: 8, of which 6 were waited for; matrix products, arithmetic and copies ran while one was open for 8% of the time, Pallas kernels for 0%

profile of v7, /device:TPU:1, one launch (start us, length us, event | category | flops | bytes accessed | tf_op | source)
XLA Modules:
  0.0 117.2 jit_solution(15009037549797551850)
XLA Ops:
  0.0 0.9 reshape.296
  3.4 1.1 pad_maximum_fusion
  4.5 13.1 %all-to-all-start = ((bf16[64,2,1536]{2,1,0:T(2,128)(2,1)}), bf16[64,2,1536]{2,1,0:T(2,128)(2,1)}, u32[]{:S(2)}, u32[]{:S(2)}) async-start(bf16[64,2,1536]{2,1,0:T(2,128)(2,1)} %pad_maximum_fusion), calls=%async_computation | async-start | bytes 786432 | tf_op jit(solution)/shard_map/all_to_all | solution.py:52
  19.7 13.0 %all-to-all-done = bf16[64,2,1536]{2,1,0:T(2,128)(2,1)} async-done(((bf16[64,2,1536]{2,1,0:T(2,128)(2,1)}), bf16[64,2,1536]{2,1,0:T(2,128)(2,1)}, u32[]{:S(2)}, u32[]{:S(2)}) %all-to-all-start) | async-done | bytes 393248 | tf_op jit(solution)/shard_map/all_to_all | solution.py:52
  32.7 1.6 %gather_fusion.2 = bf16[2,1536]{1,0:T(2,128)(2,1)S(1)} fusion(bf16[64,2,1536]{2,1,0:T(2,128)(2,1)} %all-to-all-done, s32[2]{0:T(128)S(1)} %fusion.57), kind=kCustom, calls=%fused_computation.2 | custom fusion | bytes 12304 | tf_op jit(solution)/shard_map/gather | solution.py:54
  34.5 2.4 %fusion.69 = (f32[2,5]{1,0:T(2,128)S(1)}, f32[2,5,4096]{2,1,0:T(8,128)S(1)}) fusion(bf16[2,5,128]{2,1,0:T(8,128)(2,1)S(1)} %reshape.297, bf16[2,4096,128]{2,1,0:T(8,128)(2,1)} %param.19, pred[2,4096]{1,0:T(4,128)(4,1)S(1)} %iota_compare_fusion), kind=kOutput, calls=%fused_computation.165 | convolution fusion | flops 10608630 | bytes 2271784 | tf_op jit(solution)/shard_map/rqd,rld->rql/dot_general | solution.py:63
  38.2 2.8 %collective-permute-start.2 = (f32[3,2560]{1,0:T(4,128)S(1)}, f32[3,2560]{1,0:T(4,128)S(1)}, u32[]{:S(2)}, u32[]{:S(2)}) collective-permute-start(f32[3,2560]{1,0:T(4,128)S(1)} %add_dynamic-update-slice_fusion), channel_id=1, source_target_pairs={{0,3},{1,0},{2,1},{3,2},{4,7},{5,4},{6,5},{7,6},{8,11},{9,8},{10,9... | collective-permute-start | bytes 92168 | tf_op jit(solution)/shard_map/ppermute | solution.py:97
  42.2 1.0 scatter_custom_fusion
  43.7 1.8 %collective-permute-done.1 = f32[3,2560]{1,0:T(4,128)S(1)} collective-permute-done((f32[3,2560]{1,0:T(4,128)S(1)}, f32[3,2560]{1,0:T(4,128)S(1)}, u32[]{:S(2)}, u32[]{:S(2)}) %collective-permute-start.1) | collective-permute-done | bytes 30752 | tf_op jit(solution)/shard_map/ppermute | solution.py:97
  46.2 1.4 %broadcast_select_fusion = bf16[64,2,2560]{2,1,0:T(2,128)(2,1)} fusion(pred[64,2]{1,0:T(8,128)(4,1)S(1)} %copy.39, bf16[2,2560]{1,0:T(2,128)(2,1)S(1)} %multiply_convert_fusion), kind=kLoop, calls=%fused_computation.18 | loop fusion | flops 327680 | bytes 665728 | tf_op jit(solution)/shard_map/jit(_where)/select_n | solution.py:114
  47.5 7.0 %all-to-all-start.1 = ((bf16[64,2,2560]{2,1,0:T(2,128)(2,1)}), bf16[64,2,2560]{2,1,0:T(2,128)(2,1)}, u32[]{:S(2)}, u32[]{:S(2)}) async-start(bf16[64,2,2560]{2,1,0:T(2,128)(2,1)} %broadcast_select_fusion), calls=%async_computation.1 | async-start | bytes 1310720 | tf_op jit(solution)/shard_map/all_to_all | solution.py:115
  55.5 1.4 %scatter_custom_fusion.1 = s32[24]{0:T(128)S(1)} fusion(s32[128]{0:T(128)S(1)} %get-tuple-element.6, s32[128]{0:T(128)S(1)} %broadcast.460, s32[]{:T(128)} %constant.180.clone.1), kind=kCustom, calls=%fused_computation.156 | custom fusion | flops 128 | bytes 100 | tf_op jit(solution)/shard_map/scatter-add | solution.py:122
  60.2 14.7 %all-to-all-done.1 = bf16[64,2,2560]{2,1,0:T(2,128)(2,1)} async-done(((bf16[64,2,2560]{2,1,0:T(2,128)(2,1)}), bf16[64,2,2560]{2,1,0:T(2,128)(2,1)}, u32[]{:S(2)}, u32[]{:S(2)}) %all-to-all-start.1) | async-done | bytes 655392 | tf_op jit(solution)/shard_map/all_to_all | solution.py:115
  74.9 2.1 %gather_fusion.4 = bf16[24,2560]{1,0:T(8,128)(2,1)S(1)} fusion(bf16[64,2,2560]{2,1,0:T(2,128)(2,1)} %all-to-all-done.1, s32[24]{0:T(128)S(1)} %fusion.42), kind=kCustom, calls=%fused_computation.4 | custom fusion | bytes 245952 | tf_op jit(solution)/shard_map/gather | solution.py:125
  77.0 1.9 %fusion.4 = f32[24,384]{1,0:T(8,128)S(1)} fusion(bf16[24,2560]{1,0:T(8,128)(2,1)S(1)} %gather_fusion.4, bf16[1,2560,384]{2,1,0:T(8,128)(2,1)} %param.27), kind=kOutput, calls=%fused_computation.16 | convolution fusion | flops 47185920 | bytes 2125824 | tf_op jit(solution)/shard_map/dot_general | solution.py:126
  78.9 3.8 %convolution_multiply_fusion.1 = f32[24,2560]{1,0:T(8,128)} fusion(bf16[1,384,2560]{2,1,0:T(8,128)(2,1)} %param.29, bf16[24,2560]{1,0:T(8,128)(2,1)S(1)} %gather_fusion.4, bf16[1,2560,384]{2,1,0:T(8,128)(2,1)} %param.28, f32[24]{0:T(128)S(1)} %compare_select_fusion.8, f32[24,384]{1,0:T(8,128)S(1)} %fusion.4), kind=kOutput, calls=%fused_computation.12 | convolution fusion | flops 94488576 | bytes 4337760 | tf_op jit(solution)/shard_map/dot_general | solution.py:129
  83.5 1.4 %collective-permute-start.4 = (f32[24,640]{1,0:T(8,128)S(1)}, f32[24,640]{1,0:T(8,128)S(1)}, u32[]{:S(2)}, u32[]{:S(2)}) collective-permute-start(f32[24,640]{1,0:T(8,128)S(1)} %get-tuple-element.15), channel_id=1, source_target_pairs={{0,2},{1,3},{2,0},{3,1},{4,6},{5,7},{6,4},{7,5},{8,10},{9,11},{10,... | collective-permute-start | bytes 184328 | tf_op jit(solution)/shard_map/ppermute | solution.py:133
  85.4 1.0 collective-permute-start.3
  86.5 1.7 %collective-permute-done.4 = f32[24,640]{1,0:T(8,128)S(1)} collective-permute-done((f32[24,640]{1,0:T(8,128)S(1)}, f32[24,640]{1,0:T(8,128)S(1)}, u32[]{:S(2)}, u32[]{:S(2)}) %collective-permute-start.4) | collective-permute-done | bytes 61472 | tf_op jit(solution)/shard_map/ppermute | solution.py:133
  88.2 1.5 %collective-permute-done.3 = f32[24,640]{1,0:T(8,128)S(1)} collective-permute-done((f32[24,640]{1,0:T(8,128)S(1)}, f32[24,640]{1,0:T(8,128)S(1)}, u32[]{:S(2)}, u32[]{:S(2)}) %collective-permute-start.3) | collective-permute-done | bytes 61472 | tf_op jit(solution)/shard_map/ppermute | solution.py:133
  91.3 1.3 %gather_fusion.6 = f32[64,640]{1,0:T(8,128)} fusion(f32[25,640]{1,0:T(8,128)S(1)} %concatenate.33, s32[1024]{0:T(1024)S(1)} %pad_clamp_fusion.1), kind=kCustom, calls=%fused_computation.6 | custom fusion | bytes 327936 | tf_op jit(solution)/shard_map/gather | solution.py:153
  92.6 1.0 select_add_fusion.1
  94.1 21.4 %all_to_all.19 = f32[64,1,1280]{2,1,0:T(1,128)} all-to-all(f32[64,1,1280]{2,1,0:T(1,128)S(1)} %copy.46), channel_id=1, replica_groups=mesh['req'=64,'kv'=4] {'req'}, dimensions={0} | all-to-all | bytes 655360 | tf_op jit(solution)/shard_map/all_to_all | solution.py:157
  115.4 1.2 %reduce_sum.53 = bf16[1280]{0:T(1024)(128)(2,1)S(1)} reduce(f32[64,1,1280]{2,1,0:T(1,128)} %all_to_all.19, f32[]{:T(128)} %constant.190.clone.1), dimensions={0,1}, to_apply=%region_11.12 | reduce | flops 80640 | bytes 330244 | tf_op jit(solution)/shard_map/reduce_sum | solution.py:157
  (87 shorter events, 16.2 us)
Async XLA Ops:
  0.0 37.6 %copy-start = (bf16[640,2560]{1,0:T(8,128)(2,1)S(1)}, bf16[640,2560]{1,0:T(8,128)(2,1)}, u32[]{:S(2)}) copy-start(bf16[640,2560]{1,0:T(8,128)(2,1)} %param.23) | copy-start | bytes 9830404
  0.0 17.6 %copy-start.6 = (s32[128]{0:T(128)S(1)}, s32[128]{0:T(128)}, u32[]{:S(2)}) copy-start(s32[128]{0:T(128)} %param.22) | copy-start | bytes 1540
  0.0 17.8 %copy-start.3 = (s32[128,6]{0,1:T(8,128)S(1)}, s32[128,6]{0,1:T(8,128)}, u32[]{:S(2)}) copy-start(s32[128,6]{0,1:T(8,128)} %param.25) | copy-start | bytes 9220
  0.0 17.9 %copy-start.4 = (f32[128,6]{0,1:T(8,128)S(1)}, f32[128,6]{0,1:T(8,128)}, u32[]{:S(2)}) copy-start(f32[128,6]{0,1:T(8,128)} %param.26) | copy-start | bytes 9220
  0.0 18.0 %copy-start.5 = (bf16[640]{0:T(1024)(128)(2,1)S(1)}, bf16[640]{0:T(1024)(128)(2,1)}, u32[]{:S(2)}) copy-start(bf16[640]{0:T(1024)(128)(2,1)} %param.24) | copy-start | bytes 3844
  0.0 18.4 %copy-start.1 = (s32[128]{0:T(128)S(1)}, s32[128]{0:T(128)}, u32[]{:S(2)}) copy-start(s32[128]{0:T(128)} %param.21) | copy-start | bytes 1540
  4.5 28.3 %all-to-all-start = ((bf16[64,2,1536]{2,1,0:T(2,128)(2,1)}), bf16[64,2,1536]{2,1,0:T(2,128)(2,1)}, u32[]{:S(2)}, u32[]{:S(2)}) async-start(bf16[64,2,1536]{2,1,0:T(2,128)(2,1)} %pad_maximum_fusion), calls=%async_computation | async-start | bytes 786432 | tf_op jit(solution)/shard_map/all_to_all | solution.py:52
  34.4 2.8 %copy-start.2 = (bf16[2,4096,128]{2,1,0:T(8,128)(2,1)S(1)}, bf16[2,4096,128]{2,1,0:T(8,128)(2,1)}, u32[]{:S(2)}) copy-start(bf16[2,4096,128]{2,1,0:T(8,128)(2,1)} %param.20) | copy-start | bytes 6291460
  38.2 5.4 %collective-permute-start.2 = (f32[3,2560]{1,0:T(4,128)S(1)}, f32[3,2560]{1,0:T(4,128)S(1)}, u32[]{:S(2)}, u32[]{:S(2)}) collective-permute-start(f32[3,2560]{1,0:T(4,128)S(1)} %add_dynamic-update-slice_fusion), channel_id=1, source_target_pairs={{0,3},{1,0},{2,1},{3,2},{4,7},{5,4},{6,5},{7,6},{8,11},{9,8},{10,9... | collective-permute-start | bytes 92168 | tf_op jit(solution)/shard_map/ppermute | solution.py:97
  41.1 4.4 %collective-permute-start.1 = (f32[3,2560]{1,0:T(4,128)S(1)}, f32[3,2560]{1,0:T(4,128)S(1)}, u32[]{:S(2)}, u32[]{:S(2)}) collective-permute-start(f32[3,2560]{1,0:T(4,128)S(1)} %add_dynamic-update-slice_fusion), channel_id=1, source_target_pairs={{0,2},{1,3},{2,0},{3,1},{4,6},{5,7},{6,4},{7,5},{8,10},{9,11},{10,... | collective-permute-start | bytes 92168 | tf_op jit(solution)/shard_map/ppermute | solution.py:97
  41.4 4.4 %collective-permute-start = (f32[3,2560]{1,0:T(4,128)S(1)}, f32[3,2560]{1,0:T(4,128)S(1)}, u32[]{:S(2)}, u32[]{:S(2)}) collective-permute-start(f32[3,2560]{1,0:T(4,128)S(1)} %add_dynamic-update-slice_fusion), channel_id=1, source_target_pairs={{0,1},{1,2},{2,3},{3,0},{4,5},{5,6},{6,7},{7,4},{8,9},{9,10},{10,1... | collective-permute-start | bytes 92168 | tf_op jit(solution)/shard_map/ppermute | solution.py:97
  47.5 27.3 %all-to-all-start.1 = ((bf16[64,2,2560]{2,1,0:T(2,128)(2,1)}), bf16[64,2,2560]{2,1,0:T(2,128)(2,1)}, u32[]{:S(2)}, u32[]{:S(2)}) async-start(bf16[64,2,2560]{2,1,0:T(2,128)(2,1)} %broadcast_select_fusion), calls=%async_computation.1 | async-start | bytes 1310720 | tf_op jit(solution)/shard_map/all_to_all | solution.py:115
  83.5 4.7 %collective-permute-start.4 = (f32[24,640]{1,0:T(8,128)S(1)}, f32[24,640]{1,0:T(8,128)S(1)}, u32[]{:S(2)}, u32[]{:S(2)}) collective-permute-start(f32[24,640]{1,0:T(8,128)S(1)} %get-tuple-element.15), channel_id=1, source_target_pairs={{0,2},{1,3},{2,0},{3,1},{4,6},{5,7},{6,4},{7,5},{8,10},{9,11},{10,... | collective-permute-start | bytes 184328 | tf_op jit(solution)/shard_map/ppermute | solution.py:133
  84.9 3.3 %collective-permute-start.5 = (f32[24,640]{1,0:T(8,128)S(1)}, f32[24,640]{1,0:T(8,128)S(1)}, u32[]{:S(2)}, u32[]{:S(2)}) collective-permute-start(f32[24,640]{1,0:T(8,128)S(1)} %get-tuple-element.16), channel_id=1, source_target_pairs={{0,3},{1,0},{2,1},{3,2},{4,7},{5,4},{6,5},{7,6},{8,11},{9,8},{10,9... | collective-permute-start | bytes 184328 | tf_op jit(solution)/shard_map/ppermute | solution.py:133
  85.4 4.4 %collective-permute-start.3 = (f32[24,640]{1,0:T(8,128)S(1)}, f32[24,640]{1,0:T(8,128)S(1)}, u32[]{:S(2)}, u32[]{:S(2)}) collective-permute-start(f32[24,640]{1,0:T(8,128)S(1)} %get-tuple-element.17), channel_id=1, source_target_pairs={{0,1},{1,2},{2,3},{3,0},{4,5},{5,6},{6,7},{7,4},{8,9},{9,10},{10,1... | collective-permute-start | bytes 184328 | tf_op jit(solution)/shard_map/ppermute | solution.py:133

commit v8 on v7

--- a/solution.py
+++ b/solution.py
@@ -3,7 +3,45 @@
 import jax
 import jax.numpy as jnp
 from jax import lax
+from jax.experimental import pallas as pl
+from jax.experimental.pallas import tpu as pltpu
 from jax.sharding import PartitionSpec as P
+
+
+def _ffn_body(x_ref, wg_ref, wu_ref, wd_ref, gate_ref, out_ref):
+    step = pl.program_id(0)
+
+    @pl.when(step == 0)
+    def _():
+        out_ref[...] = jnp.zeros_like(out_ref)
+
+    x = x_ref[...]
+    gate_h = jnp.dot(x, wg_ref[...], preferred_element_type=jnp.float32)
+    up_h = jnp.dot(x, wu_ref[...], preferred_element_type=jnp.float32)
+    inner = (gate_h / (1.0 + jnp.exp(-gate_h)) * up_h).astype(jnp.bfloat16)
+    out_ref[...] += jnp.dot(inner, wd_ref[...], preferred_element_type=jnp.float32)
+
+    @pl.when(step == pl.num_programs(0) - 1)
+    def _():
+        out_ref[...] = out_ref[...] * gate_ref[...]
+
+def expert_ffn(x, wg, wu, wd, row_gate, block=128):
+    rows, width = x.shape
+    hidden = wg.shape[1]
+    return pl.pallas_call(
+        _ffn_body,
+        grid=(hidden // block,),
+        in_specs=[
+            pl.BlockSpec((rows, width), lambda h: (0, 0)),
+            pl.BlockSpec((width, block), lambda h: (0, h)),
+            pl.BlockSpec((width, block), lambda h: (0, h)),
+            pl.BlockSpec((block, width), lambda h: (h, 0)),
+            pl.BlockSpec((rows, 1), lambda h: (0, 0)),
+        ],
+        out_specs=pl.BlockSpec((rows, width), lambda h: (0, 0)),
+        out_shape=jax.ShapeDtypeStruct((rows, width), jnp.float32),
+        compiler_params=pltpu.CompilerParams(dimension_semantics=("arbitrary",)),
+    )(x, wg, wu, wd, row_gate)
 
 
 def per_device(
@@ -123,12 +161,9 @@
     valid_rows = jnp.arange(capacity) < jnp.sum(uses_expert.astype(jnp.int32))
     picked_slots = slot_of[picked]
     row_block = by_slot[picked_slots // per_dev, picked_slots % per_dev]
-    gate_h = jnp.dot(row_block, gate_proj[0], preferred_element_type=jnp.float32)
-    up_h = jnp.dot(row_block, up_proj[0], preferred_element_type=jnp.float32)
-    inner_act = (jax.nn.silu(gate_h) * up_h).astype(jnp.bfloat16)
-    outputs = jnp.dot(inner_act, down_proj[0], preferred_element_type=jnp.float32)
     row_gate = jnp.where(valid_rows, token_gate[picked], 0.0)
-    weighted = outputs * row_gate[:, None]
+    weighted = expert_ffn(row_block, gate_proj[0], up_proj[0], down_proj[0], row_gate[:, None])
+
     weighted = lax.dynamic_slice_in_dim(weighted, col_start, col_count, axis=1) + sum(
         lax.ppermute(
             lax.dynamic_slice_in_dim(

time: 118 us -> 118 us (level)
  matrix products: 9.22 us -> 3.54 us
  Pallas kernels: 0 us -> 5 us
  starting transfers between devices: 26.9 us -> 28.9 us
  waiting for transfers between devices: 33.1 us -> 31.2 us
    dot_general x2 -> x0, matrix products: 5.69 us -> none  [the longest x1 3.75 us: per_device(): jnp.dot(inner_act, down_proj[0], preferred_element_type=jnp.float32)]
    pallas_call x0 -> x1, Pallas kernels: none -> 5 us  [expert_ffn(): pl.pallas_call(_ffn_body, grid=(hidden // block,), in_specs=[pl.BlockSpec...]
    ppermute x3, starting transfers between devices: 3.85 us -> 5.06 us  [per_device(): lax.ppermute(summed_in, 'kv', [(i, (i + shift) % kv_count) for i in range...]
  transfers between devices with their start and end apart: 8 -> 8, of which waited for: 6 -> 7; matrix products, arithmetic and copies ran while one was open for 8% -> 8% of each run, Pallas kernels for 0% -> 0%
where the time goes in v8:
time: 118 us; the launch traced here: 117 us
  waiting for transfers between devices  31.2 us (26%)
  starting transfers between devices  28.9 us (24%)
  blocking collectives  20.8 us (18%)
  local copies, waits for them, and re-layouts  15.6 us (13%)
  other arithmetic  11.8 us (10%)
  Pallas kernels  5 us (4%)
  matrix products  3.54 us (3%)
    all_to_all x1, blocking collectives, per_device(): lax.all_to_all(combined, 'req', 0, 0, tiled=True)  20.8 us
    all_to_all x1, waiting for transfers between devices, per_device(): by_slot = lax.all_to_all(to_experts, 'req', 0, 0, tiled=False)  13.6 us
    all_to_all x1, starting transfers between devices, per_device(): from_homes = lax.all_to_all(to_slots, 'req', 0, 0, tiled=False)  13.1 us
    all_to_all x1, waiting for transfers between devices, per_device(): from_homes = lax.all_to_all(to_slots, 'req', 0, 0, tiled=False)  12.4 us
    all_to_all x1, starting transfers between devices, per_device(): by_slot = lax.all_to_all(to_experts, 'req', 0, 0, tiled=False)  7.14 us
    ppermute x3, starting transfers between devices, per_device(): lax.ppermute(summed_in, 'kv', [(i, (i + shift) % kv_count) for i in range...  5.06 us
    pallas_call x1, Pallas kernels, expert_ffn(): pl.pallas_call(_ffn_body, grid=(hidden // block,), in_specs=[pl.BlockSpec...  5 us
    ppermute x3, waiting for transfers between devices, per_device(): lax.ppermute(lax.dynamic_slice_in_dim(weighted, (kv_index + shift) % kv_c...  3.76 us
  transfers between devices with their start and end apart: 8, of which 7 were waited for; matrix products, arithmetic and copies ran while one was open for 8% of the time, Pallas kernels for 0%

profile of v8, /device:TPU:1, one launch (start us, length us, event | category | flops | bytes accessed | tf_op | source)
XLA Modules:
  0.0 117.2 jit_solution(215262530269598467)
XLA Ops:
  3.3 1.1 pad_maximum_fusion
  4.4 13.1 %all-to-all-start = ((bf16[64,2,1536]{2,1,0:T(2,128)(2,1)}), bf16[64,2,1536]{2,1,0:T(2,128)(2,1)}, u32[]{:S(2)}, u32[]{:S(2)}) async-start(bf16[64,2,1536]{2,1,0:T(2,128)(2,1)} %pad_maximum_fusion), calls=%async_computation | async-start | bytes 786432 | tf_op jit(solution)/shard_map/all_to_all | solution.py:90
  20.3 12.4 %all-to-all-done = bf16[64,2,1536]{2,1,0:T(2,128)(2,1)} async-done(((bf16[64,2,1536]{2,1,0:T(2,128)(2,1)}), bf16[64,2,1536]{2,1,0:T(2,128)(2,1)}, u32[]{:S(2)}, u32[]{:S(2)}) %all-to-all-start) | async-done | bytes 393248 | tf_op jit(solution)/shard_map/all_to_all | solution.py:90
  32.7 1.6 %gather_fusion.2 = bf16[2,1536]{1,0:T(2,128)(2,1)S(1)} fusion(bf16[64,2,1536]{2,1,0:T(2,128)(2,1)} %all-to-all-done, s32[2]{0:T(128)S(1)} %fusion.39), kind=kCustom, calls=%fused_computation.2 | custom fusion | bytes 12304 | tf_op jit(solution)/shard_map/gather | solution.py:92
  34.5 2.4 %fusion.50 = (f32[2,5]{1,0:T(2,128)S(1)}, f32[2,5,4096]{2,1,0:T(8,128)S(1)}) fusion(bf16[2,5,128]{2,1,0:T(8,128)(2,1)S(1)} %reshape.304, bf16[2,4096,128]{2,1,0:T(8,128)(2,1)} %param.19, pred[2,4096]{1,0:T(4,128)(4,1)S(1)} %iota_compare_fusion), kind=kOutput, calls=%fused_computation.151 | convolution fusion | flops 10608630 | bytes 2271784 | tf_op jit(solution)/shard_map/rqd,rld->rql/dot_general | solution.py:101
  38.2 1.4 %collective-permute-start = (f32[3,2560]{1,0:T(4,128)S(1)}, f32[3,2560]{1,0:T(4,128)S(1)}, u32[]{:S(2)}, u32[]{:S(2)}) collective-permute-start(f32[3,2560]{1,0:T(4,128)S(1)} %add_dynamic-update-slice_fusion), channel_id=1, source_target_pairs={{0,1},{1,2},{2,3},{3,0},{4,5},{5,6},{6,7},{7,4},{8,9},{9,10},{10,1... | collective-permute-start | bytes 92168 | tf_op jit(solution)/shard_map/ppermute | solution.py:135
  39.6 2.6 %collective-permute-start.1 = (f32[3,2560]{1,0:T(4,128)S(1)}, f32[3,2560]{1,0:T(4,128)S(1)}, u32[]{:S(2)}, u32[]{:S(2)}) collective-permute-start(f32[3,2560]{1,0:T(4,128)S(1)} %add_dynamic-update-slice_fusion), channel_id=1, source_target_pairs={{0,2},{1,3},{2,0},{3,1},{4,6},{5,7},{6,4},{7,5},{8,10},{9,11},{10,... | collective-permute-start | bytes 92168 | tf_op jit(solution)/shard_map/ppermute | solution.py:135
  42.2 1.1 collective-permute-start.2
  44.2 1.1 collective-permute-done.2
  45.5 1.4 %broadcast_select_fusion = bf16[64,2,2560]{2,1,0:T(2,128)(2,1)} fusion(pred[64,2]{1,0:T(8,128)(4,1)S(1)} %copy.42, bf16[2,2560]{1,0:T(2,128)(2,1)S(1)} %multiply_convert_fusion), kind=kLoop, calls=%fused_computation.12 | loop fusion | flops 327680 | bytes 665728 | tf_op jit(solution)/shard_map/jit(_where)/select_n | solution.py:152
  46.9 7.1 %all-to-all-start.1 = ((bf16[64,2,2560]{2,1,0:T(2,128)(2,1)}), bf16[64,2,2560]{2,1,0:T(2,128)(2,1)}, u32[]{:S(2)}, u32[]{:S(2)}) async-start(bf16[64,2,2560]{2,1,0:T(2,128)(2,1)} %broadcast_select_fusion), calls=%async_computation.1 | async-start | bytes 1310720 | tf_op jit(solution)/shard_map/all_to_all | solution.py:153
  54.1 1.0 scatter_custom_fusion
  55.4 1.4 %scatter_custom_fusion.1 = s32[24]{0:T(128)S(1)} fusion(s32[128]{0:T(128)S(1)} %get-tuple-element.6, s32[128]{0:T(128)S(1)} %broadcast.464, s32[]{:T(128)} %constant.178.clone.1), kind=kCustom, calls=%fused_computation.143 | custom fusion | flops 128 | bytes 100 | tf_op jit(solution)/shard_map/scatter-add | solution.py:160
  59.5 1.2 %fusion.26.gate_ref = f32[24,1]{1,0:T(8,128)} fusion(f32[24,1]{1,0:T(8,128)S(1)} %copy.49, s32[]{:T(128)} %get-tuple-element.39), kind=kLoop, calls=%fused_computation.78 | loop fusion | flops 48 | bytes 196 | tf_op jit(solution)/shard_map/jit(_where)/select_n | solution.py:164
  60.7 13.6 %all-to-all-done.1 = bf16[64,2,2560]{2,1,0:T(2,128)(2,1)} async-done(((bf16[64,2,2560]{2,1,0:T(2,128)(2,1)}), bf16[64,2,2560]{2,1,0:T(2,128)(2,1)}, u32[]{:S(2)}, u32[]{:S(2)}) %all-to-all-start.1) | async-done | bytes 655392 | tf_op jit(solution)/shard_map/all_to_all | solution.py:153
  74.3 2.6 %gather_fusion.4 = bf16[24,2560]{1,0:T(8,128)(2,1)} fusion(bf16[64,2,2560]{2,1,0:T(2,128)(2,1)} %all-to-all-done.1, s32[24]{0:T(128)S(1)} %fusion.23), kind=kCustom, calls=%fused_computation.4 | custom fusion | bytes 245952 | tf_op jit(solution)/shard_map/gather | solution.py:163
  76.9 5.0 %shard_map.145 = f32[24,2560]{1,0:T(8,128)} custom-call(bf16[24,2560]{1,0:T(8,128)(2,1)} %gather_fusion.4, bf16[2560,384]{1,0:T(8,128)(2,1)} %bitcast.40, bf16[2560,384]{1,0:T(8,128)(2,1)} %bitcast.41, bf16[384,2560]{1,0:T(8,128)(2,1)} %bitcast.42, f32[24,1]{1,0:T(8,128)} %fusion.26.gate_ref), custom_call_target="tpu_custom_call" | custom-call | tf_op jit(solution)/shard_map/pallas_call | solution.py:31
  82.9 3.5 %collective-permute-start.4 = (f32[24,640]{1,0:T(8,128)S(1)}, f32[24,640]{1,0:T(8,128)S(1)}, u32[]{:S(2)}, u32[]{:S(2)}) collective-permute-start(f32[24,640]{1,0:T(8,128)S(1)} %get-tuple-element.15), channel_id=1, source_target_pairs={{0,2},{1,3},{2,0},{3,1},{4,6},{5,7},{6,4},{7,5},{8,10},{9,11},{10,... | collective-permute-start | bytes 184328 | tf_op jit(solution)/shard_map/ppermute | solution.py:168
  87.2 1.5 %collective-permute-done.4 = f32[24,640]{1,0:T(8,128)S(1)} collective-permute-done((f32[24,640]{1,0:T(8,128)S(1)}, f32[24,640]{1,0:T(8,128)S(1)}, u32[]{:S(2)}, u32[]{:S(2)}) %collective-permute-start.4) | collective-permute-done | bytes 61472 | tf_op jit(solution)/shard_map/ppermute | solution.py:168
  88.7 1.5 %collective-permute-done.5 = f32[24,640]{1,0:T(8,128)S(1)} collective-permute-done((f32[24,640]{1,0:T(8,128)S(1)}, f32[24,640]{1,0:T(8,128)S(1)}, u32[]{:S(2)}, u32[]{:S(2)}) %collective-permute-start.5) | collective-permute-done | bytes 61472 | tf_op jit(solution)/shard_map/ppermute | solution.py:168
  91.8 1.3 %gather_fusion.6 = f32[64,640]{1,0:T(8,128)} fusion(f32[25,640]{1,0:T(8,128)S(1)} %concatenate.33, s32[1024]{0:T(1024)S(1)} %pad_clamp_fusion.1), kind=kCustom, calls=%fused_computation.6 | custom fusion | bytes 327936 | tf_op jit(solution)/shard_map/gather | solution.py:188
  93.1 1.0 select_add_fusion.1
  94.5 20.8 %all_to_all.19 = f32[64,1,1280]{2,1,0:T(1,128)} all-to-all(f32[64,1,1280]{2,1,0:T(1,128)S(1)} %copy.50), channel_id=1, replica_groups=mesh['req'=64,'kv'=4] {'req'}, dimensions={0} | all-to-all | bytes 655360 | tf_op jit(solution)/shard_map/all_to_all | solution.py:192
  115.4 1.2 %reduce_sum.53 = bf16[1280]{0:T(1024)(128)(2,1)S(1)} reduce(f32[64,1,1280]{2,1,0:T(1,128)} %all_to_all.19, f32[]{:T(128)} %constant.188.clone.1), dimensions={0,1}, to_apply=%region_11.12 | reduce | flops 80640 | bytes 330244 | tf_op jit(solution)/shard_map/reduce_sum | solution.py:192
  (87 shorter events, 15.7 us)
Async XLA Ops:
  0.0 37.6 %copy-start = (bf16[640,2560]{1,0:T(8,128)(2,1)S(1)}, bf16[640,2560]{1,0:T(8,128)(2,1)}, u32[]{:S(2)}) copy-start(bf16[640,2560]{1,0:T(8,128)(2,1)} %param.23) | copy-start | bytes 9830404
  0.0 17.6 %copy-start.6 = (s32[128]{0:T(128)S(1)}, s32[128]{0:T(128)}, u32[]{:S(2)}) copy-start(s32[128]{0:T(128)} %param.22) | copy-start | bytes 1540
  0.0 17.8 %copy-start.5 = (bf16[640]{0:T(1024)(128)(2,1)S(1)}, bf16[640]{0:T(1024)(128)(2,1)}, u32[]{:S(2)}) copy-start(bf16[640]{0:T(1024)(128)(2,1)} %param.24) | copy-start | bytes 3844
  0.0 17.8 %copy-start.3 = (s32[128,6]{0,1:T(8,128)S(1)}, s32[128,6]{0,1:T(8,128)}, u32[]{:S(2)}) copy-start(s32[128,6]{0,1:T(8,128)} %param.25) | copy-start | bytes 9220
  0.0 17.9 %copy-start.1 = (s32[128]{0:T(128)S(1)}, s32[128]{0:T(128)}, u32[]{:S(2)}) copy-start(s32[128]{0:T(128)} %param.21) | copy-start | bytes 1540
  0.0 19.1 %copy-start.4 = (f32[128,6]{0,1:T(8,128)S(1)}, f32[128,6]{0,1:T(8,128)}, u32[]{:S(2)}) copy-start(f32[128,6]{0,1:T(8,128)} %param.26) | copy-start | bytes 9220
  4.4 28.3 %all-to-all-start = ((bf16[64,2,1536]{2,1,0:T(2,128)(2,1)}), bf16[64,2,1536]{2,1,0:T(2,128)(2,1)}, u32[]{:S(2)}, u32[]{:S(2)}) async-start(bf16[64,2,1536]{2,1,0:T(2,128)(2,1)} %pad_maximum_fusion), calls=%async_computation | async-start | bytes 786432 | tf_op jit(solution)/shard_map/all_to_all | solution.py:90
  34.3 2.8 %copy-start.2 = (bf16[2,4096,128]{2,1,0:T(8,128)(2,1)S(1)}, bf16[2,4096,128]{2,1,0:T(8,128)(2,1)}, u32[]{:S(2)}) copy-start(bf16[2,4096,128]{2,1,0:T(8,128)(2,1)} %param.20) | copy-start | bytes 6291460
  38.2 5.6 %collective-permute-start = (f32[3,2560]{1,0:T(4,128)S(1)}, f32[3,2560]{1,0:T(4,128)S(1)}, u32[]{:S(2)}, u32[]{:S(2)}) collective-permute-start(f32[3,2560]{1,0:T(4,128)S(1)} %add_dynamic-update-slice_fusion), channel_id=1, source_target_pairs={{0,1},{1,2},{2,3},{3,0},{4,5},{5,6},{6,7},{7,4},{8,9},{9,10},{10,1... | collective-permute-start | bytes 92168 | tf_op jit(solution)/shard_map/ppermute | solution.py:135
  39.6 4.6 %collective-permute-start.1 = (f32[3,2560]{1,0:T(4,128)S(1)}, f32[3,2560]{1,0:T(4,128)S(1)}, u32[]{:S(2)}, u32[]{:S(2)}) collective-permute-start(f32[3,2560]{1,0:T(4,128)S(1)} %add_dynamic-update-slice_fusion), channel_id=1, source_target_pairs={{0,2},{1,3},{2,0},{3,1},{4,6},{5,7},{6,4},{7,5},{8,10},{9,11},{10,... | collective-permute-start | bytes 92168 | tf_op jit(solution)/shard_map/ppermute | solution.py:135
  42.2 3.0 %collective-permute-start.2 = (f32[3,2560]{1,0:T(4,128)S(1)}, f32[3,2560]{1,0:T(4,128)S(1)}, u32[]{:S(2)}, u32[]{:S(2)}) collective-permute-start(f32[3,2560]{1,0:T(4,128)S(1)} %add_dynamic-update-slice_fusion), channel_id=1, source_target_pairs={{0,3},{1,0},{2,1},{3,2},{4,7},{5,4},{6,5},{7,6},{8,11},{9,8},{10,9... | collective-permute-start | bytes 92168 | tf_op jit(solution)/shard_map/ppermute | solution.py:135
  46.9 27.4 %all-to-all-start.1 = ((bf16[64,2,2560]{2,1,0:T(2,128)(2,1)}), bf16[64,2,2560]{2,1,0:T(2,128)(2,1)}, u32[]{:S(2)}, u32[]{:S(2)}) async-start(bf16[64,2,2560]{2,1,0:T(2,128)(2,1)} %broadcast_select_fusion), calls=%async_computation.1 | async-start | bytes 1310720 | tf_op jit(solution)/shard_map/all_to_all | solution.py:153
  82.8 4.4 %collective-permute-start.3 = (f32[24,640]{1,0:T(8,128)S(1)}, f32[24,640]{1,0:T(8,128)S(1)}, u32[]{:S(2)}, u32[]{:S(2)}) collective-permute-start(f32[24,640]{1,0:T(8,128)S(1)} %get-tuple-element.17), channel_id=1, source_target_pairs={{0,1},{1,2},{2,3},{3,0},{4,5},{5,6},{6,7},{7,4},{8,9},{9,10},{10,1... | collective-permute-start | bytes 184328 | tf_op jit(solution)/shard_map/ppermute | solution.py:168
  82.9 5.8 %collective-permute-start.4 = (f32[24,640]{1,0:T(8,128)S(1)}, f32[24,640]{1,0:T(8,128)S(1)}, u32[]{:S(2)}, u32[]{:S(2)}) collective-permute-start(f32[24,640]{1,0:T(8,128)S(1)} %get-tuple-element.15), channel_id=1, source_target_pairs={{0,2},{1,3},{2,0},{3,1},{4,6},{5,7},{6,4},{7,5},{8,10},{9,11},{10,... | collective-permute-start | bytes 184328 | tf_op jit(solution)/shard_map/ppermute | solution.py:168
  86.4 3.9 %collective-permute-start.5 = (f32[24,640]{1,0:T(8,128)S(1)}, f32[24,640]{1,0:T(8,128)S(1)}, u32[]{:S(2)}, u32[]{:S(2)}) collective-permute-start(f32[24,640]{1,0:T(8,128)S(1)} %get-tuple-element.16), channel_id=1, source_target_pairs={{0,3},{1,0},{2,1},{3,2},{4,7},{5,4},{6,5},{7,6},{8,11},{9,8},{10,9... | collective-permute-start | bytes 184328 | tf_op jit(solution)/shard_map/ppermute | solution.py:168

commit v9 on v7

--- a/solution.py
+++ b/solution.py
@@ -85,13 +85,10 @@
     projected = jnp.dot(attended, out_proj, preferred_element_type=jnp.float32)
 
     col_start = kv_index * col_count
-    own_cols = jnp.concatenate(
-        [residual_rows.astype(jnp.float32), norm_gain.astype(jnp.float32)[None, :]], axis=0
-    )
-    summed_in = jnp.concatenate(
-        [projected, jnp.zeros((1, model_width), jnp.float32)], axis=0
-    ) + lax.dynamic_update_slice(
-        jnp.zeros((per_dev + 1, model_width), jnp.float32), own_cols, (0, col_start)
+    summed_in = projected + lax.dynamic_update_slice(
+        jnp.zeros((per_dev, model_width), jnp.float32),
+        residual_rows.astype(jnp.float32),
+        (0, col_start),
     )
     parts = [summed_in] + [
         lax.ppermute(summed_in, "kv", [(i, (i + shift) % kv_count) for i in range(kv_count)])
@@ -100,12 +97,14 @@
     summed = parts[0]
     for part in parts[1:]:
         summed = summed + part
-    hidden = summed[:per_dev]
-    gain = summed[per_dev]
+    hidden = summed
     squares = jnp.sum(hidden * hidden, axis=1)
-    normed = (hidden * lax.rsqrt(squares / model_width + 1e-06)[:, None] * gain).astype(
-        jnp.bfloat16
-    )
+    own_hidden = lax.dynamic_slice_in_dim(hidden, col_start, col_count, axis=1)
+    normed = (
+        own_hidden
+        * lax.rsqrt(squares / model_width + 1e-06)[:, None]
+        * norm_gain.astype(jnp.float32)[None, :]
+    ).astype(jnp.bfloat16)
     local_count = gate_proj.shape[0]
     served_ids = expert_ids[served] // local_count
     wanted = jnp.any(
@@ -123,8 +122,25 @@
     valid_rows = jnp.arange(capacity) < jnp.sum(uses_expert.astype(jnp.int32))
     picked_slots = slot_of[picked]
     row_block = by_slot[picked_slots // per_dev, picked_slots % per_dev]
-    gate_h = jnp.dot(row_block, gate_proj[0], preferred_element_type=jnp.float32)
-    up_h = jnp.dot(row_block, up_proj[0], preferred_element_type=jnp.float32)
+    kv_shifts = range(1, kv_count)
+    from_peers = [
+        lax.ppermute(row_block, "kv", [(i, (i + shift) % kv_count) for i in range(kv_count)])
+        for shift in kv_shifts
+    ]
+
+    def block_rows(weights, source):
+        return lax.dynamic_slice_in_dim(weights, source * col_count, col_count, axis=0)
+
+    gate_h = jnp.dot(row_block, block_rows(gate_proj[0], kv_index), preferred_element_type=jnp.float32)
+    up_h = jnp.dot(row_block, block_rows(up_proj[0], kv_index), preferred_element_type=jnp.float32)
+    for shift, peer_rows in zip(kv_shifts, from_peers):
+        source = (kv_index - shift) % kv_count
+        gate_h = gate_h + jnp.dot(
+            peer_rows, block_rows(gate_proj[0], source), preferred_element_type=jnp.float32
+        )
+        up_h = up_h + jnp.dot(
+            peer_rows, block_rows(up_proj[0], source), preferred_element_type=jnp.float32
+        )
     inner_act = (jax.nn.silu(gate_h) * up_h).astype(jnp.bfloat16)
     outputs = jnp.dot(inner_act, down_proj[0], preferred_element_type=jnp.float32)
     row_gate = jnp.where(valid_rows, token_gate[picked], 0.0)
@@ -140,7 +156,6 @@
         for shift in range(1, kv_count)
     )
 
-    own_hidden = lax.dynamic_slice_in_dim(hidden, col_start, col_count, axis=1)
     at_pick = jnp.where(uses_expert, jnp.cumsum(uses_expert.astype(jnp.int32)) - 1, capacity)
     weighted_ext = jnp.concatenate([weighted, jnp.zeros((1, col_count), jnp.float32)], axis=0)
     halves = []

time: 118 us -> 112 us (0.949)
  waiting for transfers between devices: 33.1 us -> 17.1 us
  starting transfers between devices: 26.9 us -> 33 us
  matrix products: 9.22 us -> 14.1 us
  other arithmetic: 11.2 us -> 12.8 us
  local copies, waits for them, and re-layouts: 15 us -> 13.6 us
    all_to_all x1, waiting for transfers between devices: 13 us -> 5.37 us  [per_device(): from_homes = lax.all_to_all(to_slots, 'req', 0, 0, tiled=False)]
    dot_general x1 -> x7, matrix products: 1.93 us -> 8.31 us  [the longest x2 3.68 us: per_device(): jnp.dot(peer_rows, block_rows(gate_proj[0], source), preferred_element_ty...]
    all_to_all x1, waiting for transfers between devices: 14.7 us -> 10.5 us  [per_device(): by_slot = lax.all_to_all(to_experts, 'req', 0, 0, tiled=False)]
    ppermute x0 -> x3, starting transfers between devices: none -> 3.53 us  [per_device(): lax.ppermute(row_block, 'kv', [(i, (i + shift) % kv_count) for i in range...]
    ppermute x3, waiting for transfers between devices: 3.25 us -> 0.19 us  [per_device(): lax.ppermute(lax.dynamic_slice_in_dim(weighted, (kv_index + shift) % kv_c...]
    ppermute x3, starting transfers between devices: 2.86 us -> 4.33 us  [per_device(): lax.ppermute(lax.dynamic_slice_in_dim(weighted, (kv_index + shift) % kv_c...]
    dot_general x1, matrix products: 3.75 us -> 2.31 us  [per_device(): jnp.dot(inner_act, down_proj[0], preferred_element_type=jnp.float32)]
    gather x1, local copies, waits for them, and re-layouts: 2.09 us -> 0.81 us  [per_device(): row_block = by_slot[picked_slots // per_dev, picked_slots % per_dev]]
  transfers between devices with their start and end apart: 8 -> 11, of which waited for: 6 -> 4; matrix products, arithmetic and copies ran while one was open for 8% -> 18% of each run, Pallas kernels for 0% -> 0%
where the time goes in v9:
time: 112 us
  starting transfers between devices  33 us (29%)
  blocking collectives  20.5 us (18%)
  waiting for transfers between devices  17.1 us (15%)
  matrix products  14.1 us (13%)
  local copies, waits for them, and re-layouts  13.6 us (12%)
  other arithmetic  12.8 us (11%)
    all_to_all x1, blocking collectives, per_device(): lax.all_to_all(combined, 'req', 0, 0, tiled=True)  20.5 us
    all_to_all x1, starting transfers between devices, per_device(): from_homes = lax.all_to_all(to_slots, 'req', 0, 0, tiled=False)  13.1 us
    all_to_all x1, waiting for transfers between devices, per_device(): by_slot = lax.all_to_all(to_experts, 'req', 0, 0, tiled=False)  10.5 us
    all_to_all x1, starting transfers between devices, per_device(): by_slot = lax.all_to_all(to_experts, 'req', 0, 0, tiled=False)  6.98 us
    all_to_all x1, waiting for transfers between devices, per_device(): from_homes = lax.all_to_all(to_slots, 'req', 0, 0, tiled=False)  5.37 us
    ppermute x3, starting transfers between devices, per_device(): lax.ppermute(summed_in, 'kv', [(i, (i + shift) % kv_count) for i in range...  5.05 us
    ppermute x3, starting transfers between devices, per_device(): lax.ppermute(lax.dynamic_slice_in_dim(weighted, (kv_index + shift) % kv_c...  4.33 us
    dot_general x2, matrix products, per_device(): jnp.dot(peer_rows, block_rows(gate_proj[0], source), preferred_element_ty...  3.68 us
  transfers between devices with their start and end apart: 11, of which 4 were waited for; matrix products, arithmetic and copies ran while one was open for 18% of the time, Pallas kernels for 0%

profile of v9, /device:TPU:1, one launch (start us, length us, event | category | flops | bytes accessed | tf_op | source)
XLA Modules:
  0.0 111.7 jit_solution(16297133209144909681)
XLA Ops:
  3.3 1.1 %pad_maximum_fusion = bf16[64,2,1536]{2,1,0:T(2,128)(2,1)} fusion(bf16[64,2,640]{2,1,0:T(2,128)(2,1)S(1)} %get-tuple-element.23, bf16[64,2,128]{2,1,0:T(2,128)(2,1)S(1)} %get-tuple-element.25, bf16[64,2,128]{2,1,0:T(2,128)(2,1)S(1)} %get-tuple-element.24, bf16[64,2,640]{2,1,0:T(2,128)(2,1)S(1)} %get-tuple-element.22), kind=kLoop, calls=%fused_computation.44 | loop fusion | flops 1572864 | bytes 786432 | tf_op jit(solution)/shard_map/concatenate | solution.py:51
  4.4 13.1 %all-to-all-start = ((bf16[64,2,1536]{2,1,0:T(2,128)(2,1)}), bf16[64,2,1536]{2,1,0:T(2,128)(2,1)}, u32[]{:S(2)}, u32[]{:S(2)}) async-start(bf16[64,2,1536]{2,1,0:T(2,128)(2,1)} %pad_maximum_fusion), calls=%async_computation | async-start | bytes 786432 | tf_op jit(solution)/shard_map/all_to_all | solution.py:52
  20.5 1.4 %scatter_custom_fusion.1 = s32[24]{0:T(128)S(1)} fusion(s32[128]{0:T(128)S(1)} %get-tuple-element.6, s32[128]{0:T(128)S(1)} %broadcast.462, s32[]{:T(128)} %constant.202.clone.1), kind=kCustom, calls=%fused_computation.180 | custom fusion | flops 128 | bytes 100 | tf_op jit(solution)/shard_map/scatter-add | solution.py:121
  25.5 1.2 %compare_select_fusion.8 = f32[24]{0:T(128)} fusion(f32[24]{0:T(128)S(1)} %gather_fusion.5, s32[]{:T(128)} %get-tuple-element.37), kind=kLoop, calls=%fused_computation.145 | loop fusion | flops 48 | bytes 196 | tf_op jit(solution)/shard_map/jit(_where)/select_n | solution.py:146
  27.3 5.4 %all-to-all-done = bf16[64,2,1536]{2,1,0:T(2,128)(2,1)} async-done(((bf16[64,2,1536]{2,1,0:T(2,128)(2,1)}), bf16[64,2,1536]{2,1,0:T(2,128)(2,1)}, u32[]{:S(2)}, u32[]{:S(2)}) %all-to-all-start) | async-done | bytes 393248 | tf_op jit(solution)/shard_map/all_to_all | solution.py:52
  32.7 1.6 %gather_fusion.2 = bf16[2,1536]{1,0:T(2,128)(2,1)S(1)} fusion(bf16[64,2,1536]{2,1,0:T(2,128)(2,1)} %all-to-all-done, s32[2]{0:T(128)S(1)} %fusion.76), kind=kCustom, calls=%fused_computation.2 | custom fusion | bytes 12304 | tf_op jit(solution)/shard_map/gather | solution.py:54
  34.4 2.4 %fusion.87 = (f32[2,5]{1,0:T(2,128)S(1)}, f32[2,5,4096]{2,1,0:T(8,128)S(1)}) fusion(bf16[2,5,128]{2,1,0:T(8,128)(2,1)S(1)} %reshape.306, bf16[2,4096,128]{2,1,0:T(8,128)(2,1)} %param.19, pred[2,4096]{1,0:T(4,128)(4,1)S(1)} %iota_compare_fusion), kind=kOutput, calls=%fused_computation.188 | convolution fusion | flops 10608630 | bytes 2271784 | tf_op jit(solution)/shard_map/rqd,rld->rql/dot_general | solution.py:63
  38.1 1.4 %collective-permute-start = (f32[2,2560]{1,0:T(2,128)S(1)}, f32[2,2560]{1,0:T(2,128)S(1)}, u32[]{:S(2)}, u32[]{:S(2)}) collective-permute-start(f32[2,2560]{1,0:T(2,128)S(1)} %add_dynamic-update-slice_fusion), channel_id=1, source_target_pairs={{0,1},{1,2},{2,3},{3,0},{4,5},{5,6},{6,7},{7,4},{8,9},{9,10},{10,1... | collective-permute-start | bytes 61448 | tf_op jit(solution)/shard_map/ppermute | solution.py:94
  39.5 2.6 %collective-permute-start.1 = (f32[2,2560]{1,0:T(2,128)S(1)}, f32[2,2560]{1,0:T(2,128)S(1)}, u32[]{:S(2)}, u32[]{:S(2)}) collective-permute-start(f32[2,2560]{1,0:T(2,128)S(1)} %add_dynamic-update-slice_fusion), channel_id=1, source_target_pairs={{0,2},{1,3},{2,0},{3,1},{4,6},{5,7},{6,4},{7,5},{8,10},{9,11},{10,... | collective-permute-start | bytes 61448 | tf_op jit(solution)/shard_map/ppermute | solution.py:94
  42.1 1.1 collective-permute-start.2
  46.0 7.0 %all-to-all-start.1 = ((bf16[64,2,640]{2,1,0:T(2,128)(2,1)}), bf16[64,2,640]{2,1,0:T(2,128)(2,1)S(1)}, u32[]{:S(2)}, u32[]{:S(2)}) async-start(bf16[64,2,640]{2,1,0:T(2,128)(2,1)} %broadcast_select_fusion.4), calls=%async_computation.1 | async-start | bytes 327680 | tf_op jit(solution)/shard_map/all_to_all | solution.py:114
  54.2 10.5 %all-to-all-done.1 = bf16[64,2,640]{2,1,0:T(2,128)(2,1)S(1)} async-done(((bf16[64,2,640]{2,1,0:T(2,128)(2,1)}), bf16[64,2,640]{2,1,0:T(2,128)(2,1)S(1)}, u32[]{:S(2)}, u32[]{:S(2)}) %all-to-all-start.1) | async-done | bytes 163872 | tf_op jit(solution)/shard_map/all_to_all | solution.py:114
  65.6 2.7 %collective-permute-start.5 = (bf16[24,640]{1,0:T(8,128)(2,1)S(1)}, bf16[24,640]{1,0:T(8,128)(2,1)S(1)}, u32[]{:S(2)}, u32[]{:S(2)}) collective-permute-start(bf16[24,640]{1,0:T(8,128)(2,1)S(1)} %gather_fusion.4), channel_id=1, source_target_pairs={{0,3},{1,0},{2,1},{3,2},{4,7},{5,4},{6,5},{7,6},{8,11},{9,8},{10,9... | collective-permute-start | bytes 92168 | tf_op jit(solution)/shard_map/ppermute | solution.py:127
  69.0 1.2 %fusion.17 = f32[24,384]{1,0:T(8,128)S(1)} fusion(bf16[24,640]{1,0:T(8,128)(2,1)S(1)} %gather_fusion.4, bf16[1,2560,384]{2,1,0:T(8,128)(2,1)} %param.27, s32[]{:T(128)S(6)} %select_n.296), kind=kOutput, calls=%fused_computation.34 | convolution fusion | flops 11796480 | bytes 559108 | tf_op jit(solution)/shard_map/dot_general | solution.py:134
  70.3 1.2 %fusion.11 = f32[24,384]{1,0:T(8,128)S(1)} fusion(bf16[24,640]{1,0:T(8,128)(2,1)S(1)} %gather_fusion.4, bf16[1,2560,384]{2,1,0:T(8,128)(2,1)} %param.28, s32[]{:T(128)S(6)} %select_n.296), kind=kOutput, calls=%fused_computation.28 | convolution fusion | flops 11796480 | bytes 559108 | tf_op jit(solution)/shard_map/dot_general | solution.py:135
  71.5 1.8 %convolution_add_fusion.3 = f32[24,384]{1,0:T(8,128)} fusion(f32[24,384]{1,0:T(8,128)S(1)} %fusion.17, bf16[24,640]{1,0:T(8,128)(2,1)S(1)} %collective-permute-done.3, bf16[1,2560,384]{2,1,0:T(8,128)(2,1)} %param.27, s32[]{:T(128)S(6)} %select_n.309), kind=kOutput, calls=%fused_computation.19 | convolution fusion | flops 11805696 | bytes 595972 | tf_op jit(solution)/shard_map/dot_general | solution.py:138
  73.3 1.2 %convolution_add_fusion.1 = f32[24,384]{1,0:T(8,128)S(1)} fusion(f32[24,384]{1,0:T(8,128)S(1)} %fusion.11, bf16[24,640]{1,0:T(8,128)(2,1)S(1)} %collective-permute-done.3, bf16[1,2560,384]{2,1,0:T(8,128)(2,1)} %param.28, s32[]{:T(128)S(6)} %select_n.309), kind=kOutput, calls=%fused_computation.16 | convolution fusion | flops 11805696 | bytes 595972 | tf_op jit(solution)/shard_map/dot_general | solution.py:141
  74.6 1.8 %fusion.13 = f32[24,384]{1,0:T(8,128)} fusion(bf16[24,640]{1,0:T(8,128)(2,1)S(1)} %collective-permute-done.5, bf16[1,2560,384]{2,1,0:T(8,128)(2,1)} %param.27, s32[]{:T(128)S(6)} %select_n.313), kind=kOutput, calls=%fused_computation.30 | convolution fusion | flops 11796480 | bytes 559108 | tf_op jit(solution)/shard_map/dot_general | solution.py:138
  77.4 2.3 %convolution_multiply_fusion.1 = f32[24,2560]{1,0:T(8,128)S(1)} fusion(bf16[1,384,2560]{2,1,0:T(8,128)(2,1)} %param.29, f32[24]{0:T(128)} %compare_select_fusion.8, f32[24,384]{1,0:T(8,128)} %fusion.2, f32[24,384]{1,0:T(8,128)} %fusion.13, f32[24,384]{1,0:T(8,128)} %convolution_add_fusion.3, bf16[24,640]{1,0:T(8,128)(2,1)S(1)} %collective-permute-done.4, ...), kind=kOutput, calls=%fused_computation.12 | convolution fusion | flops 59117568 | bytes 2845188 | tf_op jit(solution)/shard_map/dot_general | solution.py:145
  80.7 1.4 %collective-permute-start.7 = (f32[24,640]{1,0:T(8,128)S(1)}, f32[24,640]{1,0:T(8,128)S(1)}, u32[]{:S(2)}, u32[]{:S(2)}) collective-permute-start(f32[24,640]{1,0:T(8,128)S(1)} %get-tuple-element.17), channel_id=1, source_target_pairs={{0,2},{1,3},{2,0},{3,1},{4,6},{5,7},{6,4},{7,5},{8,10},{9,11},{10,... | collective-permute-start | bytes 184328 | tf_op jit(solution)/shard_map/ppermute | solution.py:149
  82.2 2.0 %collective-permute-start.8 = (f32[24,640]{1,0:T(8,128)S(1)}, f32[24,640]{1,0:T(8,128)S(1)}, u32[]{:S(2)}, u32[]{:S(2)}) collective-permute-start(f32[24,640]{1,0:T(8,128)S(1)} %get-tuple-element.18), channel_id=1, source_target_pairs={{0,3},{1,0},{2,1},{3,2},{4,7},{5,4},{6,5},{7,6},{8,11},{9,8},{10,9... | collective-permute-start | bytes 184328 | tf_op jit(solution)/shard_map/ppermute | solution.py:149
  86.7 1.3 %gather_fusion.6 = f32[64,640]{1,0:T(8,128)} fusion(f32[25,640]{1,0:T(8,128)S(1)} %concatenate.18, s32[1024]{0:T(1024)S(1)} %pad_clamp_fusion.1), kind=kCustom, calls=%fused_computation.6 | custom fusion | bytes 327936 | tf_op jit(solution)/shard_map/gather | solution.py:168
  89.5 20.5 %all_to_all.19 = f32[64,1,1280]{2,1,0:T(1,128)} all-to-all(f32[64,1,1280]{2,1,0:T(1,128)S(1)} %copy.46), channel_id=1, replica_groups=mesh['req'=64,'kv'=4] {'req'}, dimensions={0} | all-to-all | bytes 655360 | tf_op jit(solution)/shard_map/all_to_all | solution.py:172
  109.9 1.2 %reduce_sum.53 = bf16[1280]{0:T(1024)(128)(2,1)S(1)} reduce(f32[64,1,1280]{2,1,0:T(1,128)} %all_to_all.19, f32[]{:T(128)} %constant.212.clone.1), dimensions={0,1}, to_apply=%region_11.12 | reduce | flops 80640 | bytes 330244 | tf_op jit(solution)/shard_map/reduce_sum | solution.py:172
  (108 shorter events, 23.7 us)
Async XLA Ops:
  0.0 37.6 %copy-start = (bf16[640,2560]{1,0:T(8,128)(2,1)S(1)}, bf16[640,2560]{1,0:T(8,128)(2,1)}, u32[]{:S(2)}) copy-start(bf16[640,2560]{1,0:T(8,128)(2,1)} %param.23) | copy-start | bytes 9830404
  0.0 17.6 %copy-start.12 = (s32[128]{0:T(128)S(1)}, s32[128]{0:T(128)}, u32[]{:S(2)}) copy-start(s32[128]{0:T(128)} %param.22) | copy-start | bytes 1540
  0.0 17.7 %copy-start.5 = (s32[128,6]{0,1:T(8,128)S(1)}, s32[128,6]{0,1:T(8,128)}, u32[]{:S(2)}) copy-start(s32[128,6]{0,1:T(8,128)} %param.25) | copy-start | bytes 9220
  0.0 19.2 %copy-start.1 = (s32[128]{0:T(128)S(1)}, s32[128]{0:T(128)}, u32[]{:S(2)}) copy-start(s32[128]{0:T(128)} %param.21) | copy-start | bytes 1540
  0.0 24.7 %copy-start.6 = (f32[128,6]{0,1:T(8,128)S(1)}, f32[128,6]{0,1:T(8,128)}, u32[]{:S(2)}) copy-start(f32[128,6]{0,1:T(8,128)} %param.26) | copy-start | bytes 9220
  4.4 28.2 %all-to-all-start = ((bf16[64,2,1536]{2,1,0:T(2,128)(2,1)}), bf16[64,2,1536]{2,1,0:T(2,128)(2,1)}, u32[]{:S(2)}, u32[]{:S(2)}) async-start(bf16[64,2,1536]{2,1,0:T(2,128)(2,1)} %pad_maximum_fusion), calls=%async_computation | async-start | bytes 786432 | tf_op jit(solution)/shard_map/all_to_all | solution.py:52
  34.3 2.8 %copy-start.2 = (bf16[2,4096,128]{2,1,0:T(8,128)(2,1)S(1)}, bf16[2,4096,128]{2,1,0:T(8,128)(2,1)}, u32[]{:S(2)}) copy-start(bf16[2,4096,128]{2,1,0:T(8,128)(2,1)} %param.20) | copy-start | bytes 6291460
  37.6 6.1 %copy-start.7 = (bf16[640]{0:T(1024)(128)(2,1)S(1)}, bf16[640]{0:T(1024)(128)(2,1)}, u32[]{:S(2)}) copy-start(bf16[640]{0:T(1024)(128)(2,1)} %param.24) | copy-start | bytes 3844
  38.1 5.7 %collective-permute-start = (f32[2,2560]{1,0:T(2,128)S(1)}, f32[2,2560]{1,0:T(2,128)S(1)}, u32[]{:S(2)}, u32[]{:S(2)}) collective-permute-start(f32[2,2560]{1,0:T(2,128)S(1)} %add_dynamic-update-slice_fusion), channel_id=1, source_target_pairs={{0,1},{1,2},{2,3},{3,0},{4,5},{5,6},{6,7},{7,4},{8,9},{9,10},{10,1... | collective-permute-start | bytes 61448 | tf_op jit(solution)/shard_map/ppermute | solution.py:94
  39.5 4.4 %collective-permute-start.1 = (f32[2,2560]{1,0:T(2,128)S(1)}, f32[2,2560]{1,0:T(2,128)S(1)}, u32[]{:S(2)}, u32[]{:S(2)}) collective-permute-start(f32[2,2560]{1,0:T(2,128)S(1)} %add_dynamic-update-slice_fusion), channel_id=1, source_target_pairs={{0,2},{1,3},{2,0},{3,1},{4,6},{5,7},{6,4},{7,5},{8,10},{9,11},{10,... | collective-permute-start | bytes 61448 | tf_op jit(solution)/shard_map/ppermute | solution.py:94
  42.1 2.8 %collective-permute-start.2 = (f32[2,2560]{1,0:T(2,128)S(1)}, f32[2,2560]{1,0:T(2,128)S(1)}, u32[]{:S(2)}, u32[]{:S(2)}) collective-permute-start(f32[2,2560]{1,0:T(2,128)S(1)} %add_dynamic-update-slice_fusion), channel_id=1, source_target_pairs={{0,3},{1,0},{2,1},{3,2},{4,7},{5,4},{6,5},{7,6},{8,11},{9,8},{10,9... | collective-permute-start | bytes 61448 | tf_op jit(solution)/shard_map/ppermute | solution.py:94
  45.1 1.0 copy-start.4
  46.0 18.6 %all-to-all-start.1 = ((bf16[64,2,640]{2,1,0:T(2,128)(2,1)}), bf16[64,2,640]{2,1,0:T(2,128)(2,1)S(1)}, u32[]{:S(2)}, u32[]{:S(2)}) async-start(bf16[64,2,640]{2,1,0:T(2,128)(2,1)} %broadcast_select_fusion.4), calls=%async_computation.1 | async-start | bytes 327680 | tf_op jit(solution)/shard_map/all_to_all | solution.py:114
  65.5 10.9 %copy-start.3 = (bf16[1,2560,384]{2,1,0:T(8,128)(2,1)S(1)}, bf16[1,2560,384]{2,1,0:T(8,128)(2,1)}, u32[]{:S(2)}) copy-start(bf16[1,2560,384]{2,1,0:T(8,128)(2,1)} %param.28) | copy-start | bytes 5898244
  65.5 6.0 %collective-permute-start.3 = (bf16[24,640]{1,0:T(8,128)(2,1)S(1)}, bf16[24,640]{1,0:T(8,128)(2,1)S(1)}, u32[]{:S(2)}, u32[]{:S(2)}) collective-permute-start(bf16[24,640]{1,0:T(8,128)(2,1)S(1)} %gather_fusion.4), channel_id=1, source_target_pairs={{0,1},{1,2},{2,3},{3,0},{4,5},{5,6},{6,7},{7,4},{8,9},{9,10},{10,1... | collective-permute-start | bytes 92168 | tf_op jit(solution)/shard_map/ppermute | solution.py:127
  65.6 9.0 %collective-permute-start.5 = (bf16[24,640]{1,0:T(8,128)(2,1)S(1)}, bf16[24,640]{1,0:T(8,128)(2,1)S(1)}, u32[]{:S(2)}, u32[]{:S(2)}) collective-permute-start(bf16[24,640]{1,0:T(8,128)(2,1)S(1)} %gather_fusion.4), channel_id=1, source_target_pairs={{0,3},{1,0},{2,1},{3,2},{4,7},{5,4},{6,5},{7,6},{8,11},{9,8},{10,9... | collective-permute-start | bytes 92168 | tf_op jit(solution)/shard_map/ppermute | solution.py:127
  68.2 8.4 %collective-permute-start.4 = (bf16[24,640]{1,0:T(8,128)(2,1)S(1)}, bf16[24,640]{1,0:T(8,128)(2,1)S(1)}, u32[]{:S(2)}, u32[]{:S(2)}) collective-permute-start(bf16[24,640]{1,0:T(8,128)(2,1)S(1)} %gather_fusion.4), channel_id=1, source_target_pairs={{0,2},{1,3},{2,0},{3,1},{4,6},{5,7},{6,4},{7,5},{8,10},{9,11},{10,... | collective-permute-start | bytes 92168 | tf_op jit(solution)/shard_map/ppermute | solution.py:127
  79.7 8.3 %copy-start.8 = (pred[64]{0:T(512)(128)(4,1)S(1)}, pred[64]{0:T(512)(128)(4,1)}, u32[]{:S(2)}) copy-start(pred[64]{0:T(512)(128)(4,1)} %get-tuple-element.32) | copy-start | bytes 196
  79.7 8.3 %copy-start.9 = (pred[64]{0:T(512)(128)(4,1)S(1)}, pred[64]{0:T(512)(128)(4,1)}, u32[]{:S(2)}) copy-start(pred[64]{0:T(512)(128)(4,1)} %get-tuple-element.33) | copy-start | bytes 196
  79.8 8.3 %copy-start.10 = (pred[64]{0:T(512)(128)(4,1)S(1)}, pred[64]{0:T(512)(128)(4,1)}, u32[]{:S(2)}) copy-start(pred[64]{0:T(512)(128)(4,1)} %get-tuple-element.44) | copy-start | bytes 196
  79.8 8.3 %copy-start.11 = (pred[64]{0:T(512)(128)(4,1)S(1)}, pred[64]{0:T(512)(128)(4,1)}, u32[]{:S(2)}) copy-start(pred[64]{0:T(512)(128)(4,1)} %get-tuple-element.45) | copy-start | bytes 196
  79.8 5.8 %collective-permute-start.6 = (f32[24,640]{1,0:T(8,128)S(1)}, f32[24,640]{1,0:T(8,128)S(1)}, u32[]{:S(2)}, u32[]{:S(2)}) collective-permute-start(f32[24,640]{1,0:T(8,128)S(1)} %get-tuple-element.19), channel_id=1, source_target_pairs={{0,1},{1,2},{2,3},{3,0},{4,5},{5,6},{6,7},{7,4},{8,9},{9,10},{10,1... | collective-permute-start | bytes 184328 | tf_op jit(solution)/shard_map/ppermute | solution.py:149
  80.7 5.1 %collective-permute-start.7 = (f32[24,640]{1,0:T(8,128)S(1)}, f32[24,640]{1,0:T(8,128)S(1)}, u32[]{:S(2)}, u32[]{:S(2)}) collective-permute-start(f32[24,640]{1,0:T(8,128)S(1)} %get-tuple-element.17), channel_id=1, source_target_pairs={{0,2},{1,3},{2,0},{3,1},{4,6},{5,7},{6,4},{7,5},{8,10},{9,11},{10,... | collective-permute-start | bytes 184328 | tf_op jit(solution)/shard_map/ppermute | solution.py:149
  82.2 3.7 %collective-permute-start.8 = (f32[24,640]{1,0:T(8,128)S(1)}, f32[24,640]{1,0:T(8,128)S(1)}, u32[]{:S(2)}, u32[]{:S(2)}) collective-permute-start(f32[24,640]{1,0:T(8,128)S(1)} %get-tuple-element.18), channel_id=1, source_target_pairs={{0,3},{1,0},{2,1},{3,2},{4,7},{5,4},{6,5},{7,6},{8,11},{9,8},{10,9... | collective-permute-start | bytes 184328 | tf_op jit(solution)/shard_map/ppermute | solution.py:149

commit v10 on v9

--- a/solution.py
+++ b/solution.py
@@ -168,9 +168,10 @@
             weighted_ext[at_pick[j::per_dev]]
             + jnp.where((home_slot // per_dev == req_index)[:, None], own_row, 0.0)
         )
-    combined = jnp.concatenate(halves, axis=1)
-    totals_out = jnp.sum(lax.all_to_all(combined, "req", 0, 0, tiled=True), axis=0)
-    layer_rows = totals_out.reshape(per_dev, col_count)
+    combined = jnp.stack(halves, axis=1).astype(jnp.bfloat16)
+    layer_rows = jnp.sum(
+        lax.all_to_all(combined, "req", 0, 0, tiled=False).astype(jnp.float32), axis=0
+    )
     return layer_rows.astype(jnp.bfloat16)
 
 

time: 112 us -> 108 us (0.964)
  blocking collectives: 20.5 us -> 17.4 us
    all_to_all x1, blocking collectives: 20.5 us -> 17.4 us  [per_device(): lax.all_to_all(combined, 'req', 0, 0, tiled=False).astype(jnp.float32)]
  transfers between devices with their start and end apart: 11 -> 11, of which waited for: 4 -> 4; matrix products, arithmetic and copies ran while one was open for 18% -> 19% of each run, Pallas kernels for 0% -> 0%
where the time goes in v10:
time: 108 us; the launch traced here: 107 us
  starting transfers between devices  33 us (31%)
  blocking collectives  17.4 us (16%)
  waiting for transfers between devices  17.1 us (16%)
  matrix products  14.1 us (13%)
  local copies, waits for them, and re-layouts  12.9 us (12%)
  other arithmetic  12.3 us (11%)
    all_to_all x1, blocking collectives, per_device(): lax.all_to_all(combined, 'req', 0, 0, tiled=False).astype(jnp.float32)  17.4 us
    all_to_all x1, starting transfers between devices, per_device(): from_homes = lax.all_to_all(to_slots, 'req', 0, 0, tiled=False)  13.1 us
    all_to_all x1, waiting for transfers between devices, per_device(): by_slot = lax.all_to_all(to_experts, 'req', 0, 0, tiled=False)  10.5 us
    all_to_all x1, starting transfers between devices, per_device(): by_slot = lax.all_to_all(to_experts, 'req', 0, 0, tiled=False)  6.98 us
    all_to_all x1, waiting for transfers between devices, per_device(): from_homes = lax.all_to_all(to_slots, 'req', 0, 0, tiled=False)  5.37 us
    ppermute x3, starting transfers between devices, per_device(): lax.ppermute(summed_in, 'kv', [(i, (i + shift) % kv_count) for i in range...  5.05 us
    ppermute x3, starting transfers between devices, per_device(): lax.ppermute(lax.dynamic_slice_in_dim(weighted, (kv_index + shift) % kv_c...  4.33 us
    dot_general x2, matrix products, per_device(): jnp.dot(peer_rows, block_rows(gate_proj[0], source), preferred_element_ty...  3.68 us
  transfers between devices with their start and end apart: 11, of which 4 were waited for; matrix products, arithmetic and copies ran while one was open for 19% of the time, Pallas kernels for 0%

profile of v10, /device:TPU:1, one launch (start us, length us, event | category | flops | bytes accessed | tf_op | source)
XLA Modules:
  0.0 107.5 jit_solution(6396963455583087144)
XLA Ops:
  3.3 1.1 %pad_maximum_fusion = bf16[64,2,1536]{2,1,0:T(2,128)(2,1)} fusion(bf16[64,2,640]{2,1,0:T(2,128)(2,1)S(1)} %get-tuple-element.23, bf16[64,2,128]{2,1,0:T(2,128)(2,1)S(1)} %get-tuple-element.25, bf16[64,2,128]{2,1,0:T(2,128)(2,1)S(1)} %get-tuple-element.24, bf16[64,2,640]{2,1,0:T(2,128)(2,1)S(1)} %get-tuple-element.22), kind=kLoop, calls=%fused_computation.44 | loop fusion | flops 1572864 | bytes 786432 | tf_op jit(solution)/shard_map/concatenate | solution.py:51
  4.4 13.1 %all-to-all-start = ((bf16[64,2,1536]{2,1,0:T(2,128)(2,1)}), bf16[64,2,1536]{2,1,0:T(2,128)(2,1)}, u32[]{:S(2)}, u32[]{:S(2)}) async-start(bf16[64,2,1536]{2,1,0:T(2,128)(2,1)} %pad_maximum_fusion), calls=%async_computation | async-start | bytes 786432 | tf_op jit(solution)/shard_map/all_to_all | solution.py:52
  20.5 1.4 %scatter_custom_fusion.1 = s32[24]{0:T(128)S(1)} fusion(s32[128]{0:T(128)S(1)} %get-tuple-element.6, s32[128]{0:T(128)S(1)} %broadcast.608, s32[]{:T(128)} %constant.203.clone.1), kind=kCustom, calls=%fused_computation.182 | custom fusion | flops 128 | bytes 100 | tf_op jit(solution)/shard_map/scatter-add | solution.py:121
  25.5 1.2 %compare_select_fusion.8 = f32[24]{0:T(128)} fusion(f32[24]{0:T(128)S(1)} %gather_fusion.5, s32[]{:T(128)} %get-tuple-element.37), kind=kLoop, calls=%fused_computation.147 | loop fusion | flops 48 | bytes 196 | tf_op jit(solution)/shard_map/jit(_where)/select_n | solution.py:146
  27.3 5.4 %all-to-all-done = bf16[64,2,1536]{2,1,0:T(2,128)(2,1)} async-done(((bf16[64,2,1536]{2,1,0:T(2,128)(2,1)}), bf16[64,2,1536]{2,1,0:T(2,128)(2,1)}, u32[]{:S(2)}, u32[]{:S(2)}) %all-to-all-start) | async-done | bytes 393248 | tf_op jit(solution)/shard_map/all_to_all | solution.py:52
  32.7 1.6 %gather_fusion.2 = bf16[2,1536]{1,0:T(2,128)(2,1)S(1)} fusion(bf16[64,2,1536]{2,1,0:T(2,128)(2,1)} %all-to-all-done, s32[2]{0:T(128)S(1)} %fusion.78), kind=kCustom, calls=%fused_computation.2 | custom fusion | bytes 12304 | tf_op jit(solution)/shard_map/gather | solution.py:54
  34.4 2.4 %fusion.89 = (f32[2,5]{1,0:T(2,128)S(1)}, f32[2,5,4096]{2,1,0:T(8,128)S(1)}) fusion(bf16[2,5,128]{2,1,0:T(8,128)(2,1)S(1)} %reshape.492, bf16[2,4096,128]{2,1,0:T(8,128)(2,1)} %param.19, pred[2,4096]{1,0:T(4,128)(4,1)S(1)} %iota_compare_fusion), kind=kOutput, calls=%fused_computation.190 | convolution fusion | flops 10608630 | bytes 2271784 | tf_op jit(solution)/shard_map/rqd,rld->rql/dot_general | solution.py:63
  38.1 1.4 %collective-permute-start = (f32[2,2560]{1,0:T(2,128)S(1)}, f32[2,2560]{1,0:T(2,128)S(1)}, u32[]{:S(2)}, u32[]{:S(2)}) collective-permute-start(f32[2,2560]{1,0:T(2,128)S(1)} %add_dynamic-update-slice_fusion), channel_id=1, source_target_pairs={{0,1},{1,2},{2,3},{3,0},{4,5},{5,6},{6,7},{7,4},{8,9},{9,10},{10,1... | collective-permute-start | bytes 61448 | tf_op jit(solution)/shard_map/ppermute | solution.py:94
  39.5 2.6 %collective-permute-start.1 = (f32[2,2560]{1,0:T(2,128)S(1)}, f32[2,2560]{1,0:T(2,128)S(1)}, u32[]{:S(2)}, u32[]{:S(2)}) collective-permute-start(f32[2,2560]{1,0:T(2,128)S(1)} %add_dynamic-update-slice_fusion), channel_id=1, source_target_pairs={{0,2},{1,3},{2,0},{3,1},{4,6},{5,7},{6,4},{7,5},{8,10},{9,11},{10,... | collective-permute-start | bytes 61448 | tf_op jit(solution)/shard_map/ppermute | solution.py:94
  42.1 1.1 collective-permute-start.2
  43.9 1.1 collective-permute-done.2
  46.0 7.0 %all-to-all-start.1 = ((bf16[64,2,640]{2,1,0:T(2,128)(2,1)}), bf16[64,2,640]{2,1,0:T(2,128)(2,1)S(1)}, u32[]{:S(2)}, u32[]{:S(2)}) async-start(bf16[64,2,640]{2,1,0:T(2,128)(2,1)} %broadcast_select_fusion.4), calls=%async_computation.1 | async-start | bytes 327680 | tf_op jit(solution)/shard_map/all_to_all | solution.py:114
  54.2 10.5 %all-to-all-done.1 = bf16[64,2,640]{2,1,0:T(2,128)(2,1)S(1)} async-done(((bf16[64,2,640]{2,1,0:T(2,128)(2,1)}), bf16[64,2,640]{2,1,0:T(2,128)(2,1)S(1)}, u32[]{:S(2)}, u32[]{:S(2)}) %all-to-all-start.1) | async-done | bytes 163872 | tf_op jit(solution)/shard_map/all_to_all | solution.py:114
  65.6 2.7 %collective-permute-start.5 = (bf16[24,640]{1,0:T(8,128)(2,1)S(1)}, bf16[24,640]{1,0:T(8,128)(2,1)S(1)}, u32[]{:S(2)}, u32[]{:S(2)}) collective-permute-start(bf16[24,640]{1,0:T(8,128)(2,1)S(1)} %gather_fusion.4), channel_id=1, source_target_pairs={{0,3},{1,0},{2,1},{3,2},{4,7},{5,4},{6,5},{7,6},{8,11},{9,8},{10,9... | collective-permute-start | bytes 92168 | tf_op jit(solution)/shard_map/ppermute | solution.py:127
  69.0 1.2 %fusion.17 = f32[24,384]{1,0:T(8,128)S(1)} fusion(bf16[24,640]{1,0:T(8,128)(2,1)S(1)} %gather_fusion.4, bf16[1,2560,384]{2,1,0:T(8,128)(2,1)} %param.27, s32[]{:T(128)S(6)} %select_n.324), kind=kOutput, calls=%fused_computation.34 | convolution fusion | flops 11796480 | bytes 559108 | tf_op jit(solution)/shard_map/dot_general | solution.py:134
  70.3 1.2 %fusion.11 = f32[24,384]{1,0:T(8,128)S(1)} fusion(bf16[24,640]{1,0:T(8,128)(2,1)S(1)} %gather_fusion.4, bf16[1,2560,384]{2,1,0:T(8,128)(2,1)} %param.28, s32[]{:T(128)S(6)} %select_n.324), kind=kOutput, calls=%fused_computation.28 | convolution fusion | flops 11796480 | bytes 559108 | tf_op jit(solution)/shard_map/dot_general | solution.py:135
  71.5 1.8 %convolution_add_fusion.3 = f32[24,384]{1,0:T(8,128)} fusion(f32[24,384]{1,0:T(8,128)S(1)} %fusion.17, bf16[24,640]{1,0:T(8,128)(2,1)S(1)} %collective-permute-done.3, bf16[1,2560,384]{2,1,0:T(8,128)(2,1)} %param.27, s32[]{:T(128)S(6)} %select_n.337), kind=kOutput, calls=%fused_computation.19 | convolution fusion | flops 11805696 | bytes 595972 | tf_op jit(solution)/shard_map/dot_general | solution.py:138
  73.3 1.2 %convolution_add_fusion.1 = f32[24,384]{1,0:T(8,128)S(1)} fusion(f32[24,384]{1,0:T(8,128)S(1)} %fusion.11, bf16[24,640]{1,0:T(8,128)(2,1)S(1)} %collective-permute-done.3, bf16[1,2560,384]{2,1,0:T(8,128)(2,1)} %param.28, s32[]{:T(128)S(6)} %select_n.337), kind=kOutput, calls=%fused_computation.16 | convolution fusion | flops 11805696 | bytes 595972 | tf_op jit(solution)/shard_map/dot_general | solution.py:141
  74.6 1.8 %fusion.13 = f32[24,384]{1,0:T(8,128)} fusion(bf16[24,640]{1,0:T(8,128)(2,1)S(1)} %collective-permute-done.5, bf16[1,2560,384]{2,1,0:T(8,128)(2,1)} %param.27, s32[]{:T(128)S(6)} %select_n.341), kind=kOutput, calls=%fused_computation.30 | convolution fusion | flops 11796480 | bytes 559108 | tf_op jit(solution)/shard_map/dot_general | solution.py:138
  77.4 2.3 %convolution_multiply_fusion.1 = f32[24,2560]{1,0:T(8,128)S(1)} fusion(bf16[1,384,2560]{2,1,0:T(8,128)(2,1)} %param.29, f32[24]{0:T(128)} %compare_select_fusion.8, f32[24,384]{1,0:T(8,128)} %fusion.2, f32[24,384]{1,0:T(8,128)} %fusion.13, f32[24,384]{1,0:T(8,128)} %convolution_add_fusion.3, bf16[24,640]{1,0:T(8,128)(2,1)S(1)} %collective-permute-done.4, ...), kind=kOutput, calls=%fused_computation.12 | convolution fusion | flops 59117568 | bytes 2845188 | tf_op jit(solution)/shard_map/dot_general | solution.py:145
  80.7 1.4 %collective-permute-start.7 = (f32[24,640]{1,0:T(8,128)S(1)}, f32[24,640]{1,0:T(8,128)S(1)}, u32[]{:S(2)}, u32[]{:S(2)}) collective-permute-start(f32[24,640]{1,0:T(8,128)S(1)} %get-tuple-element.17), channel_id=1, source_target_pairs={{0,2},{1,3},{2,0},{3,1},{4,6},{5,7},{6,4},{7,5},{8,10},{9,11},{10,... | collective-permute-start | bytes 184328 | tf_op jit(solution)/shard_map/ppermute | solution.py:149
  82.2 2.0 %collective-permute-start.8 = (f32[24,640]{1,0:T(8,128)S(1)}, f32[24,640]{1,0:T(8,128)S(1)}, u32[]{:S(2)}, u32[]{:S(2)}) collective-permute-start(f32[24,640]{1,0:T(8,128)S(1)} %get-tuple-element.18), channel_id=1, source_target_pairs={{0,3},{1,0},{2,1},{3,2},{4,7},{5,4},{6,5},{7,6},{8,11},{9,8},{10,9... | collective-permute-start | bytes 184328 | tf_op jit(solution)/shard_map/ppermute | solution.py:149
  86.7 1.3 %gather_fusion.6 = f32[64,640]{1,0:T(8,128)} fusion(f32[25,640]{1,0:T(8,128)S(1)} %concatenate.15, s32[1024]{0:T(1024)S(1)} %pad_clamp_fusion.1), kind=kCustom, calls=%fused_computation.6 | custom fusion | bytes 327936 | tf_op jit(solution)/shard_map/gather | solution.py:168
  89.3 17.4 %all_to_all.15 = bf16[64,2,640]{2,1,0:T(2,128)(2,1)S(1)} all-to-all(bf16[64,2,640]{2,1,0:T(2,128)(2,1)S(1)} %copy.46), channel_id=1, replica_groups=mesh['req'=64,'kv'=4] {'req'}, dimensions={0} | all-to-all | bytes 327680 | tf_op jit(solution)/shard_map/all_to_all | solution.py:173
  (107 shorter events, 22.6 us)
Async XLA Ops:
  0.0 37.6 %copy-start = (bf16[640,2560]{1,0:T(8,128)(2,1)S(1)}, bf16[640,2560]{1,0:T(8,128)(2,1)}, u32[]{:S(2)}) copy-start(bf16[640,2560]{1,0:T(8,128)(2,1)} %param.23) | copy-start | bytes 9830404
  0.0 17.6 %copy-start.12 = (s32[128]{0:T(128)S(1)}, s32[128]{0:T(128)}, u32[]{:S(2)}) copy-start(s32[128]{0:T(128)} %param.22) | copy-start | bytes 1540
  0.0 17.7 %copy-start.5 = (s32[128,6]{0,1:T(8,128)S(1)}, s32[128,6]{0,1:T(8,128)}, u32[]{:S(2)}) copy-start(s32[128,6]{0,1:T(8,128)} %param.25) | copy-start | bytes 9220
  0.0 19.2 %copy-start.1 = (s32[128]{0:T(128)S(1)}, s32[128]{0:T(128)}, u32[]{:S(2)}) copy-start(s32[128]{0:T(128)} %param.21) | copy-start | bytes 1540
  0.0 24.7 %copy-start.6 = (f32[128,6]{0,1:T(8,128)S(1)}, f32[128,6]{0,1:T(8,128)}, u32[]{:S(2)}) copy-start(f32[128,6]{0,1:T(8,128)} %param.26) | copy-start | bytes 9220
  4.4 28.2 %all-to-all-start = ((bf16[64,2,1536]{2,1,0:T(2,128)(2,1)}), bf16[64,2,1536]{2,1,0:T(2,128)(2,1)}, u32[]{:S(2)}, u32[]{:S(2)}) async-start(bf16[64,2,1536]{2,1,0:T(2,128)(2,1)} %pad_maximum_fusion), calls=%async_computation | async-start | bytes 786432 | tf_op jit(solution)/shard_map/all_to_all | solution.py:52
  34.3 2.8 %copy-start.2 = (bf16[2,4096,128]{2,1,0:T(8,128)(2,1)S(1)}, bf16[2,4096,128]{2,1,0:T(8,128)(2,1)}, u32[]{:S(2)}) copy-start(bf16[2,4096,128]{2,1,0:T(8,128)(2,1)} %param.20) | copy-start | bytes 6291460
  37.6 6.1 %copy-start.7 = (bf16[640]{0:T(1024)(128)(2,1)S(1)}, bf16[640]{0:T(1024)(128)(2,1)}, u32[]{:S(2)}) copy-start(bf16[640]{0:T(1024)(128)(2,1)} %param.24) | copy-start | bytes 3844
  38.1 5.7 %collective-permute-start = (f32[2,2560]{1,0:T(2,128)S(1)}, f32[2,2560]{1,0:T(2,128)S(1)}, u32[]{:S(2)}, u32[]{:S(2)}) collective-permute-start(f32[2,2560]{1,0:T(2,128)S(1)} %add_dynamic-update-slice_fusion), channel_id=1, source_target_pairs={{0,1},{1,2},{2,3},{3,0},{4,5},{5,6},{6,7},{7,4},{8,9},{9,10},{10,1... | collective-permute-start | bytes 61448 | tf_op jit(solution)/shard_map/ppermute | solution.py:94
  39.5 4.4 %collective-permute-start.1 = (f32[2,2560]{1,0:T(2,128)S(1)}, f32[2,2560]{1,0:T(2,128)S(1)}, u32[]{:S(2)}, u32[]{:S(2)}) collective-permute-start(f32[2,2560]{1,0:T(2,128)S(1)} %add_dynamic-update-slice_fusion), channel_id=1, source_target_pairs={{0,2},{1,3},{2,0},{3,1},{4,6},{5,7},{6,4},{7,5},{8,10},{9,11},{10,... | collective-permute-start | bytes 61448 | tf_op jit(solution)/shard_map/ppermute | solution.py:94
  42.1 2.8 %collective-permute-start.2 = (f32[2,2560]{1,0:T(2,128)S(1)}, f32[2,2560]{1,0:T(2,128)S(1)}, u32[]{:S(2)}, u32[]{:S(2)}) collective-permute-start(f32[2,2560]{1,0:T(2,128)S(1)} %add_dynamic-update-slice_fusion), channel_id=1, source_target_pairs={{0,3},{1,0},{2,1},{3,2},{4,7},{5,4},{6,5},{7,6},{8,11},{9,8},{10,9... | collective-permute-start | bytes 61448 | tf_op jit(solution)/shard_map/ppermute | solution.py:94
  45.1 1.0 copy-start.4
  46.0 18.6 %all-to-all-start.1 = ((bf16[64,2,640]{2,1,0:T(2,128)(2,1)}), bf16[64,2,640]{2,1,0:T(2,128)(2,1)S(1)}, u32[]{:S(2)}, u32[]{:S(2)}) async-start(bf16[64,2,640]{2,1,0:T(2,128)(2,1)} %broadcast_select_fusion.4), calls=%async_computation.1 | async-start | bytes 327680 | tf_op jit(solution)/shard_map/all_to_all | solution.py:114
  65.5 10.9 %copy-start.3 = (bf16[1,2560,384]{2,1,0:T(8,128)(2,1)S(1)}, bf16[1,2560,384]{2,1,0:T(8,128)(2,1)}, u32[]{:S(2)}) copy-start(bf16[1,2560,384]{2,1,0:T(8,128)(2,1)} %param.28) | copy-start | bytes 5898244
  65.5 6.0 %collective-permute-start.3 = (bf16[24,640]{1,0:T(8,128)(2,1)S(1)}, bf16[24,640]{1,0:T(8,128)(2,1)S(1)}, u32[]{:S(2)}, u32[]{:S(2)}) collective-permute-start(bf16[24,640]{1,0:T(8,128)(2,1)S(1)} %gather_fusion.4), channel_id=1, source_target_pairs={{0,1},{1,2},{2,3},{3,0},{4,5},{5,6},{6,7},{7,4},{8,9},{9,10},{10,1... | collective-permute-start | bytes 92168 | tf_op jit(solution)/shard_map/ppermute | solution.py:127
  65.6 9.0 %collective-permute-start.5 = (bf16[24,640]{1,0:T(8,128)(2,1)S(1)}, bf16[24,640]{1,0:T(8,128)(2,1)S(1)}, u32[]{:S(2)}, u32[]{:S(2)}) collective-permute-start(bf16[24,640]{1,0:T(8,128)(2,1)S(1)} %gather_fusion.4), channel_id=1, source_target_pairs={{0,3},{1,0},{2,1},{3,2},{4,7},{5,4},{6,5},{7,6},{8,11},{9,8},{10,9... | collective-permute-start | bytes 92168 | tf_op jit(solution)/shard_map/ppermute | solution.py:127
  68.2 8.4 %collective-permute-start.4 = (bf16[24,640]{1,0:T(8,128)(2,1)S(1)}, bf16[24,640]{1,0:T(8,128)(2,1)S(1)}, u32[]{:S(2)}, u32[]{:S(2)}) collective-permute-start(bf16[24,640]{1,0:T(8,128)(2,1)S(1)} %gather_fusion.4), channel_id=1, source_target_pairs={{0,2},{1,3},{2,0},{3,1},{4,6},{5,7},{6,4},{7,5},{8,10},{9,11},{10,... | collective-permute-start | bytes 92168 | tf_op jit(solution)/shard_map/ppermute | solution.py:127
  79.7 8.3 %copy-start.8 = (pred[64]{0:T(512)(128)(4,1)S(1)}, pred[64]{0:T(512)(128)(4,1)}, u32[]{:S(2)}) copy-start(pred[64]{0:T(512)(128)(4,1)} %get-tuple-element.32) | copy-start | bytes 196
  79.7 8.3 %copy-start.9 = (pred[64]{0:T(512)(128)(4,1)S(1)}, pred[64]{0:T(512)(128)(4,1)}, u32[]{:S(2)}) copy-start(pred[64]{0:T(512)(128)(4,1)} %get-tuple-element.33) | copy-start | bytes 196
  79.8 8.3 %copy-start.10 = (pred[64]{0:T(512)(128)(4,1)S(1)}, pred[64]{0:T(512)(128)(4,1)}, u32[]{:S(2)}) copy-start(pred[64]{0:T(512)(128)(4,1)} %get-tuple-element.44) | copy-start | bytes 196
  79.8 8.3 %copy-start.11 = (pred[64]{0:T(512)(128)(4,1)S(1)}, pred[64]{0:T(512)(128)(4,1)}, u32[]{:S(2)}) copy-start(pred[64]{0:T(512)(128)(4,1)} %get-tuple-element.45) | copy-start | bytes 196
  79.8 5.8 %collective-permute-start.6 = (f32[24,640]{1,0:T(8,128)S(1)}, f32[24,640]{1,0:T(8,128)S(1)}, u32[]{:S(2)}, u32[]{:S(2)}) collective-permute-start(f32[24,640]{1,0:T(8,128)S(1)} %get-tuple-element.19), channel_id=1, source_target_pairs={{0,1},{1,2},{2,3},{3,0},{4,5},{5,6},{6,7},{7,4},{8,9},{9,10},{10,1... | collective-permute-start | bytes 184328 | tf_op jit(solution)/shard_map/ppermute | solution.py:149
  80.7 5.1 %collective-permute-start.7 = (f32[24,640]{1,0:T(8,128)S(1)}, f32[24,640]{1,0:T(8,128)S(1)}, u32[]{:S(2)}, u32[]{:S(2)}) collective-permute-start(f32[24,640]{1,0:T(8,128)S(1)} %get-tuple-element.17), channel_id=1, source_target_pairs={{0,2},{1,3},{2,0},{3,1},{4,6},{5,7},{6,4},{7,5},{8,10},{9,11},{10,... | collective-permute-start | bytes 184328 | tf_op jit(solution)/shard_map/ppermute | solution.py:149
  82.2 3.7 %collective-permute-start.8 = (f32[24,640]{1,0:T(8,128)S(1)}, f32[24,640]{1,0:T(8,128)S(1)}, u32[]{:S(2)}, u32[]{:S(2)}) collective-permute-start(f32[24,640]{1,0:T(8,128)S(1)} %get-tuple-element.18), channel_id=1, source_target_pairs={{0,3},{1,0},{2,1},{3,2},{4,7},{5,4},{6,5},{7,6},{8,11},{9,8},{10,9... | collective-permute-start | bytes 184328 | tf_op jit(solution)/shard_map/ppermute | solution.py:149

commit v11 on v8

--- a/solution.py
+++ b/solution.py
@@ -123,13 +123,10 @@
     projected = jnp.dot(attended, out_proj, preferred_element_type=jnp.float32)
 
     col_start = kv_index * col_count
-    own_cols = jnp.concatenate(
-        [residual_rows.astype(jnp.float32), norm_gain.astype(jnp.float32)[None, :]], axis=0
-    )
-    summed_in = jnp.concatenate(
-        [projected, jnp.zeros((1, model_width), jnp.float32)], axis=0
-    ) + lax.dynamic_update_slice(
-        jnp.zeros((per_dev + 1, model_width), jnp.float32), own_cols, (0, col_start)
+    summed_in = projected + lax.dynamic_update_slice(
+        jnp.zeros((per_dev, model_width), jnp.float32),
+        residual_rows.astype(jnp.float32),
+        (0, col_start),
     )
     parts = [summed_in] + [
         lax.ppermute(summed_in, "kv", [(i, (i + shift) % kv_count) for i in range(kv_count)])
@@ -138,12 +135,14 @@
     summed = parts[0]
     for part in parts[1:]:
         summed = summed + part
-    hidden = summed[:per_dev]
-    gain = summed[per_dev]
+    hidden = summed
     squares = jnp.sum(hidden * hidden, axis=1)
-    normed = (hidden * lax.rsqrt(squares / model_width + 1e-06)[:, None] * gain).astype(
-        jnp.bfloat16
-    )
+    own_hidden = lax.dynamic_slice_in_dim(hidden, col_start, col_count, axis=1)
+    normed = (
+        own_hidden
+        * lax.rsqrt(squares / model_width + 1e-06)[:, None]
+        * norm_gain.astype(jnp.float32)[None, :]
+    ).astype(jnp.bfloat16)
     local_count = gate_proj.shape[0]
     served_ids = expert_ids[served] // local_count
     wanted = jnp.any(
@@ -161,8 +160,22 @@
     valid_rows = jnp.arange(capacity) < jnp.sum(uses_expert.astype(jnp.int32))
     picked_slots = slot_of[picked]
     row_block = by_slot[picked_slots // per_dev, picked_slots % per_dev]
+    kv_shifts = range(1, kv_count)
+    from_peers = [
+        lax.ppermute(row_block, "kv", [(i, (i + shift) % kv_count) for i in range(kv_count)])
+        for shift in kv_shifts
+    ]
+
+    candidates = [row_block] + from_peers
+    in_order = []
+    for block in range(kv_count):
+        chosen = candidates[0]
+        for shift in kv_shifts:
+            chosen = jnp.where((kv_index - shift) % kv_count == block, candidates[shift], chosen)
+        in_order.append(chosen)
+    full_rows = jnp.concatenate(in_order, axis=1)
     row_gate = jnp.where(valid_rows, token_gate[picked], 0.0)
-    weighted = expert_ffn(row_block, gate_proj[0], up_proj[0], down_proj[0], row_gate[:, None])
+    weighted = expert_ffn(full_rows, gate_proj[0], up_proj[0], down_proj[0], row_gate[:, None])
 
     weighted = lax.dynamic_slice_in_dim(weighted, col_start, col_count, axis=1) + sum(
         lax.ppermute(
@@ -175,7 +188,6 @@
         for shift in range(1, kv_count)
     )
 
-    own_hidden = lax.dynamic_slice_in_dim(hidden, col_start, col_count, axis=1)
     at_pick = jnp.where(uses_expert, jnp.cumsum(uses_expert.astype(jnp.int32)) - 1, capacity)
     weighted_ext = jnp.concatenate([weighted, jnp.zeros((1, col_count), jnp.float32)], axis=0)
     halves = []
@@ -188,9 +200,10 @@
             weighted_ext[at_pick[j::per_dev]]
             + jnp.where((home_slot // per_dev == req_index)[:, None], own_row, 0.0)
         )
-    combined = jnp.concatenate(halves, axis=1)
-    totals_out = jnp.sum(lax.all_to_all(combined, "req", 0, 0, tiled=True), axis=0)
-    layer_rows = totals_out.reshape(per_dev, col_count)
+    combined = jnp.stack(halves, axis=1).astype(jnp.bfloat16)
+    layer_rows = jnp.sum(
+        lax.all_to_all(combined, "req", 0, 0, tiled=False).astype(jnp.float32), axis=0
+    )
     return layer_rows.astype(jnp.bfloat16)
 
 

time: 118 us -> 108 us (0.915)
  waiting for transfers between devices: 31.2 us -> 24.2 us
  starting transfers between devices: 28.9 us -> 31.8 us
  local copies, waits for them, and re-layouts: 15.6 us -> 12.9 us
  blocking collectives: 20.8 us -> 18.4 us
    all_to_all x1, waiting for transfers between devices: 12.4 us -> 8.32 us  [per_device(): from_homes = lax.all_to_all(to_slots, 'req', 0, 0, tiled=False)]
    ppermute x0 -> x3, waiting for transfers between devices: none -> 3.6 us  [per_device(): lax.ppermute(row_block, 'kv', [(i, (i + shift) % kv_count) for i in range...]
    all_to_all x1, waiting for transfers between devices: 13.6 us -> 10.3 us  [per_device(): by_slot = lax.all_to_all(to_experts, 'req', 0, 0, tiled=False)]
    ppermute x0 -> x3, starting transfers between devices: none -> 3.03 us  [per_device(): lax.ppermute(row_block, 'kv', [(i, (i + shift) % kv_count) for i in range...]
    all_to_all x1, blocking collectives: 20.8 us -> 18.4 us  [per_device(): lax.all_to_all(combined, 'req', 0, 0, tiled=False).astype(jnp.float32)]
    ppermute x3, waiting for transfers between devices: 3.76 us -> 1.92 us  [per_device(): lax.ppermute(lax.dynamic_slice_in_dim(weighted, (kv_index + shift) % kv_c...]
    gather x1, local copies, waits for them, and re-layouts: 2.61 us -> 0.81 us  [per_device(): row_block = by_slot[picked_slots // per_dev, picked_slots % per_dev]]
    ppermute x3, waiting for transfers between devices: 1.4 us -> 0.03 us  [per_device(): lax.ppermute(summed_in, 'kv', [(i, (i + shift) % kv_count) for i in range...]
  transfers between devices with their start and end apart: 8 -> 11, of which waited for: 7 -> 6; matrix products, arithmetic and copies ran while one was open for 8% -> 9% of each run, Pallas kernels for 0% -> 0%
where the time goes in v11:
time: 108 us
  starting transfers between devices  31.8 us (29%)
  waiting for transfers between devices  24.2 us (22%)
  blocking collectives  18.4 us (17%)
  local copies, waits for them, and re-layouts  12.9 us (12%)
  other arithmetic  11.5 us (11%)
  Pallas kernels  4.99 us (5%)
  matrix products  3.53 us (3%)
    all_to_all x1, blocking collectives, per_device(): lax.all_to_all(combined, 'req', 0, 0, tiled=False).astype(jnp.float32)  18.4 us
    all_to_all x1, starting transfers between devices, per_device(): from_homes = lax.all_to_all(to_slots, 'req', 0, 0, tiled=False)  13.1 us
    all_to_all x1, waiting for transfers between devices, per_device(): by_slot = lax.all_to_all(to_experts, 'req', 0, 0, tiled=False)  10.3 us
    all_to_all x1, waiting for transfers between devices, per_device(): from_homes = lax.all_to_all(to_slots, 'req', 0, 0, tiled=False)  8.32 us
    all_to_all x1, starting transfers between devices, per_device(): by_slot = lax.all_to_all(to_experts, 'req', 0, 0, tiled=False)  6.98 us
    ppermute x3, starting transfers between devices, per_device(): lax.ppermute(summed_in, 'kv', [(i, (i + shift) % kv_count) for i in range...  5.05 us
    pallas_call x1, Pallas kernels, expert_ffn(): pl.pallas_call(_ffn_body, grid=(hidden // block,), in_specs=[pl.BlockSpec...  4.99 us
    ppermute x3, waiting for transfers between devices, per_device(): lax.ppermute(row_block, 'kv', [(i, (i + shift) % kv_count) for i in range...  3.6 us
  transfers between devices with their start and end apart: 11, of which 6 were waited for; matrix products, arithmetic and copies ran while one was open for 9% of the time, Pallas kernels for 0%

profile of v11, /device:TPU:1, one launch (start us, length us, event | category | flops | bytes accessed | tf_op | source)
XLA Modules:
  0.0 107.6 jit_solution(8585111875721437054)
XLA Ops:
  0.0 0.9 reshape.490
  3.3 1.1 %pad_maximum_fusion = bf16[64,2,1536]{2,1,0:T(2,128)(2,1)} fusion(bf16[64,2,640]{2,1,0:T(2,128)(2,1)S(1)} %get-tuple-element.27, bf16[64,2,128]{2,1,0:T(2,128)(2,1)S(1)} %get-tuple-element.29, bf16[64,2,128]{2,1,0:T(2,128)(2,1)S(1)} %get-tuple-element.28, bf16[64,2,640]{2,1,0:T(2,128)(2,1)S(1)} %get-tuple-element.26), kind=kLoop, calls=%fused_computation.16 | loop fusion | flops 1572864 | bytes 786432 | tf_op jit(solution)/shard_map/concatenate | solution.py:89
  4.4 13.1 %all-to-all-start = ((bf16[64,2,1536]{2,1,0:T(2,128)(2,1)}), bf16[64,2,1536]{2,1,0:T(2,128)(2,1)}, u32[]{:S(2)}, u32[]{:S(2)}) async-start(bf16[64,2,1536]{2,1,0:T(2,128)(2,1)} %pad_maximum_fusion), calls=%async_computation | async-start | bytes 786432 | tf_op jit(solution)/shard_map/all_to_all | solution.py:90
  19.3 1.0 scatter_custom_fusion
  21.9 1.4 %scatter_custom_fusion.1 = s32[24]{0:T(128)S(1)} fusion(s32[128]{0:T(128)S(1)} %get-tuple-element.6, s32[128]{0:T(128)S(1)} %broadcast.612, s32[]{:T(128)} %constant.210.clone.1), kind=kCustom, calls=%fused_computation.149 | custom fusion | flops 128 | bytes 100 | tf_op jit(solution)/shard_map/scatter-add | solution.py:159
  24.3 8.3 %all-to-all-done = bf16[64,2,1536]{2,1,0:T(2,128)(2,1)} async-done(((bf16[64,2,1536]{2,1,0:T(2,128)(2,1)}), bf16[64,2,1536]{2,1,0:T(2,128)(2,1)}, u32[]{:S(2)}, u32[]{:S(2)}) %all-to-all-start) | async-done | bytes 393248 | tf_op jit(solution)/shard_map/all_to_all | solution.py:90
  32.7 1.6 %gather_fusion.2 = bf16[2,1536]{1,0:T(2,128)(2,1)S(1)} fusion(bf16[64,2,1536]{2,1,0:T(2,128)(2,1)} %all-to-all-done, s32[2]{0:T(128)S(1)} %fusion.41), kind=kCustom, calls=%fused_computation.2 | custom fusion | bytes 12304 | tf_op jit(solution)/shard_map/gather | solution.py:92
  34.4 2.4 %fusion.50 = (f32[2,5]{1,0:T(2,128)S(1)}, f32[2,5,4096]{2,1,0:T(8,128)S(1)}) fusion(bf16[2,5,128]{2,1,0:T(8,128)(2,1)S(1)} %reshape.491, bf16[2,4096,128]{2,1,0:T(8,128)(2,1)} %param.19, pred[2,4096]{1,0:T(4,128)(4,1)S(1)} %iota_compare_fusion), kind=kOutput, calls=%fused_computation.155 | convolution fusion | flops 10608630 | bytes 2271784 | tf_op jit(solution)/shard_map/rqd,rld->rql/dot_general | solution.py:101
  38.1 1.4 %collective-permute-start = (f32[2,2560]{1,0:T(2,128)S(1)}, f32[2,2560]{1,0:T(2,128)S(1)}, u32[]{:S(2)}, u32[]{:S(2)}) collective-permute-start(f32[2,2560]{1,0:T(2,128)S(1)} %add_dynamic-update-slice_fusion), channel_id=1, source_target_pairs={{0,1},{1,2},{2,3},{3,0},{4,5},{5,6},{6,7},{7,4},{8,9},{9,10},{10,1... | collective-permute-start | bytes 61448 | tf_op jit(solution)/shard_map/ppermute | solution.py:132
  39.5 2.6 %collective-permute-start.1 = (f32[2,2560]{1,0:T(2,128)S(1)}, f32[2,2560]{1,0:T(2,128)S(1)}, u32[]{:S(2)}, u32[]{:S(2)}) collective-permute-start(f32[2,2560]{1,0:T(2,128)S(1)} %add_dynamic-update-slice_fusion), channel_id=1, source_target_pairs={{0,2},{1,3},{2,0},{3,1},{4,6},{5,7},{6,4},{7,5},{8,10},{9,11},{10,... | collective-permute-start | bytes 61448 | tf_op jit(solution)/shard_map/ppermute | solution.py:132
  42.1 1.1 collective-permute-start.2
  46.0 7.0 %all-to-all-start.1 = ((bf16[64,2,640]{2,1,0:T(2,128)(2,1)}), bf16[64,2,640]{2,1,0:T(2,128)(2,1)S(1)}, u32[]{:S(2)}, u32[]{:S(2)}) async-start(bf16[64,2,640]{2,1,0:T(2,128)(2,1)} %broadcast_select_fusion.4), calls=%async_computation.1 | async-start | bytes 327680 | tf_op jit(solution)/shard_map/all_to_all | solution.py:152
  53.1 1.2 %fusion.28.gate_ref = f32[24,1]{1,0:T(8,128)} fusion(f32[24,1]{1,0:T(8,128)S(1)} %copy.49, s32[]{:T(128)} %get-tuple-element.41), kind=kLoop, calls=%fused_computation.84 | loop fusion | flops 48 | bytes 196 | tf_op jit(solution)/shard_map/jit(_where)/select_n | solution.py:177
  54.4 10.3 %all-to-all-done.1 = bf16[64,2,640]{2,1,0:T(2,128)(2,1)S(1)} async-done(((bf16[64,2,640]{2,1,0:T(2,128)(2,1)}), bf16[64,2,640]{2,1,0:T(2,128)(2,1)S(1)}, u32[]{:S(2)}, u32[]{:S(2)}) %all-to-all-start.1) | async-done | bytes 163872 | tf_op jit(solution)/shard_map/all_to_all | solution.py:152
  65.5 2.4 %collective-permute-start.3 = (bf16[24,640]{1,0:T(8,128)(2,1)S(1)}, bf16[24,640]{1,0:T(8,128)(2,1)S(1)}, u32[]{:S(2)}, u32[]{:S(2)}) collective-permute-start(bf16[24,640]{1,0:T(8,128)(2,1)S(1)} %gather_fusion.4), channel_id=1, source_target_pairs={{0,3},{1,0},{2,1},{3,2},{4,7},{5,4},{6,5},{7,6},{8,11},{9,8},{10,9... | collective-permute-start | bytes 92168 | tf_op jit(solution)/shard_map/ppermute | solution.py:165
  68.8 3.3 %collective-permute-done.4 = bf16[24,640]{1,0:T(8,128)(2,1)S(1)} collective-permute-done((bf16[24,640]{1,0:T(8,128)(2,1)S(1)}, bf16[24,640]{1,0:T(8,128)(2,1)S(1)}, u32[]{:S(2)}, u32[]{:S(2)}) %collective-permute-start.4) | collective-permute-done | bytes 30752 | tf_op jit(solution)/shard_map/ppermute | solution.py:165
  72.8 5.0 %shard_map.145 = f32[24,2560]{1,0:T(8,128)} custom-call(bf16[24,2560]{1,0:T(8,128)(2,1)} %pad_maximum_fusion.2.x_ref, bf16[2560,384]{1,0:T(8,128)(2,1)} %bitcast.46, bf16[2560,384]{1,0:T(8,128)(2,1)} %bitcast.47, bf16[384,2560]{1,0:T(8,128)(2,1)} %bitcast.48, f32[24,1]{1,0:T(8,128)} %fusion.28.gate_ref), custom_call_target="tpu_custom_call" | custom-call | tf_op jit(solution)/shard_map/pallas_call | solution.py:31
  77.8 0.9 constant_dynamic-slice_fusion.1
  78.8 2.0 %collective-permute-start.7 = (f32[24,640]{1,0:T(8,128)S(1)}, f32[24,640]{1,0:T(8,128)S(1)}, u32[]{:S(2)}, u32[]{:S(2)}) collective-permute-start(f32[24,640]{1,0:T(8,128)S(1)} %get-tuple-element.17), channel_id=1, source_target_pairs={{0,2},{1,3},{2,0},{3,1},{4,6},{5,7},{6,4},{7,5},{8,10},{9,11},{10,... | collective-permute-start | bytes 184328 | tf_op jit(solution)/shard_map/ppermute | solution.py:181
  80.8 1.4 %collective-permute-start.8 = (f32[24,640]{1,0:T(8,128)S(1)}, f32[24,640]{1,0:T(8,128)S(1)}, u32[]{:S(2)}, u32[]{:S(2)}) collective-permute-start(f32[24,640]{1,0:T(8,128)S(1)} %get-tuple-element.18), channel_id=1, source_target_pairs={{0,3},{1,0},{2,1},{3,2},{4,7},{5,4},{6,5},{7,6},{8,11},{9,8},{10,9... | collective-permute-start | bytes 184328 | tf_op jit(solution)/shard_map/ppermute | solution.py:181
  82.4 1.3 %collective-permute-done.6 = f32[24,640]{1,0:T(8,128)S(1)} collective-permute-done((f32[24,640]{1,0:T(8,128)S(1)}, f32[24,640]{1,0:T(8,128)S(1)}, u32[]{:S(2)}, u32[]{:S(2)}) %collective-permute-start.6) | collective-permute-done | bytes 61472 | tf_op jit(solution)/shard_map/ppermute | solution.py:181
  85.9 1.3 %gather_fusion.6 = f32[64,640]{1,0:T(8,128)} fusion(f32[25,640]{1,0:T(8,128)S(1)} %concatenate.19, s32[1024]{0:T(1024)S(1)} %pad_clamp_fusion.1), kind=kCustom, calls=%fused_computation.6 | custom fusion | bytes 327936 | tf_op jit(solution)/shard_map/gather | solution.py:200
  87.2 1.0 fusion.7
  88.4 18.4 %all_to_all.15 = bf16[64,2,640]{2,1,0:T(2,128)(2,1)S(1)} all-to-all(bf16[64,2,640]{2,1,0:T(2,128)(2,1)S(1)} %copy.50), channel_id=1, replica_groups=mesh['req'=64,'kv'=4] {'req'}, dimensions={0} | all-to-all | bytes 327680 | tf_op jit(solution)/shard_map/all_to_all | solution.py:205
  (91 shorter events, 16.7 us)
Async XLA Ops:
  0.0 37.6 %copy-start = (bf16[640,2560]{1,0:T(8,128)(2,1)S(1)}, bf16[640,2560]{1,0:T(8,128)(2,1)}, u32[]{:S(2)}) copy-start(bf16[640,2560]{1,0:T(8,128)(2,1)} %param.23) | copy-start | bytes 9830404
  0.0 17.6 %copy-start.6 = (s32[128]{0:T(128)S(1)}, s32[128]{0:T(128)}, u32[]{:S(2)}) copy-start(s32[128]{0:T(128)} %param.22) | copy-start | bytes 1540
  0.0 17.7 %copy-start.3 = (s32[128,6]{0,1:T(8,128)S(1)}, s32[128,6]{0,1:T(8,128)}, u32[]{:S(2)}) copy-start(s32[128,6]{0,1:T(8,128)} %param.25) | copy-start | bytes 9220
  0.0 17.9 %copy-start.4 = (f32[128,6]{0,1:T(8,128)S(1)}, f32[128,6]{0,1:T(8,128)}, u32[]{:S(2)}) copy-start(f32[128,6]{0,1:T(8,128)} %param.26) | copy-start | bytes 9220
  0.0 20.6 %copy-start.1 = (s32[128]{0:T(128)S(1)}, s32[128]{0:T(128)}, u32[]{:S(2)}) copy-start(s32[128]{0:T(128)} %param.21) | copy-start | bytes 1540
  4.4 28.2 %all-to-all-start = ((bf16[64,2,1536]{2,1,0:T(2,128)(2,1)}), bf16[64,2,1536]{2,1,0:T(2,128)(2,1)}, u32[]{:S(2)}, u32[]{:S(2)}) async-start(bf16[64,2,1536]{2,1,0:T(2,128)(2,1)} %pad_maximum_fusion), calls=%async_computation | async-start | bytes 786432 | tf_op jit(solution)/shard_map/all_to_all | solution.py:90
  34.3 2.8 %copy-start.2 = (bf16[2,4096,128]{2,1,0:T(8,128)(2,1)S(1)}, bf16[2,4096,128]{2,1,0:T(8,128)(2,1)}, u32[]{:S(2)}) copy-start(bf16[2,4096,128]{2,1,0:T(8,128)(2,1)} %param.20) | copy-start | bytes 6291460
  37.6 5.6 %copy-start.5 = (bf16[640]{0:T(1024)(128)(2,1)S(1)}, bf16[640]{0:T(1024)(128)(2,1)}, u32[]{:S(2)}) copy-start(bf16[640]{0:T(1024)(128)(2,1)} %param.24) | copy-start | bytes 3844
  38.1 6.8 %collective-permute-start = (f32[2,2560]{1,0:T(2,128)S(1)}, f32[2,2560]{1,0:T(2,128)S(1)}, u32[]{:S(2)}, u32[]{:S(2)}) collective-permute-start(f32[2,2560]{1,0:T(2,128)S(1)} %add_dynamic-update-slice_fusion), channel_id=1, source_target_pairs={{0,1},{1,2},{2,3},{3,0},{4,5},{5,6},{6,7},{7,4},{8,9},{9,10},{10,1... | collective-permute-start | bytes 61448 | tf_op jit(solution)/shard_map/ppermute | solution.py:132
  39.5 5.4 %collective-permute-start.1 = (f32[2,2560]{1,0:T(2,128)S(1)}, f32[2,2560]{1,0:T(2,128)S(1)}, u32[]{:S(2)}, u32[]{:S(2)}) collective-permute-start(f32[2,2560]{1,0:T(2,128)S(1)} %add_dynamic-update-slice_fusion), channel_id=1, source_target_pairs={{0,2},{1,3},{2,0},{3,1},{4,6},{5,7},{6,4},{7,5},{8,10},{9,11},{10,... | collective-permute-start | bytes 61448 | tf_op jit(solution)/shard_map/ppermute | solution.py:132
  42.1 2.8 %collective-permute-start.2 = (f32[2,2560]{1,0:T(2,128)S(1)}, f32[2,2560]{1,0:T(2,128)S(1)}, u32[]{:S(2)}, u32[]{:S(2)}) collective-permute-start(f32[2,2560]{1,0:T(2,128)S(1)} %add_dynamic-update-slice_fusion), channel_id=1, source_target_pairs={{0,3},{1,0},{2,1},{3,2},{4,7},{5,4},{6,5},{7,6},{8,11},{9,8},{10,9... | collective-permute-start | bytes 61448 | tf_op jit(solution)/shard_map/ppermute | solution.py:132
  46.0 18.6 %all-to-all-start.1 = ((bf16[64,2,640]{2,1,0:T(2,128)(2,1)}), bf16[64,2,640]{2,1,0:T(2,128)(2,1)S(1)}, u32[]{:S(2)}, u32[]{:S(2)}) async-start(bf16[64,2,640]{2,1,0:T(2,128)(2,1)} %broadcast_select_fusion.4), calls=%async_computation.1 | async-start | bytes 327680 | tf_op jit(solution)/shard_map/all_to_all | solution.py:152
  65.5 3.4 %collective-permute-start.3 = (bf16[24,640]{1,0:T(8,128)(2,1)S(1)}, bf16[24,640]{1,0:T(8,128)(2,1)S(1)}, u32[]{:S(2)}, u32[]{:S(2)}) collective-permute-start(bf16[24,640]{1,0:T(8,128)(2,1)S(1)} %gather_fusion.4), channel_id=1, source_target_pairs={{0,3},{1,0},{2,1},{3,2},{4,7},{5,4},{6,5},{7,6},{8,11},{9,8},{10,9... | collective-permute-start | bytes 92168 | tf_op jit(solution)/shard_map/ppermute | solution.py:165
  67.8 4.3 %collective-permute-start.4 = (bf16[24,640]{1,0:T(8,128)(2,1)S(1)}, bf16[24,640]{1,0:T(8,128)(2,1)S(1)}, u32[]{:S(2)}, u32[]{:S(2)}) collective-permute-start(bf16[24,640]{1,0:T(8,128)(2,1)S(1)} %gather_fusion.4), channel_id=1, source_target_pairs={{0,2},{1,3},{2,0},{3,1},{4,6},{5,7},{6,4},{7,5},{8,10},{9,11},{10,... | collective-permute-start | bytes 92168 | tf_op jit(solution)/shard_map/ppermute | solution.py:165
  67.8 4.3 %collective-permute-start.5 = (bf16[24,640]{1,0:T(8,128)(2,1)S(1)}, bf16[24,640]{1,0:T(8,128)(2,1)S(1)}, u32[]{:S(2)}, u32[]{:S(2)}) collective-permute-start(bf16[24,640]{1,0:T(8,128)(2,1)S(1)} %gather_fusion.4), channel_id=1, source_target_pairs={{0,1},{1,2},{2,3},{3,0},{4,5},{5,6},{6,7},{7,4},{8,9},{9,10},{10,1... | collective-permute-start | bytes 92168 | tf_op jit(solution)/shard_map/ppermute | solution.py:165
  78.7 5.0 %collective-permute-start.6 = (f32[24,640]{1,0:T(8,128)S(1)}, f32[24,640]{1,0:T(8,128)S(1)}, u32[]{:S(2)}, u32[]{:S(2)}) collective-permute-start(f32[24,640]{1,0:T(8,128)S(1)} %get-tuple-element.19), channel_id=1, source_target_pairs={{0,1},{1,2},{2,3},{3,0},{4,5},{5,6},{6,7},{7,4},{8,9},{9,10},{10,1... | collective-permute-start | bytes 184328 | tf_op jit(solution)/shard_map/ppermute | solution.py:181
  78.8 4.9 %collective-permute-start.7 = (f32[24,640]{1,0:T(8,128)S(1)}, f32[24,640]{1,0:T(8,128)S(1)}, u32[]{:S(2)}, u32[]{:S(2)}) collective-permute-start(f32[24,640]{1,0:T(8,128)S(1)} %get-tuple-element.17), channel_id=1, source_target_pairs={{0,2},{1,3},{2,0},{3,1},{4,6},{5,7},{6,4},{7,5},{8,10},{9,11},{10,... | collective-permute-start | bytes 184328 | tf_op jit(solution)/shard_map/ppermute | solution.py:181
  80.8 3.5 %collective-permute-start.8 = (f32[24,640]{1,0:T(8,128)S(1)}, f32[24,640]{1,0:T(8,128)S(1)}, u32[]{:S(2)}, u32[]{:S(2)}) collective-permute-start(f32[24,640]{1,0:T(8,128)S(1)} %get-tuple-element.18), channel_id=1, source_target_pairs={{0,3},{1,0},{2,1},{3,2},{4,7},{5,4},{6,5},{7,6},{8,11},{9,8},{10,9... | collective-permute-start | bytes 184328 | tf_op jit(solution)/shard_map/ppermute | solution.py:181

commit v12 on v10

--- a/solution.py
+++ b/solution.py
@@ -105,6 +105,13 @@
         * lax.rsqrt(squares / model_width + 1e-06)[:, None]
         * norm_gain.astype(jnp.float32)[None, :]
     ).astype(jnp.bfloat16)
+    hidden_part = []
+    for j in range(per_dev):
+        home_slot = slot_of[j::per_dev]
+        own_row = own_hidden[0][None, :]
+        for i in range(1, per_dev):
+            own_row = jnp.where((home_slot % per_dev == i)[:, None], own_hidden[i][None, :], own_row)
+        hidden_part.append(jnp.where((home_slot // per_dev == req_index)[:, None], own_row, 0.0))
     local_count = gate_proj.shape[0]
     served_ids = expert_ids[served] // local_count
     wanted = jnp.any(
@@ -158,16 +165,9 @@
 
     at_pick = jnp.where(uses_expert, jnp.cumsum(uses_expert.astype(jnp.int32)) - 1, capacity)
     weighted_ext = jnp.concatenate([weighted, jnp.zeros((1, col_count), jnp.float32)], axis=0)
-    halves = []
-    for j in range(per_dev):
-        home_slot = slot_of[j::per_dev]
-        own_row = own_hidden[0][None, :]
-        for i in range(1, per_dev):
-            own_row = jnp.where((home_slot % per_dev == i)[:, None], own_hidden[i][None, :], own_row)
-        halves.append(
-            weighted_ext[at_pick[j::per_dev]]
-            + jnp.where((home_slot // per_dev == req_index)[:, None], own_row, 0.0)
-        )
+    halves = [
+        weighted_ext[at_pick[j::per_dev]] + hidden_part[j] for j in range(per_dev)
+    ]
     combined = jnp.stack(halves, axis=1).astype(jnp.bfloat16)
     layer_rows = jnp.sum(
         lax.all_to_all(combined, "req", 0, 0, tiled=False).astype(jnp.float32), axis=0

time: 108 us -> 108 us (level)
  no operation moved by 1% of the time
where the time goes in v12:
time: 108 us; the launch traced here: 107 us
  starting transfers between devices  33 us (31%)
  blocking collectives  17.4 us (16%)
  waiting for transfers between devices  17.1 us (16%)
  matrix products  14.1 us (13%)
  local copies, waits for them, and re-layouts  12.9 us (12%)
  other arithmetic  12.3 us (11%)
    all_to_all x1, blocking collectives, per_device(): lax.all_to_all(combined, 'req', 0, 0, tiled=False).astype(jnp.float32)  17.4 us
    all_to_all x1, starting transfers between devices, per_device(): from_homes = lax.all_to_all(to_slots, 'req', 0, 0, tiled=False)  13.1 us
    all_to_all x1, waiting for transfers between devices, per_device(): by_slot = lax.all_to_all(to_experts, 'req', 0, 0, tiled=False)  10.5 us
    all_to_all x1, starting transfers between devices, per_device(): by_slot = lax.all_to_all(to_experts, 'req', 0, 0, tiled=False)  6.98 us
    all_to_all x1, waiting for transfers between devices, per_device(): from_homes = lax.all_to_all(to_slots, 'req', 0, 0, tiled=False)  5.37 us
    ppermute x3, starting transfers between devices, per_device(): lax.ppermute(summed_in, 'kv', [(i, (i + shift) % kv_count) for i in range...  5.05 us
    ppermute x3, starting transfers between devices, per_device(): lax.ppermute(lax.dynamic_slice_in_dim(weighted, (kv_index + shift) % kv_c...  4.33 us
    dot_general x2, matrix products, per_device(): jnp.dot(peer_rows, block_rows(gate_proj[0], source), preferred_element_ty...  3.68 us
  transfers between devices with their start and end apart: 11, of which 4 were waited for; matrix products, arithmetic and copies ran while one was open for 19% of the time, Pallas kernels for 0%

profile of v12, /device:TPU:1, one launch (start us, length us, event | category | flops | bytes accessed | tf_op | source)
XLA Modules:
  0.0 107.5 jit_solution(6396963455583087144)
XLA Ops:
  3.3 1.1 %pad_maximum_fusion = bf16[64,2,1536]{2,1,0:T(2,128)(2,1)} fusion(bf16[64,2,640]{2,1,0:T(2,128)(2,1)S(1)} %get-tuple-element.23, bf16[64,2,128]{2,1,0:T(2,128)(2,1)S(1)} %get-tuple-element.25, bf16[64,2,128]{2,1,0:T(2,128)(2,1)S(1)} %get-tuple-element.24, bf16[64,2,640]{2,1,0:T(2,128)(2,1)S(1)} %get-tuple-element.22), kind=kLoop, calls=%fused_computation.44 | loop fusion | flops 1572864 | bytes 786432 | tf_op jit(solution)/shard_map/concatenate | solution.py:51
  4.4 13.1 %all-to-all-start = ((bf16[64,2,1536]{2,1,0:T(2,128)(2,1)}), bf16[64,2,1536]{2,1,0:T(2,128)(2,1)}, u32[]{:S(2)}, u32[]{:S(2)}) async-start(bf16[64,2,1536]{2,1,0:T(2,128)(2,1)} %pad_maximum_fusion), calls=%async_computation | async-start | bytes 786432 | tf_op jit(solution)/shard_map/all_to_all | solution.py:52
  20.5 1.4 %scatter_custom_fusion.1 = s32[24]{0:T(128)S(1)} fusion(s32[128]{0:T(128)S(1)} %get-tuple-element.6, s32[128]{0:T(128)S(1)} %broadcast.608, s32[]{:T(128)} %constant.203.clone.1), kind=kCustom, calls=%fused_computation.182 | custom fusion | flops 128 | bytes 100 | tf_op jit(solution)/shard_map/scatter-add | solution.py:128
  25.5 1.2 %compare_select_fusion.8 = f32[24]{0:T(128)} fusion(f32[24]{0:T(128)S(1)} %gather_fusion.5, s32[]{:T(128)} %get-tuple-element.37), kind=kLoop, calls=%fused_computation.147 | loop fusion | flops 48 | bytes 196 | tf_op jit(solution)/shard_map/jit(_where)/select_n | solution.py:153
  27.3 5.4 %all-to-all-done = bf16[64,2,1536]{2,1,0:T(2,128)(2,1)} async-done(((bf16[64,2,1536]{2,1,0:T(2,128)(2,1)}), bf16[64,2,1536]{2,1,0:T(2,128)(2,1)}, u32[]{:S(2)}, u32[]{:S(2)}) %all-to-all-start) | async-done | bytes 393248 | tf_op jit(solution)/shard_map/all_to_all | solution.py:52
  32.7 1.6 %gather_fusion.2 = bf16[2,1536]{1,0:T(2,128)(2,1)S(1)} fusion(bf16[64,2,1536]{2,1,0:T(2,128)(2,1)} %all-to-all-done, s32[2]{0:T(128)S(1)} %fusion.78), kind=kCustom, calls=%fused_computation.2 | custom fusion | bytes 12304 | tf_op jit(solution)/shard_map/gather | solution.py:54
  34.4 2.4 %fusion.89 = (f32[2,5]{1,0:T(2,128)S(1)}, f32[2,5,4096]{2,1,0:T(8,128)S(1)}) fusion(bf16[2,5,128]{2,1,0:T(8,128)(2,1)S(1)} %reshape.492, bf16[2,4096,128]{2,1,0:T(8,128)(2,1)} %param.19, pred[2,4096]{1,0:T(4,128)(4,1)S(1)} %iota_compare_fusion), kind=kOutput, calls=%fused_computation.190 | convolution fusion | flops 10608630 | bytes 2271784 | tf_op jit(solution)/shard_map/rqd,rld->rql/dot_general | solution.py:63
  38.1 1.4 %collective-permute-start = (f32[2,2560]{1,0:T(2,128)S(1)}, f32[2,2560]{1,0:T(2,128)S(1)}, u32[]{:S(2)}, u32[]{:S(2)}) collective-permute-start(f32[2,2560]{1,0:T(2,128)S(1)} %add_dynamic-update-slice_fusion), channel_id=1, source_target_pairs={{0,1},{1,2},{2,3},{3,0},{4,5},{5,6},{6,7},{7,4},{8,9},{9,10},{10,1... | collective-permute-start | bytes 61448 | tf_op jit(solution)/shard_map/ppermute | solution.py:94
  39.5 2.6 %collective-permute-start.1 = (f32[2,2560]{1,0:T(2,128)S(1)}, f32[2,2560]{1,0:T(2,128)S(1)}, u32[]{:S(2)}, u32[]{:S(2)}) collective-permute-start(f32[2,2560]{1,0:T(2,128)S(1)} %add_dynamic-update-slice_fusion), channel_id=1, source_target_pairs={{0,2},{1,3},{2,0},{3,1},{4,6},{5,7},{6,4},{7,5},{8,10},{9,11},{10,... | collective-permute-start | bytes 61448 | tf_op jit(solution)/shard_map/ppermute | solution.py:94
  42.1 1.1 collective-permute-start.2
  43.9 1.1 collective-permute-done.2
  46.0 7.0 %all-to-all-start.1 = ((bf16[64,2,640]{2,1,0:T(2,128)(2,1)}), bf16[64,2,640]{2,1,0:T(2,128)(2,1)S(1)}, u32[]{:S(2)}, u32[]{:S(2)}) async-start(bf16[64,2,640]{2,1,0:T(2,128)(2,1)} %broadcast_select_fusion.4), calls=%async_computation.1 | async-start | bytes 327680 | tf_op jit(solution)/shard_map/all_to_all | solution.py:121
  54.2 10.5 %all-to-all-done.1 = bf16[64,2,640]{2,1,0:T(2,128)(2,1)S(1)} async-done(((bf16[64,2,640]{2,1,0:T(2,128)(2,1)}), bf16[64,2,640]{2,1,0:T(2,128)(2,1)S(1)}, u32[]{:S(2)}, u32[]{:S(2)}) %all-to-all-start.1) | async-done | bytes 163872 | tf_op jit(solution)/shard_map/all_to_all | solution.py:121
  65.6 2.7 %collective-permute-start.5 = (bf16[24,640]{1,0:T(8,128)(2,1)S(1)}, bf16[24,640]{1,0:T(8,128)(2,1)S(1)}, u32[]{:S(2)}, u32[]{:S(2)}) collective-permute-start(bf16[24,640]{1,0:T(8,128)(2,1)S(1)} %gather_fusion.4), channel_id=1, source_target_pairs={{0,3},{1,0},{2,1},{3,2},{4,7},{5,4},{6,5},{7,6},{8,11},{9,8},{10,9... | collective-permute-start | bytes 92168 | tf_op jit(solution)/shard_map/ppermute | solution.py:134
  69.0 1.2 %fusion.17 = f32[24,384]{1,0:T(8,128)S(1)} fusion(bf16[24,640]{1,0:T(8,128)(2,1)S(1)} %gather_fusion.4, bf16[1,2560,384]{2,1,0:T(8,128)(2,1)} %param.27, s32[]{:T(128)S(6)} %select_n.324), kind=kOutput, calls=%fused_computation.34 | convolution fusion | flops 11796480 | bytes 559108 | tf_op jit(solution)/shard_map/dot_general | solution.py:141
  70.3 1.2 %fusion.11 = f32[24,384]{1,0:T(8,128)S(1)} fusion(bf16[24,640]{1,0:T(8,128)(2,1)S(1)} %gather_fusion.4, bf16[1,2560,384]{2,1,0:T(8,128)(2,1)} %param.28, s32[]{:T(128)S(6)} %select_n.324), kind=kOutput, calls=%fused_computation.28 | convolution fusion | flops 11796480 | bytes 559108 | tf_op jit(solution)/shard_map/dot_general | solution.py:142
  71.5 1.8 %convolution_add_fusion.3 = f32[24,384]{1,0:T(8,128)} fusion(f32[24,384]{1,0:T(8,128)S(1)} %fusion.17, bf16[24,640]{1,0:T(8,128)(2,1)S(1)} %collective-permute-done.3, bf16[1,2560,384]{2,1,0:T(8,128)(2,1)} %param.27, s32[]{:T(128)S(6)} %select_n.337), kind=kOutput, calls=%fused_computation.19 | convolution fusion | flops 11805696 | bytes 595972 | tf_op jit(solution)/shard_map/dot_general | solution.py:145
  73.3 1.2 %convolution_add_fusion.1 = f32[24,384]{1,0:T(8,128)S(1)} fusion(f32[24,384]{1,0:T(8,128)S(1)} %fusion.11, bf16[24,640]{1,0:T(8,128)(2,1)S(1)} %collective-permute-done.3, bf16[1,2560,384]{2,1,0:T(8,128)(2,1)} %param.28, s32[]{:T(128)S(6)} %select_n.337), kind=kOutput, calls=%fused_computation.16 | convolution fusion | flops 11805696 | bytes 595972 | tf_op jit(solution)/shard_map/dot_general | solution.py:148
  74.6 1.8 %fusion.13 = f32[24,384]{1,0:T(8,128)} fusion(bf16[24,640]{1,0:T(8,128)(2,1)S(1)} %collective-permute-done.5, bf16[1,2560,384]{2,1,0:T(8,128)(2,1)} %param.27, s32[]{:T(128)S(6)} %select_n.341), kind=kOutput, calls=%fused_computation.30 | convolution fusion | flops 11796480 | bytes 559108 | tf_op jit(solution)/shard_map/dot_general | solution.py:145
  77.4 2.3 %convolution_multiply_fusion.1 = f32[24,2560]{1,0:T(8,128)S(1)} fusion(bf16[1,384,2560]{2,1,0:T(8,128)(2,1)} %param.29, f32[24]{0:T(128)} %compare_select_fusion.8, f32[24,384]{1,0:T(8,128)} %fusion.2, f32[24,384]{1,0:T(8,128)} %fusion.13, f32[24,384]{1,0:T(8,128)} %convolution_add_fusion.3, bf16[24,640]{1,0:T(8,128)(2,1)S(1)} %collective-permute-done.4, ...), kind=kOutput, calls=%fused_computation.12 | convolution fusion | flops 59117568 | bytes 2845188 | tf_op jit(solution)/shard_map/dot_general | solution.py:152
  80.7 1.4 %collective-permute-start.7 = (f32[24,640]{1,0:T(8,128)S(1)}, f32[24,640]{1,0:T(8,128)S(1)}, u32[]{:S(2)}, u32[]{:S(2)}) collective-permute-start(f32[24,640]{1,0:T(8,128)S(1)} %get-tuple-element.17), channel_id=1, source_target_pairs={{0,2},{1,3},{2,0},{3,1},{4,6},{5,7},{6,4},{7,5},{8,10},{9,11},{10,... | collective-permute-start | bytes 184328 | tf_op jit(solution)/shard_map/ppermute | solution.py:156
  82.2 2.0 %collective-permute-start.8 = (f32[24,640]{1,0:T(8,128)S(1)}, f32[24,640]{1,0:T(8,128)S(1)}, u32[]{:S(2)}, u32[]{:S(2)}) collective-permute-start(f32[24,640]{1,0:T(8,128)S(1)} %get-tuple-element.18), channel_id=1, source_target_pairs={{0,3},{1,0},{2,1},{3,2},{4,7},{5,4},{6,5},{7,6},{8,11},{9,8},{10,9... | collective-permute-start | bytes 184328 | tf_op jit(solution)/shard_map/ppermute | solution.py:156
  86.7 1.3 %gather_fusion.6 = f32[64,640]{1,0:T(8,128)} fusion(f32[25,640]{1,0:T(8,128)S(1)} %concatenate.15, s32[1024]{0:T(1024)S(1)} %pad_clamp_fusion.1), kind=kCustom, calls=%fused_computation.6 | custom fusion | bytes 327936 | tf_op jit(solution)/shard_map/gather | solution.py:169
  89.3 17.4 %all_to_all.15 = bf16[64,2,640]{2,1,0:T(2,128)(2,1)S(1)} all-to-all(bf16[64,2,640]{2,1,0:T(2,128)(2,1)S(1)} %copy.46), channel_id=1, replica_groups=mesh['req'=64,'kv'=4] {'req'}, dimensions={0} | all-to-all | bytes 327680 | tf_op jit(solution)/shard_map/all_to_all | solution.py:173
  (107 shorter events, 22.6 us)
Async XLA Ops:
  0.0 37.6 %copy-start = (bf16[640,2560]{1,0:T(8,128)(2,1)S(1)}, bf16[640,2560]{1,0:T(8,128)(2,1)}, u32[]{:S(2)}) copy-start(bf16[640,2560]{1,0:T(8,128)(2,1)} %param.23) | copy-start | bytes 9830404
  0.0 17.6 %copy-start.12 = (s32[128]{0:T(128)S(1)}, s32[128]{0:T(128)}, u32[]{:S(2)}) copy-start(s32[128]{0:T(128)} %param.22) | copy-start | bytes 1540
  0.0 17.7 %copy-start.5 = (s32[128,6]{0,1:T(8,128)S(1)}, s32[128,6]{0,1:T(8,128)}, u32[]{:S(2)}) copy-start(s32[128,6]{0,1:T(8,128)} %param.25) | copy-start | bytes 9220
  0.0 19.2 %copy-start.1 = (s32[128]{0:T(128)S(1)}, s32[128]{0:T(128)}, u32[]{:S(2)}) copy-start(s32[128]{0:T(128)} %param.21) | copy-start | bytes 1540
  0.0 24.7 %copy-start.6 = (f32[128,6]{0,1:T(8,128)S(1)}, f32[128,6]{0,1:T(8,128)}, u32[]{:S(2)}) copy-start(f32[128,6]{0,1:T(8,128)} %param.26) | copy-start | bytes 9220
  4.4 28.2 %all-to-all-start = ((bf16[64,2,1536]{2,1,0:T(2,128)(2,1)}), bf16[64,2,1536]{2,1,0:T(2,128)(2,1)}, u32[]{:S(2)}, u32[]{:S(2)}) async-start(bf16[64,2,1536]{2,1,0:T(2,128)(2,1)} %pad_maximum_fusion), calls=%async_computation | async-start | bytes 786432 | tf_op jit(solution)/shard_map/all_to_all | solution.py:52
  34.3 2.8 %copy-start.2 = (bf16[2,4096,128]{2,1,0:T(8,128)(2,1)S(1)}, bf16[2,4096,128]{2,1,0:T(8,128)(2,1)}, u32[]{:S(2)}) copy-start(bf16[2,4096,128]{2,1,0:T(8,128)(2,1)} %param.20) | copy-start | bytes 6291460
  37.6 6.1 %copy-start.7 = (bf16[640]{0:T(1024)(128)(2,1)S(1)}, bf16[640]{0:T(1024)(128)(2,1)}, u32[]{:S(2)}) copy-start(bf16[640]{0:T(1024)(128)(2,1)} %param.24) | copy-start | bytes 3844
  38.1 5.7 %collective-permute-start = (f32[2,2560]{1,0:T(2,128)S(1)}, f32[2,2560]{1,0:T(2,128)S(1)}, u32[]{:S(2)}, u32[]{:S(2)}) collective-permute-start(f32[2,2560]{1,0:T(2,128)S(1)} %add_dynamic-update-slice_fusion), channel_id=1, source_target_pairs={{0,1},{1,2},{2,3},{3,0},{4,5},{5,6},{6,7},{7,4},{8,9},{9,10},{10,1... | collective-permute-start | bytes 61448 | tf_op jit(solution)/shard_map/ppermute | solution.py:94
  39.5 4.4 %collective-permute-start.1 = (f32[2,2560]{1,0:T(2,128)S(1)}, f32[2,2560]{1,0:T(2,128)S(1)}, u32[]{:S(2)}, u32[]{:S(2)}) collective-permute-start(f32[2,2560]{1,0:T(2,128)S(1)} %add_dynamic-update-slice_fusion), channel_id=1, source_target_pairs={{0,2},{1,3},{2,0},{3,1},{4,6},{5,7},{6,4},{7,5},{8,10},{9,11},{10,... | collective-permute-start | bytes 61448 | tf_op jit(solution)/shard_map/ppermute | solution.py:94
  42.1 2.8 %collective-permute-start.2 = (f32[2,2560]{1,0:T(2,128)S(1)}, f32[2,2560]{1,0:T(2,128)S(1)}, u32[]{:S(2)}, u32[]{:S(2)}) collective-permute-start(f32[2,2560]{1,0:T(2,128)S(1)} %add_dynamic-update-slice_fusion), channel_id=1, source_target_pairs={{0,3},{1,0},{2,1},{3,2},{4,7},{5,4},{6,5},{7,6},{8,11},{9,8},{10,9... | collective-permute-start | bytes 61448 | tf_op jit(solution)/shard_map/ppermute | solution.py:94
  45.1 1.0 copy-start.4
  46.0 18.6 %all-to-all-start.1 = ((bf16[64,2,640]{2,1,0:T(2,128)(2,1)}), bf16[64,2,640]{2,1,0:T(2,128)(2,1)S(1)}, u32[]{:S(2)}, u32[]{:S(2)}) async-start(bf16[64,2,640]{2,1,0:T(2,128)(2,1)} %broadcast_select_fusion.4), calls=%async_computation.1 | async-start | bytes 327680 | tf_op jit(solution)/shard_map/all_to_all | solution.py:121
  65.5 10.9 %copy-start.3 = (bf16[1,2560,384]{2,1,0:T(8,128)(2,1)S(1)}, bf16[1,2560,384]{2,1,0:T(8,128)(2,1)}, u32[]{:S(2)}) copy-start(bf16[1,2560,384]{2,1,0:T(8,128)(2,1)} %param.28) | copy-start | bytes 5898244
  65.5 6.0 %collective-permute-start.3 = (bf16[24,640]{1,0:T(8,128)(2,1)S(1)}, bf16[24,640]{1,0:T(8,128)(2,1)S(1)}, u32[]{:S(2)}, u32[]{:S(2)}) collective-permute-start(bf16[24,640]{1,0:T(8,128)(2,1)S(1)} %gather_fusion.4), channel_id=1, source_target_pairs={{0,1},{1,2},{2,3},{3,0},{4,5},{5,6},{6,7},{7,4},{8,9},{9,10},{10,1... | collective-permute-start | bytes 92168 | tf_op jit(solution)/shard_map/ppermute | solution.py:134
  65.6 9.0 %collective-permute-start.5 = (bf16[24,640]{1,0:T(8,128)(2,1)S(1)}, bf16[24,640]{1,0:T(8,128)(2,1)S(1)}, u32[]{:S(2)}, u32[]{:S(2)}) collective-permute-start(bf16[24,640]{1,0:T(8,128)(2,1)S(1)} %gather_fusion.4), channel_id=1, source_target_pairs={{0,3},{1,0},{2,1},{3,2},{4,7},{5,4},{6,5},{7,6},{8,11},{9,8},{10,9... | collective-permute-start | bytes 92168 | tf_op jit(solution)/shard_map/ppermute | solution.py:134
  68.2 8.4 %collective-permute-start.4 = (bf16[24,640]{1,0:T(8,128)(2,1)S(1)}, bf16[24,640]{1,0:T(8,128)(2,1)S(1)}, u32[]{:S(2)}, u32[]{:S(2)}) collective-permute-start(bf16[24,640]{1,0:T(8,128)(2,1)S(1)} %gather_fusion.4), channel_id=1, source_target_pairs={{0,2},{1,3},{2,0},{3,1},{4,6},{5,7},{6,4},{7,5},{8,10},{9,11},{10,... | collective-permute-start | bytes 92168 | tf_op jit(solution)/shard_map/ppermute | solution.py:134
  79.7 8.3 %copy-start.8 = (pred[64]{0:T(512)(128)(4,1)S(1)}, pred[64]{0:T(512)(128)(4,1)}, u32[]{:S(2)}) copy-start(pred[64]{0:T(512)(128)(4,1)} %get-tuple-element.32) | copy-start | bytes 196
  79.7 8.3 %copy-start.9 = (pred[64]{0:T(512)(128)(4,1)S(1)}, pred[64]{0:T(512)(128)(4,1)}, u32[]{:S(2)}) copy-start(pred[64]{0:T(512)(128)(4,1)} %get-tuple-element.33) | copy-start | bytes 196
  79.8 8.3 %copy-start.10 = (pred[64]{0:T(512)(128)(4,1)S(1)}, pred[64]{0:T(512)(128)(4,1)}, u32[]{:S(2)}) copy-start(pred[64]{0:T(512)(128)(4,1)} %get-tuple-element.44) | copy-start | bytes 196
  79.8 8.3 %copy-start.11 = (pred[64]{0:T(512)(128)(4,1)S(1)}, pred[64]{0:T(512)(128)(4,1)}, u32[]{:S(2)}) copy-start(pred[64]{0:T(512)(128)(4,1)} %get-tuple-element.45) | copy-start | bytes 196
  79.8 5.8 %collective-permute-start.6 = (f32[24,640]{1,0:T(8,128)S(1)}, f32[24,640]{1,0:T(8,128)S(1)}, u32[]{:S(2)}, u32[]{:S(2)}) collective-permute-start(f32[24,640]{1,0:T(8,128)S(1)} %get-tuple-element.19), channel_id=1, source_target_pairs={{0,1},{1,2},{2,3},{3,0},{4,5},{5,6},{6,7},{7,4},{8,9},{9,10},{10,1... | collective-permute-start | bytes 184328 | tf_op jit(solution)/shard_map/ppermute | solution.py:156
  80.7 5.1 %collective-permute-start.7 = (f32[24,640]{1,0:T(8,128)S(1)}, f32[24,640]{1,0:T(8,128)S(1)}, u32[]{:S(2)}, u32[]{:S(2)}) collective-permute-start(f32[24,640]{1,0:T(8,128)S(1)} %get-tuple-element.17), channel_id=1, source_target_pairs={{0,2},{1,3},{2,0},{3,1},{4,6},{5,7},{6,4},{7,5},{8,10},{9,11},{10,... | collective-permute-start | bytes 184328 | tf_op jit(solution)/shard_map/ppermute | solution.py:156
  82.2 3.7 %collective-permute-start.8 = (f32[24,640]{1,0:T(8,128)S(1)}, f32[24,640]{1,0:T(8,128)S(1)}, u32[]{:S(2)}, u32[]{:S(2)}) collective-permute-start(f32[24,640]{1,0:T(8,128)S(1)} %get-tuple-element.18), channel_id=1, source_target_pairs={{0,3},{1,0},{2,1},{3,2},{4,7},{5,4},{6,5},{7,6},{8,11},{9,8},{10,9... | collective-permute-start | bytes 184328 | tf_op jit(solution)/shard_map/ppermute | solution.py:156

commit v13 on v10

--- a/solution.py
+++ b/solution.py
@@ -142,19 +142,21 @@
             peer_rows, block_rows(up_proj[0], source), preferred_element_type=jnp.float32
         )
     inner_act = (jax.nn.silu(gate_h) * up_h).astype(jnp.bfloat16)
-    outputs = jnp.dot(inner_act, down_proj[0], preferred_element_type=jnp.float32)
     row_gate = jnp.where(valid_rows, token_gate[picked], 0.0)
-    weighted = outputs * row_gate[:, None]
-    weighted = lax.dynamic_slice_in_dim(weighted, col_start, col_count, axis=1) + sum(
+
+    def down_block(block):
+        cols = lax.dynamic_slice_in_dim(down_proj[0], block * col_count, col_count, axis=1)
+        return jnp.dot(inner_act, cols, preferred_element_type=jnp.float32) * row_gate[:, None]
+
+    sent = [
         lax.ppermute(
-            lax.dynamic_slice_in_dim(
-                weighted, ((kv_index + shift) % kv_count) * col_count, col_count, axis=1
-            ),
+            down_block((kv_index + shift) % kv_count),
             "kv",
             [(i, (i + shift) % kv_count) for i in range(kv_count)],
         )
         for shift in range(1, kv_count)
-    )
+    ]
+    weighted = down_block(kv_index) + sum(sent)
 
     at_pick = jnp.where(uses_expert, jnp.cumsum(uses_expert.astype(jnp.int32)) - 1, capacity)
     weighted_ext = jnp.concatenate([weighted, jnp.zeros((1, col_count), jnp.float32)], axis=0)

time: 108 us -> 107 us (level)
  waiting for transfers between devices: 17.1 us -> 20.5 us
  other arithmetic: 12.3 us -> 9.41 us
  matrix products: 14.1 us -> 12.1 us
    dot_general x2 -> x3, matrix products: 3.68 us -> 1.59 us  [per_device(): jnp.dot(peer_rows, block_rows(gate_proj[0], source), preferred_element_ty...]
    dot_general x1 -> x4, matrix products: 2.31 us -> 0.74 us  [down_block(): jnp.dot(inner_act, cols, preferred_element_type=jnp.float32)]
    dot_general x3, matrix products: 2.2 us -> 3.66 us  [per_device(): jnp.dot(peer_rows, block_rows(up_proj[0], source), preferred_element_type...]
    gather x2, other arithmetic: 1.25 us -> 0.01 us  [per_device(): weighted_ext[at_pick[j::per_dev]]]
    ppermute x3, waiting for transfers between devices: 0.19 us -> 1.37 us  [per_device(): lax.ppermute(down_block((kv_index + shift) % kv_count), 'kv', [(i, (i + s...]
    all_to_all x1, waiting for transfers between devices: 10.5 us -> 11.6 us  [per_device(): by_slot = lax.all_to_all(to_experts, 'req', 0, 0, tiled=False)]
  transfers between devices with their start and end apart: 11 -> 11, of which waited for: 4 -> 4; matrix products, arithmetic and copies ran while one was open for 19% -> 15% of each run, Pallas kernels for 0% -> 0%
where the time goes in v13:
time: 107 us; the launch traced here: 106 us
  starting transfers between devices  33.8 us (32%)
  waiting for transfers between devices  20.5 us (19%)
  blocking collectives  17.7 us (17%)
  matrix products  12.1 us (11%)
  local copies, waits for them, and re-layouts  12 us (11%)
  other arithmetic  9.41 us (9%)
    all_to_all x1, blocking collectives, per_device(): lax.all_to_all(combined, 'req', 0, 0, tiled=False).astype(jnp.float32)  17.7 us
    all_to_all x1, starting transfers between devices, per_device(): from_homes = lax.all_to_all(to_slots, 'req', 0, 0, tiled=False)  13.1 us
    all_to_all x1, waiting for transfers between devices, per_device(): by_slot = lax.all_to_all(to_experts, 'req', 0, 0, tiled=False)  11.6 us
    all_to_all x1, starting transfers between devices, per_device(): by_slot = lax.all_to_all(to_experts, 'req', 0, 0, tiled=False)  6.98 us
    all_to_all x1, waiting for transfers between devices, per_device(): from_homes = lax.all_to_all(to_slots, 'req', 0, 0, tiled=False)  6.44 us
    ppermute x3, starting transfers between devices, per_device(): lax.ppermute(down_block((kv_index + shift) % kv_count), 'kv', [(i, (i + s...  5.09 us
    ppermute x3, starting transfers between devices, per_device(): lax.ppermute(summed_in, 'kv', [(i, (i + shift) % kv_count) for i in range...  5.05 us
    dot_general x3, matrix products, per_device(): jnp.dot(peer_rows, block_rows(up_proj[0], source), preferred_element_type...  3.66 us
  transfers between devices with their start and end apart: 11, of which 4 were waited for; matrix products, arithmetic and copies ran while one was open for 15% of the time, Pallas kernels for 0%

profile of v13, /device:TPU:1, one launch (start us, length us, event | category | flops | bytes accessed | tf_op | source)
XLA Modules:
  0.0 106.1 jit_solution(4800630606200499764)
XLA Ops:
  3.3 1.1 %pad_maximum_fusion = bf16[64,2,1536]{2,1,0:T(2,128)(2,1)} fusion(bf16[64,2,640]{2,1,0:T(2,128)(2,1)S(1)} %get-tuple-element.20, bf16[64,2,128]{2,1,0:T(2,128)(2,1)S(1)} %get-tuple-element.22, bf16[64,2,128]{2,1,0:T(2,128)(2,1)S(1)} %get-tuple-element.21, bf16[64,2,640]{2,1,0:T(2,128)(2,1)S(1)} %get-tuple-element.19), kind=kLoop, calls=%fused_computation.54 | loop fusion | flops 1572864 | bytes 786432 | tf_op jit(solution)/shard_map/concatenate | solution.py:51
  4.4 13.1 %all-to-all-start = ((bf16[64,2,1536]{2,1,0:T(2,128)(2,1)}), bf16[64,2,1536]{2,1,0:T(2,128)(2,1)}, u32[]{:S(2)}, u32[]{:S(2)}) async-start(bf16[64,2,1536]{2,1,0:T(2,128)(2,1)} %pad_maximum_fusion), calls=%async_computation | async-start | bytes 786432 | tf_op jit(solution)/shard_map/all_to_all | solution.py:52
  20.5 1.4 %scatter_custom_fusion.1 = s32[24]{0:T(128)S(1)} fusion(s32[128]{0:T(128)S(1)} %get-tuple-element.6, s32[128]{0:T(128)S(1)} %broadcast.608, s32[]{:T(128)} %constant.207.clone.1), kind=kCustom, calls=%fused_computation.192 | custom fusion | flops 128 | bytes 100 | tf_op jit(solution)/shard_map/scatter-add | solution.py:121
  26.2 6.4 %all-to-all-done = bf16[64,2,1536]{2,1,0:T(2,128)(2,1)} async-done(((bf16[64,2,1536]{2,1,0:T(2,128)(2,1)}), bf16[64,2,1536]{2,1,0:T(2,128)(2,1)}, u32[]{:S(2)}, u32[]{:S(2)}) %all-to-all-start) | async-done | bytes 393248 | tf_op jit(solution)/shard_map/all_to_all | solution.py:52
  32.7 1.6 %gather_fusion.2 = bf16[2,1536]{1,0:T(2,128)(2,1)S(1)} fusion(bf16[64,2,1536]{2,1,0:T(2,128)(2,1)} %all-to-all-done, s32[2]{0:T(128)S(1)} %fusion.87), kind=kCustom, calls=%fused_computation.2 | custom fusion | bytes 12304 | tf_op jit(solution)/shard_map/gather | solution.py:54
  34.4 2.4 %fusion.96 = (f32[2,5]{1,0:T(2,128)S(1)}, f32[2,5,4096]{2,1,0:T(8,128)S(1)}) fusion(bf16[2,5,128]{2,1,0:T(8,128)(2,1)S(1)} %reshape.496, bf16[2,4096,128]{2,1,0:T(8,128)(2,1)} %param.19, pred[2,4096]{1,0:T(4,128)(4,1)S(1)} %iota_compare_fusion), kind=kOutput, calls=%fused_computation.198 | convolution fusion | flops 10608630 | bytes 2271784 | tf_op jit(solution)/shard_map/rqd,rld->rql/dot_general | solution.py:63
  38.1 1.4 %collective-permute-start = (f32[2,2560]{1,0:T(2,128)S(1)}, f32[2,2560]{1,0:T(2,128)S(1)}, u32[]{:S(2)}, u32[]{:S(2)}) collective-permute-start(f32[2,2560]{1,0:T(2,128)S(1)} %add_dynamic-update-slice_fusion), channel_id=1, source_target_pairs={{0,1},{1,2},{2,3},{3,0},{4,5},{5,6},{6,7},{7,4},{8,9},{9,10},{10,1... | collective-permute-start | bytes 61448 | tf_op jit(solution)/shard_map/ppermute | solution.py:94
  39.5 2.6 %collective-permute-start.1 = (f32[2,2560]{1,0:T(2,128)S(1)}, f32[2,2560]{1,0:T(2,128)S(1)}, u32[]{:S(2)}, u32[]{:S(2)}) collective-permute-start(f32[2,2560]{1,0:T(2,128)S(1)} %add_dynamic-update-slice_fusion), channel_id=1, source_target_pairs={{0,2},{1,3},{2,0},{3,1},{4,6},{5,7},{6,4},{7,5},{8,10},{9,11},{10,... | collective-permute-start | bytes 61448 | tf_op jit(solution)/shard_map/ppermute | solution.py:94
  42.1 1.1 %collective-permute-start.2 = (f32[2,2560]{1,0:T(2,128)S(1)}, f32[2,2560]{1,0:T(2,128)S(1)}, u32[]{:S(2)}, u32[]{:S(2)}) collective-permute-start(f32[2,2560]{1,0:T(2,128)S(1)} %add_dynamic-update-slice_fusion), channel_id=1, source_target_pairs={{0,3},{1,0},{2,1},{3,2},{4,7},{5,4},{6,5},{7,6},{8,11},{9,8},{10,9... | collective-permute-start | bytes 61448 | tf_op jit(solution)/shard_map/ppermute | solution.py:94
  43.9 1.1 %collective-permute-done.2 = f32[2,2560]{1,0:T(2,128)S(1)} collective-permute-done((f32[2,2560]{1,0:T(2,128)S(1)}, f32[2,2560]{1,0:T(2,128)S(1)}, u32[]{:S(2)}, u32[]{:S(2)}) %collective-permute-start.2) | collective-permute-done | bytes 20512 | tf_op jit(solution)/shard_map/ppermute | solution.py:94
  46.0 7.0 %all-to-all-start.1 = ((bf16[64,2,640]{2,1,0:T(2,128)(2,1)}), bf16[64,2,640]{2,1,0:T(2,128)(2,1)S(1)}, u32[]{:S(2)}, u32[]{:S(2)}) async-start(bf16[64,2,640]{2,1,0:T(2,128)(2,1)} %broadcast_select_fusion.4), calls=%async_computation.1 | async-start | bytes 327680 | tf_op jit(solution)/shard_map/all_to_all | solution.py:114
  53.0 11.6 %all-to-all-done.1 = bf16[64,2,640]{2,1,0:T(2,128)(2,1)S(1)} async-done(((bf16[64,2,640]{2,1,0:T(2,128)(2,1)}), bf16[64,2,640]{2,1,0:T(2,128)(2,1)S(1)}, u32[]{:S(2)}, u32[]{:S(2)}) %all-to-all-start.1) | async-done | bytes 163872 | tf_op jit(solution)/shard_map/all_to_all | solution.py:114
  65.6 2.7 %collective-permute-start.5 = (bf16[24,640]{1,0:T(8,128)(2,1)S(1)}, bf16[24,640]{1,0:T(8,128)(2,1)S(1)}, u32[]{:S(2)}, u32[]{:S(2)}) collective-permute-start(bf16[24,640]{1,0:T(8,128)(2,1)S(1)} %gather_fusion.4), channel_id=1, source_target_pairs={{0,3},{1,0},{2,1},{3,2},{4,7},{5,4},{6,5},{7,6},{8,11},{9,8},{10,9... | collective-permute-start | bytes 92168 | tf_op jit(solution)/shard_map/ppermute | solution.py:127
  69.0 1.2 %fusion.14 = f32[24,384]{1,0:T(8,128)S(1)} fusion(bf16[24,640]{1,0:T(8,128)(2,1)S(1)} %gather_fusion.4, bf16[1,2560,384]{2,1,0:T(8,128)(2,1)} %param.28, s32[]{:T(128)S(6)} %select_n.324), kind=kOutput, calls=%fused_computation.34 | convolution fusion | flops 11796480 | bytes 559108 | tf_op jit(solution)/shard_map/dot_general | solution.py:135
  70.3 1.4 %fusion.20 = f32[24,384]{1,0:T(8,128)S(1)} fusion(bf16[24,640]{1,0:T(8,128)(2,1)S(1)} %gather_fusion.4, bf16[1,2560,384]{2,1,0:T(8,128)(2,1)} %param.27, s32[]{:T(128)S(6)} %select_n.324), kind=kOutput, calls=%fused_computation.40 | convolution fusion | flops 11796480 | bytes 559108 | tf_op jit(solution)/shard_map/dot_general | solution.py:134
  71.6 1.2 %convolution_add_fusion.1 = f32[24,384]{1,0:T(8,128)S(1)} fusion(f32[24,384]{1,0:T(8,128)S(1)} %fusion.14, bf16[24,640]{1,0:T(8,128)(2,1)S(1)} %collective-permute-done.3, bf16[1,2560,384]{2,1,0:T(8,128)(2,1)} %param.28, s32[]{:T(128)S(6)} %select_n.337), kind=kOutput, calls=%fused_computation.18 | convolution fusion | flops 11805696 | bytes 595972 | tf_op jit(solution)/shard_map/dot_general | solution.py:141
  72.9 1.2 %convolution_add_fusion.3 = f32[24,384]{1,0:T(8,128)S(1)} fusion(f32[24,384]{1,0:T(8,128)S(1)} %fusion.20, bf16[24,640]{1,0:T(8,128)(2,1)S(1)} %collective-permute-done.3, bf16[1,2560,384]{2,1,0:T(8,128)(2,1)} %param.27, s32[]{:T(128)S(6)} %select_n.337), kind=kOutput, calls=%fused_computation.21 | convolution fusion | flops 11805696 | bytes 595972 | tf_op jit(solution)/shard_map/dot_general | solution.py:138
  74.1 1.2 %fusion.10 = f32[24,384]{1,0:T(8,128)S(1)} fusion(bf16[24,640]{1,0:T(8,128)(2,1)S(1)} %collective-permute-done.5, bf16[1,2560,384]{2,1,0:T(8,128)(2,1)} %param.28, s32[]{:T(128)S(6)} %select_n.341), kind=kOutput, calls=%fused_computation.30 | convolution fusion | flops 11796480 | bytes 559108 | tf_op jit(solution)/shard_map/dot_general | solution.py:141
  75.7 1.2 %multiply_convert_fusion = bf16[24,384]{1,0:T(8,128)(2,1)S(1)} fusion(f32[24,384]{1,0:T(8,128)S(1)} %fusion.2, f32[24,384]{1,0:T(8,128)S(1)} %fusion.10, f32[24,384]{1,0:T(8,128)S(1)} %convolution_add_fusion.1, bf16[24,640]{1,0:T(8,128)(2,1)S(1)} %collective-permute-done.4, bf16[1,2560,384]{2,1,0:T(8,128)(2,1)} %param.28, s32[]{:T(128)S(6)} %select_n.339), kind=kOutput, calls=%fused_computation.82 | convolution fusion | flops 11870208 | bytes 651268 | tf_op jit(solution)/shard_map/dot_general | solution.py:141
  77.2 2.3 %collective-permute-start.7 = (f32[24,640]{1,0:T(8,128)S(1)}, f32[24,640]{1,0:T(8,128)S(1)}, u32[]{:S(2)}, u32[]{:S(2)}) collective-permute-start(f32[24,640]{1,0:T(8,128)S(1)} %convolution_multiply_fusion.2), channel_id=1, source_target_pairs={{0,2},{1,3},{2,0},{3,1},{4,6},{5,7},{6,4},{7,5},{8,10},{9,11},{10,... | collective-permute-start | bytes 184328 | tf_op jit(solution)/shard_map/ppermute | solution.py:152
  79.9 2.7 %collective-permute-start.8 = (f32[24,640]{1,0:T(8,128)S(1)}, f32[24,640]{1,0:T(8,128)S(1)}, u32[]{:S(2)}, u32[]{:S(2)}) collective-permute-start(f32[24,640]{1,0:T(8,128)S(1)} %convolution_multiply_fusion.1), channel_id=1, source_target_pairs={{0,3},{1,0},{2,1},{3,2},{4,7},{5,4},{6,5},{7,6},{8,11},{9,8},{10,9... | collective-permute-start | bytes 184328 | tf_op jit(solution)/shard_map/ppermute | solution.py:152
  82.8 1.4 %collective-permute-done.6 = f32[24,640]{1,0:T(8,128)S(1)} collective-permute-done((f32[24,640]{1,0:T(8,128)S(1)}, f32[24,640]{1,0:T(8,128)S(1)}, u32[]{:S(2)}, u32[]{:S(2)}) %collective-permute-start.6) | collective-permute-done | bytes 61472 | tf_op jit(solution)/shard_map/ppermute | solution.py:152
  85.0 1.3 %gather_fusion.6 = f32[64,640]{1,0:T(8,128)} fusion(f32[25,640]{1,0:T(8,128)S(1)} %concatenate.15, s32[1024]{0:T(1024)S(1)} %pad_clamp_fusion.1), kind=kCustom, calls=%fused_computation.6 | custom fusion | bytes 327936 | tf_op jit(solution)/shard_map/gather | solution.py:170
  87.6 17.7 %all_to_all.15 = bf16[64,2,640]{2,1,0:T(2,128)(2,1)S(1)} all-to-all(bf16[64,2,640]{2,1,0:T(2,128)(2,1)S(1)} %copy.46), channel_id=1, replica_groups=mesh['req'=64,'kv'=4] {'req'}, dimensions={0} | all-to-all | bytes 327680 | tf_op jit(solution)/shard_map/all_to_all | solution.py:175
  (101 shorter events, 19.1 us)
Async XLA Ops:
  0.0 37.6 %copy-start = (bf16[640,2560]{1,0:T(8,128)(2,1)S(1)}, bf16[640,2560]{1,0:T(8,128)(2,1)}, u32[]{:S(2)}) copy-start(bf16[640,2560]{1,0:T(8,128)(2,1)} %param.23) | copy-start | bytes 9830404
  0.0 17.6 %copy-start.8 = (s32[128]{0:T(128)S(1)}, s32[128]{0:T(128)}, u32[]{:S(2)}) copy-start(s32[128]{0:T(128)} %param.22) | copy-start | bytes 1540
  0.0 17.7 %copy-start.5 = (s32[128,6]{0,1:T(8,128)S(1)}, s32[128,6]{0,1:T(8,128)}, u32[]{:S(2)}) copy-start(s32[128,6]{0,1:T(8,128)} %param.25) | copy-start | bytes 9220
  0.0 17.9 %copy-start.6 = (f32[128,6]{0,1:T(8,128)S(1)}, f32[128,6]{0,1:T(8,128)}, u32[]{:S(2)}) copy-start(f32[128,6]{0,1:T(8,128)} %param.26) | copy-start | bytes 9220
  0.0 19.3 %copy-start.1 = (s32[128]{0:T(128)S(1)}, s32[128]{0:T(128)}, u32[]{:S(2)}) copy-start(s32[128]{0:T(128)} %param.21) | copy-start | bytes 1540
  4.4 28.2 %all-to-all-start = ((bf16[64,2,1536]{2,1,0:T(2,128)(2,1)}), bf16[64,2,1536]{2,1,0:T(2,128)(2,1)}, u32[]{:S(2)}, u32[]{:S(2)}) async-start(bf16[64,2,1536]{2,1,0:T(2,128)(2,1)} %pad_maximum_fusion), calls=%async_computation | async-start | bytes 786432 | tf_op jit(solution)/shard_map/all_to_all | solution.py:52
  34.3 2.8 %copy-start.2 = (bf16[2,4096,128]{2,1,0:T(8,128)(2,1)S(1)}, bf16[2,4096,128]{2,1,0:T(8,128)(2,1)}, u32[]{:S(2)}) copy-start(bf16[2,4096,128]{2,1,0:T(8,128)(2,1)} %param.20) | copy-start | bytes 6291460
  37.6 6.1 %copy-start.7 = (bf16[640]{0:T(1024)(128)(2,1)S(1)}, bf16[640]{0:T(1024)(128)(2,1)}, u32[]{:S(2)}) copy-start(bf16[640]{0:T(1024)(128)(2,1)} %param.24) | copy-start | bytes 3844
  38.1 5.7 %collective-permute-start = (f32[2,2560]{1,0:T(2,128)S(1)}, f32[2,2560]{1,0:T(2,128)S(1)}, u32[]{:S(2)}, u32[]{:S(2)}) collective-permute-start(f32[2,2560]{1,0:T(2,128)S(1)} %add_dynamic-update-slice_fusion), channel_id=1, source_target_pairs={{0,1},{1,2},{2,3},{3,0},{4,5},{5,6},{6,7},{7,4},{8,9},{9,10},{10,1... | collective-permute-start | bytes 61448 | tf_op jit(solution)/shard_map/ppermute | solution.py:94
  39.5 4.4 %collective-permute-start.1 = (f32[2,2560]{1,0:T(2,128)S(1)}, f32[2,2560]{1,0:T(2,128)S(1)}, u32[]{:S(2)}, u32[]{:S(2)}) collective-permute-start(f32[2,2560]{1,0:T(2,128)S(1)} %add_dynamic-update-slice_fusion), channel_id=1, source_target_pairs={{0,2},{1,3},{2,0},{3,1},{4,6},{5,7},{6,4},{7,5},{8,10},{9,11},{10,... | collective-permute-start | bytes 61448 | tf_op jit(solution)/shard_map/ppermute | solution.py:94
  42.1 2.8 %collective-permute-start.2 = (f32[2,2560]{1,0:T(2,128)S(1)}, f32[2,2560]{1,0:T(2,128)S(1)}, u32[]{:S(2)}, u32[]{:S(2)}) collective-permute-start(f32[2,2560]{1,0:T(2,128)S(1)} %add_dynamic-update-slice_fusion), channel_id=1, source_target_pairs={{0,3},{1,0},{2,1},{3,2},{4,7},{5,4},{6,5},{7,6},{8,11},{9,8},{10,9... | collective-permute-start | bytes 61448 | tf_op jit(solution)/shard_map/ppermute | solution.py:94
  46.0 18.6 %all-to-all-start.1 = ((bf16[64,2,640]{2,1,0:T(2,128)(2,1)}), bf16[64,2,640]{2,1,0:T(2,128)(2,1)S(1)}, u32[]{:S(2)}, u32[]{:S(2)}) async-start(bf16[64,2,640]{2,1,0:T(2,128)(2,1)} %broadcast_select_fusion.4), calls=%async_computation.1 | async-start | bytes 327680 | tf_op jit(solution)/shard_map/all_to_all | solution.py:114
  65.5 9.8 %copy-start.3 = (bf16[1,2560,384]{2,1,0:T(8,128)(2,1)S(1)}, bf16[1,2560,384]{2,1,0:T(8,128)(2,1)}, u32[]{:S(2)}) copy-start(bf16[1,2560,384]{2,1,0:T(8,128)(2,1)} %param.27) | copy-start | bytes 5898244
  65.5 6.1 %collective-permute-start.3 = (bf16[24,640]{1,0:T(8,128)(2,1)S(1)}, bf16[24,640]{1,0:T(8,128)(2,1)S(1)}, u32[]{:S(2)}, u32[]{:S(2)}) collective-permute-start(bf16[24,640]{1,0:T(8,128)(2,1)S(1)} %gather_fusion.4), channel_id=1, source_target_pairs={{0,1},{1,2},{2,3},{3,0},{4,5},{5,6},{6,7},{7,4},{8,9},{9,10},{10,1... | collective-permute-start | bytes 92168 | tf_op jit(solution)/shard_map/ppermute | solution.py:127
  65.6 8.5 %collective-permute-start.5 = (bf16[24,640]{1,0:T(8,128)(2,1)S(1)}, bf16[24,640]{1,0:T(8,128)(2,1)S(1)}, u32[]{:S(2)}, u32[]{:S(2)}) collective-permute-start(bf16[24,640]{1,0:T(8,128)(2,1)S(1)} %gather_fusion.4), channel_id=1, source_target_pairs={{0,3},{1,0},{2,1},{3,2},{4,7},{5,4},{6,5},{7,6},{8,11},{9,8},{10,9... | collective-permute-start | bytes 92168 | tf_op jit(solution)/shard_map/ppermute | solution.py:127
  68.2 7.3 %collective-permute-start.4 = (bf16[24,640]{1,0:T(8,128)(2,1)S(1)}, bf16[24,640]{1,0:T(8,128)(2,1)S(1)}, u32[]{:S(2)}, u32[]{:S(2)}) collective-permute-start(bf16[24,640]{1,0:T(8,128)(2,1)S(1)} %gather_fusion.4), channel_id=1, source_target_pairs={{0,2},{1,3},{2,0},{3,1},{4,6},{5,7},{6,4},{7,5},{8,10},{9,11},{10,... | collective-permute-start | bytes 92168 | tf_op jit(solution)/shard_map/ppermute | solution.py:127
  70.2 6.7 %copy-start.4 = (bf16[1,384,2560]{2,1,0:T(8,128)(2,1)S(1)}, bf16[1,384,2560]{2,1,0:T(8,128)(2,1)}, u32[]{:S(2)}) copy-start(bf16[1,384,2560]{2,1,0:T(8,128)(2,1)} %param.29) | copy-start | bytes 5898244
  77.2 5.6 %collective-permute-start.7 = (f32[24,640]{1,0:T(8,128)S(1)}, f32[24,640]{1,0:T(8,128)S(1)}, u32[]{:S(2)}, u32[]{:S(2)}) collective-permute-start(f32[24,640]{1,0:T(8,128)S(1)} %convolution_multiply_fusion.2), channel_id=1, source_target_pairs={{0,2},{1,3},{2,0},{3,1},{4,6},{5,7},{6,4},{7,5},{8,10},{9,11},{10,... | collective-permute-start | bytes 184328 | tf_op jit(solution)/shard_map/ppermute | solution.py:152
  79.6 4.5 %collective-permute-start.6 = (f32[24,640]{1,0:T(8,128)S(1)}, f32[24,640]{1,0:T(8,128)S(1)}, u32[]{:S(2)}, u32[]{:S(2)}) collective-permute-start(f32[24,640]{1,0:T(8,128)S(1)} %convolution_multiply_fusion.3), channel_id=1, source_target_pairs={{0,1},{1,2},{2,3},{3,0},{4,5},{5,6},{6,7},{7,4},{8,9},{9,10},{10,1... | collective-permute-start | bytes 184328 | tf_op jit(solution)/shard_map/ppermute | solution.py:152
  79.9 4.2 %collective-permute-start.8 = (f32[24,640]{1,0:T(8,128)S(1)}, f32[24,640]{1,0:T(8,128)S(1)}, u32[]{:S(2)}, u32[]{:S(2)}) collective-permute-start(f32[24,640]{1,0:T(8,128)S(1)} %convolution_multiply_fusion.1), channel_id=1, source_target_pairs={{0,3},{1,0},{2,1},{3,2},{4,7},{5,4},{6,5},{7,6},{8,11},{9,8},{10,9... | collective-permute-start | bytes 184328 | tf_op jit(solution)/shard_map/ppermute | solution.py:152

commit v14 on v13

--- a/solution.py
+++ b/solution.py
@@ -90,10 +90,15 @@
         residual_rows.astype(jnp.float32),
         (0, col_start),
     )
-    parts = [summed_in] + [
-        lax.ppermute(summed_in, "kv", [(i, (i + shift) % kv_count) for i in range(kv_count)])
-        for shift in range(1, kv_count)
-    ]
+    far_last = sorted(range(1, kv_count), key=lambda shift: min(shift, kv_count - shift))
+    far_first = far_last[::-1]
+    sent_rows = {
+        shift: lax.ppermute(
+            summed_in, "kv", [(i, (i + shift) % kv_count) for i in range(kv_count)]
+        )
+        for shift in far_first
+    }
+    parts = [summed_in] + [sent_rows[shift] for shift in far_last]
     summed = parts[0]
     for part in parts[1:]:
         summed = summed + part
@@ -122,11 +127,12 @@
     valid_rows = jnp.arange(capacity) < jnp.sum(uses_expert.astype(jnp.int32))
     picked_slots = slot_of[picked]
     row_block = by_slot[picked_slots // per_dev, picked_slots % per_dev]
-    kv_shifts = range(1, kv_count)
-    from_peers = [
-        lax.ppermute(row_block, "kv", [(i, (i + shift) % kv_count) for i in range(kv_count)])
-        for shift in kv_shifts
-    ]
+    peer_rows_of = {
+        shift: lax.ppermute(row_block, "kv", [(i, (i + shift) % kv_count) for i in range(kv_count)])
+        for shift in far_first
+    }
+    kv_shifts = far_last
+    from_peers = [peer_rows_of[shift] for shift in kv_shifts]
 
     def block_rows(weights, source):
         return lax.dynamic_slice_in_dim(weights, source * col_count, col_count, axis=0)
@@ -154,9 +160,9 @@
             "kv",
             [(i, (i + shift) % kv_count) for i in range(kv_count)],
         )
-        for shift in range(1, kv_count)
+        for shift in far_first
     ]
-    weighted = down_block(kv_index) + sum(sent)
+    weighted = down_block(kv_index) + sum(sent[::-1])
 
     at_pick = jnp.where(uses_expert, jnp.cumsum(uses_expert.astype(jnp.int32)) - 1, capacity)
     weighted_ext = jnp.concatenate([weighted, jnp.zeros((1, col_count), jnp.float32)], axis=0)

time: 107 us -> 107 us (level)
  waiting for transfers between devices: 20.5 us -> 23.8 us
  starting transfers between devices: 33.8 us -> 31.4 us
    ppermute x3, waiting for transfers between devices: 1.37 us -> 3.86 us  [per_device(): lax.ppermute(down_block((kv_index + shift) % kv_count), 'kv', [(i, (i + s...]
    ppermute x3, starting transfers between devices: 5.09 us -> 2.96 us  [per_device(): lax.ppermute(down_block((kv_index + shift) % kv_count), 'kv', [(i, (i + s...]
  transfers between devices with their start and end apart: 11 -> 11, of which waited for: 4 -> 5; matrix products, arithmetic and copies ran while one was open for 15% -> 15% of each run, Pallas kernels for 0% -> 0%
where the time goes in v14:
time: 107 us
  starting transfers between devices  31.4 us (29%)
  waiting for transfers between devices  23.8 us (22%)
  blocking collectives  17.5 us (16%)
  matrix products  12.1 us (11%)
  local copies, waits for them, and re-layouts  12 us (11%)
  other arithmetic  9.41 us (9%)
    all_to_all x1, blocking collectives, per_device(): lax.all_to_all(combined, 'req', 0, 0, tiled=False).astype(jnp.float32)  17.5 us
    all_to_all x1, starting transfers between devices, per_device(): from_homes = lax.all_to_all(to_slots, 'req', 0, 0, tiled=False)  13.1 us
    all_to_all x1, waiting for transfers between devices, per_device(): by_slot = lax.all_to_all(to_experts, 'req', 0, 0, tiled=False)  11.6 us
    all_to_all x1, starting transfers between devices, per_device(): by_slot = lax.all_to_all(to_experts, 'req', 0, 0, tiled=False)  7.01 us
    all_to_all x1, waiting for transfers between devices, per_device(): from_homes = lax.all_to_all(to_slots, 'req', 0, 0, tiled=False)  6.44 us
    ppermute x3, starting transfers between devices, per_device(): lax.ppermute(summed_in, 'kv', [(i, (i + shift) % kv_count) for i in range...  4.44 us
    ppermute x3, waiting for transfers between devices, per_device(): lax.ppermute(down_block((kv_index + shift) % kv_count), 'kv', [(i, (i + s...  3.86 us
    ppermute x3, starting transfers between devices, per_device(): lax.ppermute(row_block, 'kv', [(i, (i + shift) % kv_count) for i in range...  3.85 us
  transfers between devices with their start and end apart: 11, of which 5 were waited for; matrix products, arithmetic and copies ran while one was open for 15% of the time, Pallas kernels for 0%

profile of v14, /device:TPU:1, one launch (start us, length us, event | category | flops | bytes accessed | tf_op | source)
XLA Modules:
  0.0 106.8 jit_solution(5091492268515985763)
XLA Ops:
  4.4 13.1 %all-to-all-start = ((bf16[64,2,1536]{2,1,0:T(2,128)(2,1)}), bf16[64,2,1536]{2,1,0:T(2,128)(2,1)}, u32[]{:S(2)}, u32[]{:S(2)}) async-start(bf16[64,2,1536]{2,1,0:T(2,128)(2,1)} %pad_maximum_fusion), calls=%async_computation | async-start | bytes 786432 | tf_op jit(solution)/shard_map/all_to_all | solution.py:52
  20.5 1.4 %scatter_custom_fusion.1 = s32[24]{0:T(128)S(1)} fusion(s32[128]{0:T(128)S(1)} %get-tuple-element.6, s32[128]{0:T(128)S(1)} %broadcast.608, s32[]{:T(128)} %constant.207.clone.1), kind=kCustom, calls=%fused_computation.192 | custom fusion | flops 128 | bytes 100 | tf_op jit(solution)/shard_map/scatter-add | solution.py:126
  26.2 6.4 %all-to-all-done = bf16[64,2,1536]{2,1,0:T(2,128)(2,1)} async-done(((bf16[64,2,1536]{2,1,0:T(2,128)(2,1)}), bf16[64,2,1536]{2,1,0:T(2,128)(2,1)}, u32[]{:S(2)}, u32[]{:S(2)}) %all-to-all-start) | async-done | bytes 393248 | tf_op jit(solution)/shard_map/all_to_all | solution.py:52
  32.7 1.6 %gather_fusion.2 = bf16[2,1536]{1,0:T(2,128)(2,1)S(1)} fusion(bf16[64,2,1536]{2,1,0:T(2,128)(2,1)} %all-to-all-done, s32[2]{0:T(128)S(1)} %fusion.87), kind=kCustom, calls=%fused_computation.2 | custom fusion | bytes 12304 | tf_op jit(solution)/shard_map/gather | solution.py:54
  34.4 2.4 %fusion.96 = (f32[2,5]{1,0:T(2,128)S(1)}, f32[2,5,4096]{2,1,0:T(8,128)S(1)}) fusion(bf16[2,5,128]{2,1,0:T(8,128)(2,1)S(1)} %reshape.496, bf16[2,4096,128]{2,1,0:T(8,128)(2,1)} %param.19, pred[2,4096]{1,0:T(4,128)(4,1)S(1)} %iota_compare_fusion), kind=kOutput, calls=%fused_computation.198 | convolution fusion | flops 10608630 | bytes 2271784 | tf_op jit(solution)/shard_map/rqd,rld->rql/dot_general | solution.py:63
  38.1 1.4 %collective-permute-start = (f32[2,2560]{1,0:T(2,128)S(1)}, f32[2,2560]{1,0:T(2,128)S(1)}, u32[]{:S(2)}, u32[]{:S(2)}) collective-permute-start(f32[2,2560]{1,0:T(2,128)S(1)} %add_dynamic-update-slice_fusion), channel_id=1, source_target_pairs={{0,1},{1,2},{2,3},{3,0},{4,5},{5,6},{6,7},{7,4},{8,9},{9,10},{10,1... | collective-permute-start | bytes 61448 | tf_op jit(solution)/shard_map/ppermute | solution.py:96
  39.5 1.5 %collective-permute-start.1 = (f32[2,2560]{1,0:T(2,128)S(1)}, f32[2,2560]{1,0:T(2,128)S(1)}, u32[]{:S(2)}, u32[]{:S(2)}) collective-permute-start(f32[2,2560]{1,0:T(2,128)S(1)} %add_dynamic-update-slice_fusion), channel_id=1, source_target_pairs={{0,3},{1,0},{2,1},{3,2},{4,7},{5,4},{6,5},{7,6},{8,11},{9,8},{10,9... | collective-permute-start | bytes 61448 | tf_op jit(solution)/shard_map/ppermute | solution.py:96
  41.0 1.6 %collective-permute-start.2 = (f32[2,2560]{1,0:T(2,128)S(1)}, f32[2,2560]{1,0:T(2,128)S(1)}, u32[]{:S(2)}, u32[]{:S(2)}) collective-permute-start(f32[2,2560]{1,0:T(2,128)S(1)} %add_dynamic-update-slice_fusion), channel_id=1, source_target_pairs={{0,2},{1,3},{2,0},{3,1},{4,6},{5,7},{6,4},{7,5},{8,10},{9,11},{10,... | collective-permute-start | bytes 61448 | tf_op jit(solution)/shard_map/ppermute | solution.py:96
  43.3 1.9 %collective-permute-done.2 = f32[2,2560]{1,0:T(2,128)S(1)} collective-permute-done((f32[2,2560]{1,0:T(2,128)S(1)}, f32[2,2560]{1,0:T(2,128)S(1)}, u32[]{:S(2)}, u32[]{:S(2)}) %collective-permute-start.2) | collective-permute-done | bytes 20512 | tf_op jit(solution)/shard_map/ppermute | solution.py:96
  46.3 7.0 %all-to-all-start.1 = ((bf16[64,2,640]{2,1,0:T(2,128)(2,1)}), bf16[64,2,640]{2,1,0:T(2,128)(2,1)S(1)}, u32[]{:S(2)}, u32[]{:S(2)}) async-start(bf16[64,2,640]{2,1,0:T(2,128)(2,1)} %broadcast_select_fusion.4), calls=%async_computation.1 | async-start | bytes 327680 | tf_op jit(solution)/shard_map/all_to_all | solution.py:119
  53.3 11.6 %all-to-all-done.1 = bf16[64,2,640]{2,1,0:T(2,128)(2,1)S(1)} async-done(((bf16[64,2,640]{2,1,0:T(2,128)(2,1)}), bf16[64,2,640]{2,1,0:T(2,128)(2,1)S(1)}, u32[]{:S(2)}, u32[]{:S(2)}) %all-to-all-start.1) | async-done | bytes 163872 | tf_op jit(solution)/shard_map/all_to_all | solution.py:119
  65.9 2.6 %collective-permute-start.5 = (bf16[24,640]{1,0:T(8,128)(2,1)S(1)}, bf16[24,640]{1,0:T(8,128)(2,1)S(1)}, u32[]{:S(2)}, u32[]{:S(2)}) collective-permute-start(bf16[24,640]{1,0:T(8,128)(2,1)S(1)} %gather_fusion.4), channel_id=1, source_target_pairs={{0,2},{1,3},{2,0},{3,1},{4,6},{5,7},{6,4},{7,5},{8,10},{9,11},{10,... | collective-permute-start | bytes 92168 | tf_op jit(solution)/shard_map/ppermute | solution.py:131
  69.6 1.2 %fusion.14 = f32[24,384]{1,0:T(8,128)S(1)} fusion(bf16[24,640]{1,0:T(8,128)(2,1)S(1)} %gather_fusion.4, bf16[1,2560,384]{2,1,0:T(8,128)(2,1)} %param.28, s32[]{:T(128)S(6)} %select_n.324), kind=kOutput, calls=%fused_computation.34 | convolution fusion | flops 11796480 | bytes 559108 | tf_op jit(solution)/shard_map/dot_general | solution.py:141
  70.8 1.4 %fusion.20 = f32[24,384]{1,0:T(8,128)S(1)} fusion(bf16[24,640]{1,0:T(8,128)(2,1)S(1)} %gather_fusion.4, bf16[1,2560,384]{2,1,0:T(8,128)(2,1)} %param.27, s32[]{:T(128)S(6)} %select_n.324), kind=kOutput, calls=%fused_computation.40 | convolution fusion | flops 11796480 | bytes 559108 | tf_op jit(solution)/shard_map/dot_general | solution.py:140
  72.2 1.2 %convolution_add_fusion.1 = f32[24,384]{1,0:T(8,128)S(1)} fusion(f32[24,384]{1,0:T(8,128)S(1)} %fusion.14, bf16[24,640]{1,0:T(8,128)(2,1)S(1)} %collective-permute-done.3, bf16[1,2560,384]{2,1,0:T(8,128)(2,1)} %param.28, s32[]{:T(128)S(6)} %select_n.337), kind=kOutput, calls=%fused_computation.18 | convolution fusion | flops 11805696 | bytes 595972 | tf_op jit(solution)/shard_map/dot_general | solution.py:147
  73.4 1.2 %convolution_add_fusion.3 = f32[24,384]{1,0:T(8,128)S(1)} fusion(f32[24,384]{1,0:T(8,128)S(1)} %fusion.20, bf16[24,640]{1,0:T(8,128)(2,1)S(1)} %collective-permute-done.3, bf16[1,2560,384]{2,1,0:T(8,128)(2,1)} %param.27, s32[]{:T(128)S(6)} %select_n.337), kind=kOutput, calls=%fused_computation.21 | convolution fusion | flops 11805696 | bytes 595972 | tf_op jit(solution)/shard_map/dot_general | solution.py:144
  74.7 1.2 %fusion.10 = f32[24,384]{1,0:T(8,128)S(1)} fusion(bf16[24,640]{1,0:T(8,128)(2,1)S(1)} %collective-permute-done.5, bf16[1,2560,384]{2,1,0:T(8,128)(2,1)} %param.28, s32[]{:T(128)S(6)} %select_n.341), kind=kOutput, calls=%fused_computation.30 | convolution fusion | flops 11796480 | bytes 559108 | tf_op jit(solution)/shard_map/dot_general | solution.py:147
  76.3 1.2 %multiply_convert_fusion = bf16[24,384]{1,0:T(8,128)(2,1)S(1)} fusion(f32[24,384]{1,0:T(8,128)S(1)} %fusion.2, f32[24,384]{1,0:T(8,128)S(1)} %fusion.10, f32[24,384]{1,0:T(8,128)S(1)} %convolution_add_fusion.1, bf16[24,640]{1,0:T(8,128)(2,1)S(1)} %collective-permute-done.4, bf16[1,2560,384]{2,1,0:T(8,128)(2,1)} %param.28, s32[]{:T(128)S(6)} %select_n.339), kind=kOutput, calls=%fused_computation.82 | convolution fusion | flops 11870208 | bytes 651268 | tf_op jit(solution)/shard_map/dot_general | solution.py:147
  78.0 1.5 %collective-permute-start.6 = (f32[24,640]{1,0:T(8,128)S(1)}, f32[24,640]{1,0:T(8,128)S(1)}, u32[]{:S(2)}, u32[]{:S(2)}) collective-permute-start(f32[24,640]{1,0:T(8,128)S(1)} %convolution_multiply_fusion.3), channel_id=1, source_target_pairs={{0,1},{1,2},{2,3},{3,0},{4,5},{5,6},{6,7},{7,4},{8,9},{9,10},{10,1... | collective-permute-start | bytes 184328 | tf_op jit(solution)/shard_map/ppermute | solution.py:158
  79.7 1.4 %collective-permute-start.8 = (f32[24,640]{1,0:T(8,128)S(1)}, f32[24,640]{1,0:T(8,128)S(1)}, u32[]{:S(2)}, u32[]{:S(2)}) collective-permute-start(f32[24,640]{1,0:T(8,128)S(1)} %convolution_multiply_fusion.1), channel_id=1, source_target_pairs={{0,2},{1,3},{2,0},{3,1},{4,6},{5,7},{6,4},{7,5},{8,10},{9,11},{10,... | collective-permute-start | bytes 184328 | tf_op jit(solution)/shard_map/ppermute | solution.py:158
  81.2 1.2 %collective-permute-done.6 = f32[24,640]{1,0:T(8,128)S(1)} collective-permute-done((f32[24,640]{1,0:T(8,128)S(1)}, f32[24,640]{1,0:T(8,128)S(1)}, u32[]{:S(2)}, u32[]{:S(2)}) %collective-permute-start.6) | collective-permute-done | bytes 61472 | tf_op jit(solution)/shard_map/ppermute | solution.py:158
  82.4 2.7 %collective-permute-done.8 = f32[24,640]{1,0:T(8,128)S(1)} collective-permute-done((f32[24,640]{1,0:T(8,128)S(1)}, f32[24,640]{1,0:T(8,128)S(1)}, u32[]{:S(2)}, u32[]{:S(2)}) %collective-permute-start.8) | collective-permute-done | bytes 61472 | tf_op jit(solution)/shard_map/ppermute | solution.py:158
  86.0 1.3 %gather_fusion.6 = f32[64,640]{1,0:T(8,128)} fusion(f32[25,640]{1,0:T(8,128)S(1)} %concatenate.15, s32[1024]{0:T(1024)S(1)} %pad_clamp_fusion.1), kind=kCustom, calls=%fused_computation.6 | custom fusion | bytes 327936 | tf_op jit(solution)/shard_map/gather | solution.py:176
  88.5 17.5 %all_to_all.15 = bf16[64,2,640]{2,1,0:T(2,128)(2,1)S(1)} all-to-all(bf16[64,2,640]{2,1,0:T(2,128)(2,1)S(1)} %copy.46), channel_id=1, replica_groups=mesh['req'=64,'kv'=4] {'req'}, dimensions={0} | all-to-all | bytes 327680 | tf_op jit(solution)/shard_map/all_to_all | solution.py:181
  (101 shorter events, 20.5 us)
Async XLA Ops:
  0.0 37.6 %copy-start = (bf16[640,2560]{1,0:T(8,128)(2,1)S(1)}, bf16[640,2560]{1,0:T(8,128)(2,1)}, u32[]{:S(2)}) copy-start(bf16[640,2560]{1,0:T(8,128)(2,1)} %param.23) | copy-start | bytes 9830404
  0.0 17.6 %copy-start.8 = (s32[128]{0:T(128)S(1)}, s32[128]{0:T(128)}, u32[]{:S(2)}) copy-start(s32[128]{0:T(128)} %param.22) | copy-start | bytes 1540
  0.0 17.7 %copy-start.5 = (s32[128,6]{0,1:T(8,128)S(1)}, s32[128,6]{0,1:T(8,128)}, u32[]{:S(2)}) copy-start(s32[128,6]{0,1:T(8,128)} %param.25) | copy-start | bytes 9220
  0.0 17.9 %copy-start.6 = (f32[128,6]{0,1:T(8,128)S(1)}, f32[128,6]{0,1:T(8,128)}, u32[]{:S(2)}) copy-start(f32[128,6]{0,1:T(8,128)} %param.26) | copy-start | bytes 9220
  0.0 19.3 %copy-start.1 = (s32[128]{0:T(128)S(1)}, s32[128]{0:T(128)}, u32[]{:S(2)}) copy-start(s32[128]{0:T(128)} %param.21) | copy-start | bytes 1540
  4.4 28.2 %all-to-all-start = ((bf16[64,2,1536]{2,1,0:T(2,128)(2,1)}), bf16[64,2,1536]{2,1,0:T(2,128)(2,1)}, u32[]{:S(2)}, u32[]{:S(2)}) async-start(bf16[64,2,1536]{2,1,0:T(2,128)(2,1)} %pad_maximum_fusion), calls=%async_computation | async-start | bytes 786432 | tf_op jit(solution)/shard_map/all_to_all | solution.py:52
  34.3 2.8 %copy-start.2 = (bf16[2,4096,128]{2,1,0:T(8,128)(2,1)S(1)}, bf16[2,4096,128]{2,1,0:T(8,128)(2,1)}, u32[]{:S(2)}) copy-start(bf16[2,4096,128]{2,1,0:T(8,128)(2,1)} %param.20) | copy-start | bytes 6291460
  37.6 5.5 %copy-start.7 = (bf16[640]{0:T(1024)(128)(2,1)S(1)}, bf16[640]{0:T(1024)(128)(2,1)}, u32[]{:S(2)}) copy-start(bf16[640]{0:T(1024)(128)(2,1)} %param.24) | copy-start | bytes 3844
  38.1 5.1 %collective-permute-start = (f32[2,2560]{1,0:T(2,128)S(1)}, f32[2,2560]{1,0:T(2,128)S(1)}, u32[]{:S(2)}, u32[]{:S(2)}) collective-permute-start(f32[2,2560]{1,0:T(2,128)S(1)} %add_dynamic-update-slice_fusion), channel_id=1, source_target_pairs={{0,1},{1,2},{2,3},{3,0},{4,5},{5,6},{6,7},{7,4},{8,9},{9,10},{10,1... | collective-permute-start | bytes 61448 | tf_op jit(solution)/shard_map/ppermute | solution.py:96
  39.5 3.8 %collective-permute-start.1 = (f32[2,2560]{1,0:T(2,128)S(1)}, f32[2,2560]{1,0:T(2,128)S(1)}, u32[]{:S(2)}, u32[]{:S(2)}) collective-permute-start(f32[2,2560]{1,0:T(2,128)S(1)} %add_dynamic-update-slice_fusion), channel_id=1, source_target_pairs={{0,3},{1,0},{2,1},{3,2},{4,7},{5,4},{6,5},{7,6},{8,11},{9,8},{10,9... | collective-permute-start | bytes 61448 | tf_op jit(solution)/shard_map/ppermute | solution.py:96
  41.0 4.1 %collective-permute-start.2 = (f32[2,2560]{1,0:T(2,128)S(1)}, f32[2,2560]{1,0:T(2,128)S(1)}, u32[]{:S(2)}, u32[]{:S(2)}) collective-permute-start(f32[2,2560]{1,0:T(2,128)S(1)} %add_dynamic-update-slice_fusion), channel_id=1, source_target_pairs={{0,2},{1,3},{2,0},{3,1},{4,6},{5,7},{6,4},{7,5},{8,10},{9,11},{10,... | collective-permute-start | bytes 61448 | tf_op jit(solution)/shard_map/ppermute | solution.py:96
  46.3 18.7 %all-to-all-start.1 = ((bf16[64,2,640]{2,1,0:T(2,128)(2,1)}), bf16[64,2,640]{2,1,0:T(2,128)(2,1)S(1)}, u32[]{:S(2)}, u32[]{:S(2)}) async-start(bf16[64,2,640]{2,1,0:T(2,128)(2,1)} %broadcast_select_fusion.4), calls=%async_computation.1 | async-start | bytes 327680 | tf_op jit(solution)/shard_map/all_to_all | solution.py:119
  65.7 10.2 %copy-start.3 = (bf16[1,2560,384]{2,1,0:T(8,128)(2,1)S(1)}, bf16[1,2560,384]{2,1,0:T(8,128)(2,1)}, u32[]{:S(2)}) copy-start(bf16[1,2560,384]{2,1,0:T(8,128)(2,1)} %param.27) | copy-start | bytes 5898244
  65.8 6.4 %collective-permute-start.3 = (bf16[24,640]{1,0:T(8,128)(2,1)S(1)}, bf16[24,640]{1,0:T(8,128)(2,1)S(1)}, u32[]{:S(2)}, u32[]{:S(2)}) collective-permute-start(bf16[24,640]{1,0:T(8,128)(2,1)S(1)} %gather_fusion.4), channel_id=1, source_target_pairs={{0,1},{1,2},{2,3},{3,0},{4,5},{5,6},{6,7},{7,4},{8,9},{9,10},{10,1... | collective-permute-start | bytes 92168 | tf_op jit(solution)/shard_map/ppermute | solution.py:131
  65.9 8.7 %collective-permute-start.5 = (bf16[24,640]{1,0:T(8,128)(2,1)S(1)}, bf16[24,640]{1,0:T(8,128)(2,1)S(1)}, u32[]{:S(2)}, u32[]{:S(2)}) collective-permute-start(bf16[24,640]{1,0:T(8,128)(2,1)S(1)} %gather_fusion.4), channel_id=1, source_target_pairs={{0,2},{1,3},{2,0},{3,1},{4,6},{5,7},{6,4},{7,5},{8,10},{9,11},{10,... | collective-permute-start | bytes 92168 | tf_op jit(solution)/shard_map/ppermute | solution.py:131
  68.5 7.6 %collective-permute-start.4 = (bf16[24,640]{1,0:T(8,128)(2,1)S(1)}, bf16[24,640]{1,0:T(8,128)(2,1)S(1)}, u32[]{:S(2)}, u32[]{:S(2)}) collective-permute-start(bf16[24,640]{1,0:T(8,128)(2,1)S(1)} %gather_fusion.4), channel_id=1, source_target_pairs={{0,3},{1,0},{2,1},{3,2},{4,7},{5,4},{6,5},{7,6},{8,11},{9,8},{10,9... | collective-permute-start | bytes 92168 | tf_op jit(solution)/shard_map/ppermute | solution.py:131
  70.8 6.7 %copy-start.4 = (bf16[1,384,2560]{2,1,0:T(8,128)(2,1)S(1)}, bf16[1,384,2560]{2,1,0:T(8,128)(2,1)}, u32[]{:S(2)}) copy-start(bf16[1,384,2560]{2,1,0:T(8,128)(2,1)} %param.29) | copy-start | bytes 5898244
  77.7 3.5 %collective-permute-start.7 = (f32[24,640]{1,0:T(8,128)S(1)}, f32[24,640]{1,0:T(8,128)S(1)}, u32[]{:S(2)}, u32[]{:S(2)}) collective-permute-start(f32[24,640]{1,0:T(8,128)S(1)} %convolution_multiply_fusion.2), channel_id=1, source_target_pairs={{0,3},{1,0},{2,1},{3,2},{4,7},{5,4},{6,5},{7,6},{8,11},{9,8},{10,9... | collective-permute-start | bytes 184328 | tf_op jit(solution)/shard_map/ppermute | solution.py:158
  78.0 4.4 %collective-permute-start.6 = (f32[24,640]{1,0:T(8,128)S(1)}, f32[24,640]{1,0:T(8,128)S(1)}, u32[]{:S(2)}, u32[]{:S(2)}) collective-permute-start(f32[24,640]{1,0:T(8,128)S(1)} %convolution_multiply_fusion.3), channel_id=1, source_target_pairs={{0,1},{1,2},{2,3},{3,0},{4,5},{5,6},{6,7},{7,4},{8,9},{9,10},{10,1... | collective-permute-start | bytes 184328 | tf_op jit(solution)/shard_map/ppermute | solution.py:158
  79.7 5.3 %collective-permute-start.8 = (f32[24,640]{1,0:T(8,128)S(1)}, f32[24,640]{1,0:T(8,128)S(1)}, u32[]{:S(2)}, u32[]{:S(2)}) collective-permute-start(f32[24,640]{1,0:T(8,128)S(1)} %convolution_multiply_fusion.1), channel_id=1, source_target_pairs={{0,2},{1,3},{2,0},{3,1},{4,6},{5,7},{6,4},{7,5},{8,10},{9,11},{10,... | collective-permute-start | bytes 184328 | tf_op jit(solution)/shard_map/ppermute | solution.py:158

commit v15 on v13

--- a/solution.py
+++ b/solution.py
@@ -51,7 +51,15 @@
     to_slots = jnp.concatenate([to_slot_rows(piece) for piece in pieces], axis=2)
     from_homes = lax.all_to_all(to_slots, "req", 0, 0, tiled=False)
     served = lax.dynamic_slice_in_dim(slot_order, req_index * per_dev, per_dev)
-    mine = from_homes[served // per_dev, jnp.arange(per_dev)]
+    mine = jnp.concatenate(
+        [
+            lax.dynamic_slice(
+                from_homes, (served[j] // per_dev, j, 0), (1, 1, from_homes.shape[2])
+            )[0]
+            for j in range(per_dev)
+        ],
+        axis=0,
+    )
     query_rows = mine[:, :q_width].reshape(per_dev, -1, head_dim)
     self_key_row = mine[:, q_width:q_width + head_dim]
     self_value_row = mine[:, q_width + head_dim:q_width + 2 * head_dim]

time: 107 us -> 110 us (1.028)
  waiting for transfers between devices: 20.5 us -> 14.8 us
  between operations: 0.6 us -> 5.78 us
  starting transfers between devices: 33.8 us -> 38 us
    all_to_all x1, waiting for transfers between devices: 6.44 us -> 0.71 us  [per_device(): from_homes = lax.all_to_all(to_slots, 'req', 0, 0, tiled=False)]
    all_to_all x1, starting transfers between devices: 6.98 us -> 11.1 us  [per_device(): by_slot = lax.all_to_all(to_experts, 'req', 0, 0, tiled=False)]
    gather x1 -> x0, local copies, waits for them, and re-layouts: 1.6 us -> none  [per_device(): mine = from_homes[served // per_dev, jnp.arange(per_dev)]]
where the time goes in v15:
time: 110 us; the launch traced here: 109 us
  starting transfers between devices  38 us (35%)
  blocking collectives  17.7 us (16%)
  waiting for transfers between devices  14.8 us (13%)
  matrix products  12.1 us (11%)
  local copies, waits for them, and re-layouts  11.7 us (11%)
  other arithmetic  9.35 us (8%)
  between operations  5.78 us (5%)
    all_to_all x1, blocking collectives, per_device(): lax.all_to_all(combined, 'req', 0, 0, tiled=False).astype(jnp.float32)  17.7 us
    all_to_all x1, starting transfers between devices, per_device(): from_homes = lax.all_to_all(to_slots, 'req', 0, 0, tiled=False)  13.1 us
    all_to_all x1, waiting for transfers between devices, per_device(): by_slot = lax.all_to_all(to_experts, 'req', 0, 0, tiled=False)  11.6 us
    all_to_all x1, starting transfers between devices, per_device(): by_slot = lax.all_to_all(to_experts, 'req', 0, 0, tiled=False)  11.1 us
    ppermute x3, starting transfers between devices, per_device(): lax.ppermute(down_block((kv_index + shift) % kv_count), 'kv', [(i, (i + s...  5.09 us
    ppermute x3, starting transfers between devices, per_device(): lax.ppermute(summed_in, 'kv', [(i, (i + shift) % kv_count) for i in range...  5.06 us
    dot_general x3, matrix products, per_device(): jnp.dot(peer_rows, block_rows(up_proj[0], source), preferred_element_type...  3.66 us
    ppermute x3, starting transfers between devices, per_device(): lax.ppermute(row_block, 'kv', [(i, (i + shift) % kv_count) for i in range...  3.53 us
  transfers between devices with their start and end apart: 11, of which 4 were waited for; matrix products, arithmetic and copies ran while one was open for 15% of the time, Pallas kernels for 0%

profile of v15, /device:TPU:1, one launch (start us, length us, event | category | flops | bytes accessed | tf_op | source)
XLA Modules:
  0.0 109.4 jit_solution(5169619476720869574)
XLA Ops:
  3.3 1.1 %pad_maximum_fusion = bf16[64,2,1536]{2,1,0:T(2,128)(2,1)} fusion(bf16[64,2,640]{2,1,0:T(2,128)(2,1)S(1)} %get-tuple-element.24, bf16[64,2,128]{2,1,0:T(2,128)(2,1)S(1)} %get-tuple-element.26, bf16[64,2,128]{2,1,0:T(2,128)(2,1)S(1)} %get-tuple-element.25, bf16[64,2,640]{2,1,0:T(2,128)(2,1)S(1)} %get-tuple-element.23), kind=kLoop, calls=%fused_computation.53 | loop fusion | flops 1572864 | bytes 786432 | tf_op jit(solution)/shard_map/concatenate | solution.py:51
  4.4 13.1 %all-to-all-start = ((bf16[64,2,1536]{2,1,0:T(2,128)(2,1)}), bf16[64,2,1536]{2,1,0:T(2,128)(2,1)}, u32[]{:S(2)}, u32[]{:S(2)}) async-start(bf16[64,2,1536]{2,1,0:T(2,128)(2,1)} %pad_maximum_fusion), calls=%async_computation | async-start | bytes 786432 | tf_op jit(solution)/shard_map/all_to_all | solution.py:52
  26.2 1.4 %scatter_custom_fusion.1 = s32[24]{0:T(128)S(1)} fusion(s32[128]{0:T(128)S(1)} %get-tuple-element.6, s32[128]{0:T(128)S(1)} %broadcast.579, s32[]{:T(128)} %constant.212.clone.1), kind=kCustom, calls=%fused_computation.185 | custom fusion | flops 128 | bytes 100 | tf_op jit(solution)/shard_map/scatter-add | solution.py:129
  28.6 1.0 scatter_custom_fusion
  33.6 2.4 %fusion.92 = (f32[2,5]{1,0:T(2,128)S(1)}, f32[2,5,4096]{2,1,0:T(8,128)S(1)}) fusion(bf16[2,5,128]{2,1,0:T(8,128)(2,1)S(1)} %reshape.496, bf16[2,4096,128]{2,1,0:T(8,128)(2,1)} %param.19, pred[2,4096]{1,0:T(4,128)(4,1)S(1)} %iota_compare_fusion), kind=kOutput, calls=%fused_computation.192 | convolution fusion | flops 10608630 | bytes 2271784 | tf_op jit(solution)/shard_map/rqd,rld->rql/dot_general | solution.py:71
  37.3 1.4 %collective-permute-start = (f32[2,2560]{1,0:T(2,128)S(1)}, f32[2,2560]{1,0:T(2,128)S(1)}, u32[]{:S(2)}, u32[]{:S(2)}) collective-permute-start(f32[2,2560]{1,0:T(2,128)S(1)} %add_dynamic-update-slice_fusion), channel_id=1, source_target_pairs={{0,1},{1,2},{2,3},{3,0},{4,5},{5,6},{6,7},{7,4},{8,9},{9,10},{10,1... | collective-permute-start | bytes 61448 | tf_op jit(solution)/shard_map/ppermute | solution.py:102
  38.7 2.6 %collective-permute-start.1 = (f32[2,2560]{1,0:T(2,128)S(1)}, f32[2,2560]{1,0:T(2,128)S(1)}, u32[]{:S(2)}, u32[]{:S(2)}) collective-permute-start(f32[2,2560]{1,0:T(2,128)S(1)} %add_dynamic-update-slice_fusion), channel_id=1, source_target_pairs={{0,2},{1,3},{2,0},{3,1},{4,6},{5,7},{6,4},{7,5},{8,10},{9,11},{10,... | collective-permute-start | bytes 61448 | tf_op jit(solution)/shard_map/ppermute | solution.py:102
  41.3 1.1 collective-permute-start.2
  43.0 1.1 collective-permute-done.2
  45.2 11.1 %all-to-all-start.1 = ((bf16[64,2,640]{2,1,0:T(2,128)(2,1)}), bf16[64,2,640]{2,1,0:T(2,128)(2,1)S(1)}, u32[]{:S(2)}, u32[]{:S(2)}) async-start(bf16[64,2,640]{2,1,0:T(2,128)(2,1)} %broadcast_select_fusion.4), calls=%async_computation.1 | async-start | bytes 327680 | tf_op jit(solution)/shard_map/all_to_all | solution.py:122
  56.4 11.6 %all-to-all-done.1 = bf16[64,2,640]{2,1,0:T(2,128)(2,1)S(1)} async-done(((bf16[64,2,640]{2,1,0:T(2,128)(2,1)}), bf16[64,2,640]{2,1,0:T(2,128)(2,1)S(1)}, u32[]{:S(2)}, u32[]{:S(2)}) %all-to-all-start.1) | async-done | bytes 163872 | tf_op jit(solution)/shard_map/all_to_all | solution.py:122
  68.9 2.7 %collective-permute-start.5 = (bf16[24,640]{1,0:T(8,128)(2,1)S(1)}, bf16[24,640]{1,0:T(8,128)(2,1)S(1)}, u32[]{:S(2)}, u32[]{:S(2)}) collective-permute-start(bf16[24,640]{1,0:T(8,128)(2,1)S(1)} %gather_fusion.3), channel_id=1, source_target_pairs={{0,3},{1,0},{2,1},{3,2},{4,7},{5,4},{6,5},{7,6},{8,11},{9,8},{10,9... | collective-permute-start | bytes 92168 | tf_op jit(solution)/shard_map/ppermute | solution.py:135
  72.4 1.2 %fusion.14 = f32[24,384]{1,0:T(8,128)S(1)} fusion(bf16[24,640]{1,0:T(8,128)(2,1)S(1)} %gather_fusion.3, bf16[1,2560,384]{2,1,0:T(8,128)(2,1)} %param.28, s32[]{:T(128)S(6)} %select_n.330), kind=kOutput, calls=%fused_computation.33 | convolution fusion | flops 11796480 | bytes 559108 | tf_op jit(solution)/shard_map/dot_general | solution.py:143
  73.6 1.4 %fusion.20 = f32[24,384]{1,0:T(8,128)S(1)} fusion(bf16[24,640]{1,0:T(8,128)(2,1)S(1)} %gather_fusion.3, bf16[1,2560,384]{2,1,0:T(8,128)(2,1)} %param.27, s32[]{:T(128)S(6)} %select_n.330), kind=kOutput, calls=%fused_computation.39 | convolution fusion | flops 11796480 | bytes 559108 | tf_op jit(solution)/shard_map/dot_general | solution.py:142
  75.0 1.2 %convolution_add_fusion.1 = f32[24,384]{1,0:T(8,128)S(1)} fusion(f32[24,384]{1,0:T(8,128)S(1)} %fusion.14, bf16[24,640]{1,0:T(8,128)(2,1)S(1)} %collective-permute-done.3, bf16[1,2560,384]{2,1,0:T(8,128)(2,1)} %param.28, s32[]{:T(128)S(6)} %select_n.343), kind=kOutput, calls=%fused_computation.17 | convolution fusion | flops 11805696 | bytes 595972 | tf_op jit(solution)/shard_map/dot_general | solution.py:149
  76.2 1.2 %convolution_add_fusion.3 = f32[24,384]{1,0:T(8,128)S(1)} fusion(f32[24,384]{1,0:T(8,128)S(1)} %fusion.20, bf16[24,640]{1,0:T(8,128)(2,1)S(1)} %collective-permute-done.3, bf16[1,2560,384]{2,1,0:T(8,128)(2,1)} %param.27, s32[]{:T(128)S(6)} %select_n.343), kind=kOutput, calls=%fused_computation.20 | convolution fusion | flops 11805696 | bytes 595972 | tf_op jit(solution)/shard_map/dot_general | solution.py:146
  77.4 1.2 %fusion.10 = f32[24,384]{1,0:T(8,128)S(1)} fusion(bf16[24,640]{1,0:T(8,128)(2,1)S(1)} %collective-permute-done.5, bf16[1,2560,384]{2,1,0:T(8,128)(2,1)} %param.28, s32[]{:T(128)S(6)} %select_n.347), kind=kOutput, calls=%fused_computation.29 | convolution fusion | flops 11796480 | bytes 559108 | tf_op jit(solution)/shard_map/dot_general | solution.py:149
  79.1 1.2 %multiply_convert_fusion = bf16[24,384]{1,0:T(8,128)(2,1)S(1)} fusion(f32[24,384]{1,0:T(8,128)S(1)} %fusion.2, f32[24,384]{1,0:T(8,128)S(1)} %fusion.10, f32[24,384]{1,0:T(8,128)S(1)} %convolution_add_fusion.1, bf16[24,640]{1,0:T(8,128)(2,1)S(1)} %collective-permute-done.4, bf16[1,2560,384]{2,1,0:T(8,128)(2,1)} %param.28, s32[]{:T(128)S(6)} %select_n.345), kind=kOutput, calls=%fused_computation.81 | convolution fusion | flops 11870208 | bytes 651268 | tf_op jit(solution)/shard_map/dot_general | solution.py:149
  80.5 2.3 %collective-permute-start.7 = (f32[24,640]{1,0:T(8,128)S(1)}, f32[24,640]{1,0:T(8,128)S(1)}, u32[]{:S(2)}, u32[]{:S(2)}) collective-permute-start(f32[24,640]{1,0:T(8,128)S(1)} %convolution_multiply_fusion.2), channel_id=1, source_target_pairs={{0,2},{1,3},{2,0},{3,1},{4,6},{5,7},{6,4},{7,5},{8,10},{9,11},{10,... | collective-permute-start | bytes 184328 | tf_op jit(solution)/shard_map/ppermute | solution.py:160
  83.2 2.7 %collective-permute-start.8 = (f32[24,640]{1,0:T(8,128)S(1)}, f32[24,640]{1,0:T(8,128)S(1)}, u32[]{:S(2)}, u32[]{:S(2)}) collective-permute-start(f32[24,640]{1,0:T(8,128)S(1)} %convolution_multiply_fusion.1), channel_id=1, source_target_pairs={{0,3},{1,0},{2,1},{3,2},{4,7},{5,4},{6,5},{7,6},{8,11},{9,8},{10,9... | collective-permute-start | bytes 184328 | tf_op jit(solution)/shard_map/ppermute | solution.py:160
  86.1 1.4 %collective-permute-done.6 = f32[24,640]{1,0:T(8,128)S(1)} collective-permute-done((f32[24,640]{1,0:T(8,128)S(1)}, f32[24,640]{1,0:T(8,128)S(1)}, u32[]{:S(2)}, u32[]{:S(2)}) %collective-permute-start.6) | collective-permute-done | bytes 61472 | tf_op jit(solution)/shard_map/ppermute | solution.py:160
  88.4 1.3 %gather_fusion.5 = f32[64,640]{1,0:T(8,128)} fusion(f32[25,640]{1,0:T(8,128)S(1)} %concatenate.15, s32[1024]{0:T(1024)S(1)} %pad_clamp_fusion.1), kind=kCustom, calls=%fused_computation.5 | custom fusion | bytes 327936 | tf_op jit(solution)/shard_map/gather | solution.py:178
  89.7 1.0 fusion.37
  90.9 17.7 %all_to_all.15 = bf16[64,2,640]{2,1,0:T(2,128)(2,1)S(1)} all-to-all(bf16[64,2,640]{2,1,0:T(2,128)(2,1)S(1)} %copy.46), channel_id=1, replica_groups=mesh['req'=64,'kv'=4] {'req'}, dimensions={0} | all-to-all | bytes 327680 | tf_op jit(solution)/shard_map/all_to_all | solution.py:183
  (101 shorter events, 19.1 us)
Async XLA Ops:
  0.0 36.7 %copy-start = (bf16[640,2560]{1,0:T(8,128)(2,1)S(1)}, bf16[640,2560]{1,0:T(8,128)(2,1)}, u32[]{:S(2)}) copy-start(bf16[640,2560]{1,0:T(8,128)(2,1)} %param.23) | copy-start | bytes 9830404
  0.0 17.6 %copy-start.7 = (s32[128]{0:T(128)S(1)}, s32[128]{0:T(128)}, u32[]{:S(2)}) copy-start(s32[128]{0:T(128)} %param.22) | copy-start | bytes 1540
  0.0 23.5 %copy-start.5 = (s32[128,6]{0,1:T(8,128)S(1)}, s32[128,6]{0,1:T(8,128)}, u32[]{:S(2)}) copy-start(s32[128,6]{0,1:T(8,128)} %param.25) | copy-start | bytes 9220
  0.0 23.6 %copy-start.6 = (f32[128,6]{0,1:T(8,128)S(1)}, f32[128,6]{0,1:T(8,128)}, u32[]{:S(2)}) copy-start(f32[128,6]{0,1:T(8,128)} %param.26) | copy-start | bytes 9220
  0.0 25.0 %copy-start.1 = (s32[128]{0:T(128)S(1)}, s32[128]{0:T(128)}, u32[]{:S(2)}) copy-start(s32[128]{0:T(128)} %param.21) | copy-start | bytes 1540
  4.4 28.2 %all-to-all-start = ((bf16[64,2,1536]{2,1,0:T(2,128)(2,1)}), bf16[64,2,1536]{2,1,0:T(2,128)(2,1)}, u32[]{:S(2)}, u32[]{:S(2)}) async-start(bf16[64,2,1536]{2,1,0:T(2,128)(2,1)} %pad_maximum_fusion), calls=%async_computation | async-start | bytes 786432 | tf_op jit(solution)/shard_map/all_to_all | solution.py:52
  33.4 2.8 %copy-start.2 = (bf16[2,4096,128]{2,1,0:T(8,128)(2,1)S(1)}, bf16[2,4096,128]{2,1,0:T(8,128)(2,1)}, u32[]{:S(2)}) copy-start(bf16[2,4096,128]{2,1,0:T(8,128)(2,1)} %param.20) | copy-start | bytes 6291460
  36.7 6.1 %copy-start.8 = (bf16[640]{0:T(1024)(128)(2,1)S(1)}, bf16[640]{0:T(1024)(128)(2,1)}, u32[]{:S(2)}) copy-start(bf16[640]{0:T(1024)(128)(2,1)} %param.24) | copy-start | bytes 3844
  37.3 5.7 %collective-permute-start = (f32[2,2560]{1,0:T(2,128)S(1)}, f32[2,2560]{1,0:T(2,128)S(1)}, u32[]{:S(2)}, u32[]{:S(2)}) collective-permute-start(f32[2,2560]{1,0:T(2,128)S(1)} %add_dynamic-update-slice_fusion), channel_id=1, source_target_pairs={{0,1},{1,2},{2,3},{3,0},{4,5},{5,6},{6,7},{7,4},{8,9},{9,10},{10,1... | collective-permute-start | bytes 61448 | tf_op jit(solution)/shard_map/ppermute | solution.py:102
  38.7 4.4 %collective-permute-start.1 = (f32[2,2560]{1,0:T(2,128)S(1)}, f32[2,2560]{1,0:T(2,128)S(1)}, u32[]{:S(2)}, u32[]{:S(2)}) collective-permute-start(f32[2,2560]{1,0:T(2,128)S(1)} %add_dynamic-update-slice_fusion), channel_id=1, source_target_pairs={{0,2},{1,3},{2,0},{3,1},{4,6},{5,7},{6,4},{7,5},{8,10},{9,11},{10,... | collective-permute-start | bytes 61448 | tf_op jit(solution)/shard_map/ppermute | solution.py:102
  41.3 2.8 %collective-permute-start.2 = (f32[2,2560]{1,0:T(2,128)S(1)}, f32[2,2560]{1,0:T(2,128)S(1)}, u32[]{:S(2)}, u32[]{:S(2)}) collective-permute-start(f32[2,2560]{1,0:T(2,128)S(1)} %add_dynamic-update-slice_fusion), channel_id=1, source_target_pairs={{0,3},{1,0},{2,1},{3,2},{4,7},{5,4},{6,5},{7,6},{8,11},{9,8},{10,9... | collective-permute-start | bytes 61448 | tf_op jit(solution)/shard_map/ppermute | solution.py:102
  45.2 22.8 %all-to-all-start.1 = ((bf16[64,2,640]{2,1,0:T(2,128)(2,1)}), bf16[64,2,640]{2,1,0:T(2,128)(2,1)S(1)}, u32[]{:S(2)}, u32[]{:S(2)}) async-start(bf16[64,2,640]{2,1,0:T(2,128)(2,1)} %broadcast_select_fusion.4), calls=%async_computation.1 | async-start | bytes 327680 | tf_op jit(solution)/shard_map/all_to_all | solution.py:122
  68.8 9.8 %copy-start.3 = (bf16[1,2560,384]{2,1,0:T(8,128)(2,1)S(1)}, bf16[1,2560,384]{2,1,0:T(8,128)(2,1)}, u32[]{:S(2)}) copy-start(bf16[1,2560,384]{2,1,0:T(8,128)(2,1)} %param.27) | copy-start | bytes 5898244
  68.8 6.1 %collective-permute-start.3 = (bf16[24,640]{1,0:T(8,128)(2,1)S(1)}, bf16[24,640]{1,0:T(8,128)(2,1)S(1)}, u32[]{:S(2)}, u32[]{:S(2)}) collective-permute-start(bf16[24,640]{1,0:T(8,128)(2,1)S(1)} %gather_fusion.3), channel_id=1, source_target_pairs={{0,1},{1,2},{2,3},{3,0},{4,5},{5,6},{6,7},{7,4},{8,9},{9,10},{10,1... | collective-permute-start | bytes 92168 | tf_op jit(solution)/shard_map/ppermute | solution.py:135
  68.9 8.5 %collective-permute-start.5 = (bf16[24,640]{1,0:T(8,128)(2,1)S(1)}, bf16[24,640]{1,0:T(8,128)(2,1)S(1)}, u32[]{:S(2)}, u32[]{:S(2)}) collective-permute-start(bf16[24,640]{1,0:T(8,128)(2,1)S(1)} %gather_fusion.3), channel_id=1, source_target_pairs={{0,3},{1,0},{2,1},{3,2},{4,7},{5,4},{6,5},{7,6},{8,11},{9,8},{10,9... | collective-permute-start | bytes 92168 | tf_op jit(solution)/shard_map/ppermute | solution.py:135
  71.6 7.3 %collective-permute-start.4 = (bf16[24,640]{1,0:T(8,128)(2,1)S(1)}, bf16[24,640]{1,0:T(8,128)(2,1)S(1)}, u32[]{:S(2)}, u32[]{:S(2)}) collective-permute-start(bf16[24,640]{1,0:T(8,128)(2,1)S(1)} %gather_fusion.3), channel_id=1, source_target_pairs={{0,2},{1,3},{2,0},{3,1},{4,6},{5,7},{6,4},{7,5},{8,10},{9,11},{10,... | collective-permute-start | bytes 92168 | tf_op jit(solution)/shard_map/ppermute | solution.py:135
  73.6 6.7 %copy-start.4 = (bf16[1,384,2560]{2,1,0:T(8,128)(2,1)S(1)}, bf16[1,384,2560]{2,1,0:T(8,128)(2,1)}, u32[]{:S(2)}) copy-start(bf16[1,384,2560]{2,1,0:T(8,128)(2,1)} %param.29) | copy-start | bytes 5898244
  80.5 5.6 %collective-permute-start.7 = (f32[24,640]{1,0:T(8,128)S(1)}, f32[24,640]{1,0:T(8,128)S(1)}, u32[]{:S(2)}, u32[]{:S(2)}) collective-permute-start(f32[24,640]{1,0:T(8,128)S(1)} %convolution_multiply_fusion.2), channel_id=1, source_target_pairs={{0,2},{1,3},{2,0},{3,1},{4,6},{5,7},{6,4},{7,5},{8,10},{9,11},{10,... | collective-permute-start | bytes 184328 | tf_op jit(solution)/shard_map/ppermute | solution.py:160
  83.0 4.5 %collective-permute-start.6 = (f32[24,640]{1,0:T(8,128)S(1)}, f32[24,640]{1,0:T(8,128)S(1)}, u32[]{:S(2)}, u32[]{:S(2)}) collective-permute-start(f32[24,640]{1,0:T(8,128)S(1)} %convolution_multiply_fusion.3), channel_id=1, source_target_pairs={{0,1},{1,2},{2,3},{3,0},{4,5},{5,6},{6,7},{7,4},{8,9},{9,10},{10,1... | collective-permute-start | bytes 184328 | tf_op jit(solution)/shard_map/ppermute | solution.py:160
  83.2 4.2 %collective-permute-start.8 = (f32[24,640]{1,0:T(8,128)S(1)}, f32[24,640]{1,0:T(8,128)S(1)}, u32[]{:S(2)}, u32[]{:S(2)}) collective-permute-start(f32[24,640]{1,0:T(8,128)S(1)} %convolution_multiply_fusion.1), channel_id=1, source_target_pairs={{0,3},{1,0},{2,1},{3,2},{4,7},{5,4},{6,5},{7,6},{8,11},{9,8},{10,9... | collective-permute-start | bytes 184328 | tf_op jit(solution)/shard_map/ppermute | solution.py:160
